TPU v7x, 256 devices: a whole 4x4x8 slice. The times are simulated.
256 devices in a mesh: gx: 16 (over z, core), gy: 16 (over x, y).
Axes of the slice: x: 4, y: 4, z: 8, core: 2. Of those that a mesh axis runs over, the one named last changes fastest.
Arguments:
- forcing: float32 [4, 8, 4096, 2048], P(None, None, 'gx', 'gy'), may hold values from -150 to 150
- velocity: float32 [2, 4096, 2048], P(None, 'gx', 'gy'), may hold values from -0.6 to 0.6
- viscosity: float32 [4096, 2048], P('gx', 'gy'), may hold values from 0.05 to 0.25
- sound: float32 [4096, 2048], P('gx', 'gy'), may hold values from 0.4 to 1
- coupling: float32 [4, 4, 4096, 2048], P(None, None, 'gx', 'gy'), may hold values from -1.5 to 1.5
Outputs:
- basis: float32 [4, 8, 4096, 2048], P(None, None, 'gx', 'gy')
- factor: float32 [8, 8], replicated
All inputs are finite; a program needn't handle non-finite values.
Results may differ from a plain program's by a relative error of at most 0.000055.
Values sent between devices are 32-bit elements; how exact they have to be, the bound alone decides.
No kernel may reach another device: no remote copies, remote signals or barrier semaphores. Data moves between devices by JAX's collectives and lax.ppermute only.
A program may use at most 128 MiB of HBM per device.

v0:
```python
import jax
import jax.numpy as jnp
from jax import lax
from jax.sharding import PartitionSpec as P

STEP = 0.5


def with_halo(cells, sides, width):
    for axis, dim in sides:
        count = lax.axis_size(axis)
        ends = count - 1
        head = lax.slice_in_dim(cells, 0, width, axis=dim)
        tail = lax.slice_in_dim(cells, cells.shape[dim] - width, cells.shape[dim], axis=dim)
        cells = jnp.concatenate(
            [
                lax.ppermute(tail, axis, [(i, (i + 1) % count) for i in range(ends)]),
                cells,
                lax.ppermute(head, axis, [((i + 1) % count, i) for i in range(ends)]),
            ],
            axis=dim,
        )
    return cells


def tendency(padded, velocity, viscosity, sound, coupling):
    center = padded[:, :, 1:-1, 1:-1]
    east = padded[:, :, 2:, 1:-1]
    west = padded[:, :, :-2, 1:-1]
    north = padded[:, :, 1:-1, 2:]
    south = padded[:, :, 1:-1, :-2]
    grad_x = 0.5 * (east - west)
    grad_y = 0.5 * (north - south)
    laplace = east + west + north + south - 4.0 * center
    transport = viscosity * laplace - velocity[0] * grad_x - velocity[1] * grad_y
    divergence = grad_x[1] + grad_y[2]
    acoustic = jnp.stack(
        [-sound * divergence, -sound * grad_x[3], -sound * grad_y[3], -sound * divergence]
    )
    mixing = coupling[:, 0][:, None] * center[0][None]
    for inner in range(1, 4):
        mixing = mixing + coupling[:, inner][:, None] * center[inner][None]
    return transport + acoustic - mixing


def extend(state):
    return with_halo(state, (("gx", 2), ("gy", 3)), 1)


def local(forcing, velocity, viscosity, sound, coupling):
    first = tendency(extend(forcing), velocity, viscosity, sound, coupling) + forcing
    middle = forcing + STEP * first
    second = tendency(extend(middle), velocity, viscosity, sound, coupling) + forcing
    response = forcing + 0.5 * STEP * (first + second)
    rows_total = float(
        4 * forcing.shape[2] * forcing.shape[3] * lax.axis_size("gx") * lax.axis_size("gy")
    )
    local_gram = (
        jnp.einsum("vcxy,vdxy->cd", response, response, precision=lax.Precision.HIGHEST)
        / rows_total
    )
    lower = jnp.linalg.cholesky(lax.psum(local_gram, ("gx", "gy")))
    identity = jnp.eye(lower.shape[0], dtype=lower.dtype)
    inverse = lax.linalg.triangular_solve(lower, identity, left_side=True, lower=True)
    basis = jnp.einsum("cd,vdxy->vcxy", inverse, response, precision=lax.Precision.HIGHEST)
    return (basis, lower.T)


def solution(mesh):
    in_specs = (
        P(None, None, "gx", "gy"),
        P(None, "gx", "gy"),
        P("gx", "gy"),
        P("gx", "gy"),
        P(None, None, "gx", "gy"),
    )
    out_specs = (P(None, None, "gx", "gy"), P())
    return jax.shard_map(local, mesh=mesh, in_specs=in_specs, out_specs=out_specs, check_vma=False)
```

profile of v0, /device:TPU:2, one launch (start us, length us, event | category | flops | bytes accessed | tf_op | source)
XLA Modules:
  0.0 233.7 jit_solution(18305960756760041180)
XLA Ops:
  2.9 3.2 %collective-permute-start.1 = (f32[4,8,1,128]{3,1,2,0:T(8,128)S(1)}, f32[4,8,1,128]{3,1,2,0:T(8,128)S(1)}, u32[]{:S(2)}, u32[]{:S(2)}) collective-permute-start(f32[4,8,1,128]{3,1,2,0:T(8,128)S(1)} %bitcast.56), channel_id=1, source_target_pairs={{0,16},{16,32},{32,48},{48,64},{64,80},{80,96},{96,112},{112,128},... | collective-permute-start | bytes 49160 | tf_op jit(solution)/shard_map/ppermute | solution.py:17
  6.1 3.8 %slice_bitcast_fusion.7 = (f32[8,256,128]{2,1,0:T(8,128)}, f32[8,256,128]{2,1,0:T(8,128)S(1)}, f32[8,256,128]{2,1,0:T(8,128)}, f32[8,256,128]{2,1,0:T(8,128)}) fusion(f32[4,8,256,128]{3,2,1,0:T(8,128)} %param.5), kind=kLoop, calls=%fused_computation.51 | loop fusion | bytes 8388608 | tf_op jit(solution)/shard_map/mul | solution.py:40
  11.4 5.4 %copy.76 = f32[4,8,256,128]{2,1,3,0:T(8,128)} copy(f32[4,8,256,128]{3,2,1,0:T(8,128)} %param.5) | data formatting | bytes 8388608 | tf_op args[0]
  21.1 3.5 %collective-permute-start.3 = (f32[4,8,258,1]{2,1,3,0:T(8,128)}, f32[4,8,258,1]{2,1,3,0:T(8,128)}, u32[]{:S(2)}, u32[]{:S(2)}) collective-permute-start(f32[4,8,258,1]{2,1,3,0:T(8,128)} %get-tuple-element.16), channel_id=1, source_target_pairs={{0,1},{1,2},{2,3},{3,4},{4,5},{5,6},{6,7},{7,8},{8,9},{9,10},{10,1... | collective-permute-start | bytes 99080 | tf_op jit(solution)/shard_map/ppermute | solution.py:17
  24.6 4.5 %collective-permute-start.2 = (f32[4,8,258,1]{2,1,3,0:T(8,128)}, f32[4,8,258,1]{2,1,3,0:T(8,128)}, u32[]{:S(2)}, u32[]{:S(2)}) collective-permute-start(f32[4,8,258,1]{2,1,3,0:T(8,128)} %get-tuple-element.17), channel_id=1, source_target_pairs={{1,0},{2,1},{3,2},{4,3},{5,4},{6,5},{7,6},{8,7},{9,8},{10,9},{11,1... | collective-permute-start | bytes 99080 | tf_op jit(solution)/shard_map/ppermute | solution.py:19
  31.8 2.6 %copy.64 = f32[8,256,128]{1,0,2:T(8,128)} copy(f32[8,256,128]{2,1,0:T(8,128)} %get-tuple-element.35) | data formatting | bytes 2097152 | tf_op jit(solution)/shard_map/mul | solution.py:42
  35.6 2.6 %copy.62 = f32[8,256,128]{1,0,2:T(8,128)} copy(f32[8,256,128]{2,1,0:T(8,128)} %get-tuple-element.34) | data formatting | bytes 2097152 | tf_op jit(solution)/shard_map/mul | solution.py:42
  40.3 2.7 %copy.60 = f32[8,256,128]{1,0,2:T(8,128)} copy(f32[8,256,128]{2,1,0:T(8,128)} %get-tuple-element.32) | data formatting | bytes 2097152 | tf_op jit(solution)/shard_map/mul | solution.py:40
  47.9 10.8 %fusion.8 = (f32[4,8,256,128]{2,1,3,0:T(8,128)S(1)}, f32[4,8,256,128]{2,1,3,0:T(8,128)S(1)}) fusion(f32[4,8,1,128]{2,1,3,0:T(8,128)S(1)} %copy.48, f32[4,8,256,128]{2,1,3,0:T(8,128)} %copy.76, f32[4,8,1,128]{2,1,3,0:T(8,128)} %copy.50, f32[4,8,258,1]{2,1,3,0:T(8,128)} %collective-permute-done.3, f32[4,8,258,1]{2,1,3,0:T(8,128)} %collective-permute-done.2), kind=kLoop, calls=%fused_computation.27 | loop fusion | flops 12582912 | bytes 12681728 | tf_op jit(solution)/shard_map/mul | solution.py:32
  62.8 11.5 %multiply_add_fusion = (f32[4,8,256,128]{2,1,3,0:T(8,128)S(1)}, f32[4,8,256,128]{2,1,3,0:T(8,128)}) fusion(f32[4,8,256,128]{2,1,3,0:T(8,128)S(1)} %copy-done.2, f32[8,256,128]{1,0,2:T(8,128)} %copy.66, f32[4,256,128]{1,2,0:T(8,128)S(1)} %copy.65, f32[8,256,128]{1,0,2:T(8,128)} %copy.64, f32[4,256,128]{1,2,0:T(8,128)S(1)} %copy.63, f32[8,256,128]{1,0,2:T(8,128)} %copy.62, ...), kind=kLoop, calls=%fused_computation.25 | loop fusion | flops 36700160 | bytes 22512128 | tf_op jit(solution)/shard_map/add | solution.py:52
  74.3 2.5 %fusion.18 = (f32[4,8,1,128]{2,1,3,0:T(8,128)S(1)}, f32[4,8,1,128]{2,1,3,0:T(8,128)}) fusion(f32[4,8,256,128]{2,1,3,0:T(8,128)S(1)} %get-tuple-element.8), kind=kLoop, calls=%fused_computation.74 | loop fusion | bytes 65536 | tf_op jit(solution)/shard_map/slice | solution.py:14
  76.9 2.2 copy.69
  81.7 4.1 %collective-permute-start.5 = (f32[4,8,1,128]{3,1,2,0:T(8,128)}, f32[4,8,1,128]{3,1,2,0:T(8,128)}, u32[]{:S(2)}, u32[]{:S(2)}) collective-permute-start(f32[4,8,1,128]{3,1,2,0:T(8,128)} %copy.71), channel_id=1, source_target_pairs={{0,16},{16,32},{32,48},{48,64},{64,80},{80,96},{96,112},{112,128},... | collective-permute-start | bytes 49160 | tf_op jit(solution)/shard_map/ppermute | solution.py:17
  87.2 2.8 %copy.72 = f32[4,8,1,128]{2,1,3,0:T(8,128)} copy(f32[4,8,1,128]{3,1,2,0:T(8,128)} %collective-permute-done.5) | data formatting | bytes 32768 | tf_op jit(solution)/shard_map/ppermute | solution.py:17
  91.0 2.1 collective-permute-start.7
  93.1 6.3 %collective-permute-start.6 = (f32[4,8,258,1]{2,1,3,0:T(8,128)S(1)}, f32[4,8,258,1]{2,1,3,0:T(8,128)S(1)}, u32[]{:S(2)}, u32[]{:S(2)}) collective-permute-start(f32[4,8,258,1]{2,1,3,0:T(8,128)S(1)} %get-tuple-element.13), channel_id=1, source_target_pairs={{1,0},{2,1},{3,2},{4,3},{5,4},{6,5},{7,6},{8,7},{9,8},{10,9},{11,1... | collective-permute-start | bytes 99080 | tf_op jit(solution)/shard_map/ppermute | solution.py:19
  101.5 6.9 %fusion.10 = (f32[4,8,256,128]{2,1,3,0:T(8,128)}, f32[4,8,256,128]{2,1,3,0:T(8,128)}) fusion(f32[4,8,1,128]{2,1,3,0:T(8,128)S(1)} %copy.70, f32[4,8,256,128]{2,1,3,0:T(8,128)S(1)} %copy-done.1, f32[4,8,1,128]{2,1,3,0:T(8,128)S(1)} %copy-done.5, f32[4,8,258,1]{2,1,3,0:T(8,128)S(1)} %collective-permute-done.7, f32[4,8,258,1]{2,1,3,0:T(8,128)S(1)} %collective-permute-done.6), kind=kLoop, calls=%fused_computation.29 | loop fusion | flops 12582912 | bytes 12681728 | tf_op jit(solution)/shard_map/mul | solution.py:32
  108.5 4.0 %slice_multiply_fusion.1 = (f32[1,8,256,128]{2,1,3,0:T(8,128)S(1)}, f32[1,8,256,128]{2,1,3,0:T(8,128)}, f32[1,8,256,128]{2,1,3,0:T(8,128)}) fusion(f32[4,8,256,128]{2,1,3,0:T(8,128)} %get-tuple-element.10, f32[256,128]{0,1:T(8,128)S(1)} %copy-done.11, f32[4,8,256,128]{2,1,3,0:T(8,128)} %get-tuple-element.11), kind=kLoop, calls=%fused_computation.41 | loop fusion | flops 1048576 | bytes 7471104 | tf_op jit(solution)/shard_map/mul | solution.py:38
  112.6 11.4 %fusion.6 = f32[4,8,256,128]{2,1,3,0:T(8,128)} fusion(f32[4,8,256,128]{2,1,3,0:T(8,128)S(1)} %copy-done.3, f32[4,8,256,128]{2,1,3,0:T(8,128)S(1)} %copy-done.6, f32[1,8,256,128]{2,1,3,0:T(8,128)} %get-tuple-element.19, f32[1,8,256,128]{2,1,3,0:T(8,128)} %get-tuple-element.20, f32[1,8,256,128]{2,1,3,0:T(8,128)S(1)} %get-tuple-element.18, ...), kind=kLoop, calls=%fused_computation.24 | loop fusion | flops 37748736 | bytes 26706432 | tf_op jit(solution)/shard_map/add | solution.py:54
  124.0 5.5 %copy.80 = f32[4,8,256,128]{3,1,2,0:T(8,128)} copy(f32[4,8,256,128]{2,1,3,0:T(8,128)} %fusion.6) | data formatting | bytes 8388608 | tf_op jit(solution)/shard_map/add | solution.py:54
  129.5 12.6 %fusion.11 = f32[8,8]{0,1:T(8,128)S(1)} fusion(f32[4,8,256,128]{2,1,3,0:T(8,128)} %fusion.6), kind=kOutput, calls=%fused_computation.35 | convolution fusion | flops 100663360 | bytes 4194560 | tf_op jit(solution)/shard_map/vcxy,vdxy->cd/dot_general | solution.py:59
  142.1 79.9 %psum.7 = f32[8,8]{0,1:T(8,128)S(1)} all-reduce(f32[8,8]{0,1:T(8,128)S(1)} %fusion.11), channel_id=1, replica_groups=mesh['gx'=16,'gy'=16] {'gx','gy'}, use_global_device_ids=true, to_apply=%region_0.0 | all-reduce | flops 64 | bytes 512 | tf_op jit(solution)/shard_map/psum | solution.py:62
  224.9 5.3 %convolution_bitcast_fusion = f32[4,8,256,128]{3,1,2,0:T(8,128)S(1)} fusion(f32[4,8,256,128]{3,1,2,0:T(8,128)} %copy.80, f32[8,8,1,1]{1,0,3,2:T(8,128)S(1)} %convolution_bitcast_fusion.1), kind=kOutput, calls=%fused_computation.30 | convolution fusion | flops 100663296 | bytes 8388864 | tf_op jit(solution)/shard_map/cd,vdxy->vcxy/dot_general | solution.py:65
  230.3 2.8 %copy.81 = f32[4,8,256,128]{3,2,1,0:T(8,128)} copy(f32[4,8,256,128]{3,1,2,0:T(8,128)S(1)} %convolution_bitcast_fusion) | data formatting | bytes 8388608
  (66 shorter events, 33.8 us)
Async XLA Ops:
  1.6 15.2 %collective-permute-start = (f32[4,8,1,128]{3,1,2,0:T(8,128)S(1)}, f32[4,8,1,128]{3,1,2,0:T(8,128)S(1)}, u32[]{:S(2)}, u32[]{:S(2)}) collective-permute-start(f32[4,8,1,128]{3,1,2,0:T(8,128)S(1)} %bitcast.57), channel_id=1, source_target_pairs={{16,0},{32,16},{48,32},{64,48},{80,64},{96,80},{112,96},{128,112},... | collective-permute-start | bytes 49160 | tf_op jit(solution)/shard_map/ppermute | solution.py:19
  2.9 7.0 %copy-start.9 = (f32[4,4,256,128]{3,2,1,0:T(8,128)S(1)}, f32[4,4,256,128]{3,2,1,0:T(8,128)}, u32[]{:S(2)}) copy-start(f32[4,4,256,128]{3,2,1,0:T(8,128)} %param.9) | copy-start | bytes 6291460
  2.9 14.6 %collective-permute-start.1 = (f32[4,8,1,128]{3,1,2,0:T(8,128)S(1)}, f32[4,8,1,128]{3,1,2,0:T(8,128)S(1)}, u32[]{:S(2)}, u32[]{:S(2)}) collective-permute-start(f32[4,8,1,128]{3,1,2,0:T(8,128)S(1)} %bitcast.56), channel_id=1, source_target_pairs={{0,16},{16,32},{32,48},{48,64},{64,80},{80,96},{96,112},{112,128},... | collective-permute-start | bytes 49160 | tf_op jit(solution)/shard_map/ppermute | solution.py:17
  19.5 9.5 %copy-start.12 = (f32[2,256,128]{2,1,0:T(8,128)S(1)}, f32[2,256,128]{2,1,0:T(8,128)}, u32[]{:S(2)}) copy-start(f32[2,256,128]{2,1,0:T(8,128)} %param.6) | copy-start | bytes 786436
  21.1 26.8 %collective-permute-start.3 = (f32[4,8,258,1]{2,1,3,0:T(8,128)}, f32[4,8,258,1]{2,1,3,0:T(8,128)}, u32[]{:S(2)}, u32[]{:S(2)}) collective-permute-start(f32[4,8,258,1]{2,1,3,0:T(8,128)} %get-tuple-element.16), channel_id=1, source_target_pairs={{0,1},{1,2},{2,3},{3,4},{4,5},{5,6},{6,7},{7,8},{8,9},{9,10},{10,1... | collective-permute-start | bytes 99080 | tf_op jit(solution)/shard_map/ppermute | solution.py:17
  24.6 23.3 %collective-permute-start.2 = (f32[4,8,258,1]{2,1,3,0:T(8,128)}, f32[4,8,258,1]{2,1,3,0:T(8,128)}, u32[]{:S(2)}, u32[]{:S(2)}) collective-permute-start(f32[4,8,258,1]{2,1,3,0:T(8,128)} %get-tuple-element.17), channel_id=1, source_target_pairs={{1,0},{2,1},{3,2},{4,3},{5,4},{6,5},{7,6},{8,7},{9,8},{10,9},{11,1... | collective-permute-start | bytes 99080 | tf_op jit(solution)/shard_map/ppermute | solution.py:19
  47.9 10.9 %copy-start.10 = (f32[256,128]{0,1:T(8,128)S(1)}, f32[256,128]{0,1:T(8,128)}, u32[]{:S(2)}) copy-start(f32[256,128]{0,1:T(8,128)} %copy.58) | copy-start | bytes 393220
  58.8 3.3 %copy-start.2 = (f32[4,8,256,128]{2,1,3,0:T(8,128)S(1)}, f32[4,8,256,128]{2,1,3,0:T(8,128)}, u32[]{:S(2)}) copy-start(f32[4,8,256,128]{2,1,3,0:T(8,128)} %copy.76) | copy-start | bytes 12582916
  58.8 4.0 %copy-start.4 = (f32[4,8,1,128]{2,1,3,0:T(8,128)S(1)}, f32[4,8,1,128]{2,1,3,0:T(8,128)}, u32[]{:S(2)}) copy-start(f32[4,8,1,128]{2,1,3,0:T(8,128)} %copy.50) | copy-start | bytes 49156
  74.3 2.7 %copy-start = (f32[4,8,256,128]{2,1,3,0:T(8,128)}, f32[4,8,256,128]{2,1,3,0:T(8,128)S(1)}, u32[]{:S(2)}) copy-start(f32[4,8,256,128]{2,1,3,0:T(8,128)S(1)} %get-tuple-element.8) | copy-start | bytes 12582916
  79.2 6.7 %collective-permute-start.4 = (f32[4,8,1,128]{3,1,2,0:T(8,128)S(1)}, f32[4,8,1,128]{3,1,2,0:T(8,128)}, u32[]{:S(2)}, u32[]{:S(2)}) collective-permute-start(f32[4,8,1,128]{3,1,2,0:T(8,128)S(1)} %copy.69), channel_id=1, source_target_pairs={{16,0},{32,16},{48,32},{64,48},{80,64},{96,80},{112,96},{128,112},... | collective-permute-start | bytes 49160 | tf_op jit(solution)/shard_map/ppermute | solution.py:19
  81.7 5.5 %collective-permute-start.5 = (f32[4,8,1,128]{3,1,2,0:T(8,128)}, f32[4,8,1,128]{3,1,2,0:T(8,128)}, u32[]{:S(2)}, u32[]{:S(2)}) collective-permute-start(f32[4,8,1,128]{3,1,2,0:T(8,128)} %copy.71), channel_id=1, source_target_pairs={{0,16},{16,32},{32,48},{48,64},{64,80},{80,96},{96,112},{112,128},... | collective-permute-start | bytes 49160 | tf_op jit(solution)/shard_map/ppermute | solution.py:17
  90.0 9.5 %copy-start.1 = (f32[4,8,256,128]{2,1,3,0:T(8,128)S(1)}, f32[4,8,256,128]{2,1,3,0:T(8,128)}, u32[]{:S(2)}) copy-start(f32[4,8,256,128]{2,1,3,0:T(8,128)} %copy-done) | copy-start | bytes 12582916
  91.0 10.5 %collective-permute-start.7 = (f32[4,8,258,1]{2,1,3,0:T(8,128)S(1)}, f32[4,8,258,1]{2,1,3,0:T(8,128)S(1)}, u32[]{:S(2)}, u32[]{:S(2)}) collective-permute-start(f32[4,8,258,1]{2,1,3,0:T(8,128)S(1)} %get-tuple-element.12), channel_id=1, source_target_pairs={{0,1},{1,2},{2,3},{3,4},{4,5},{5,6},{6,7},{7,8},{8,9},{9,10},{10,1... | collective-permute-start | bytes 99080 | tf_op jit(solution)/shard_map/ppermute | solution.py:17
  93.1 8.4 %copy-start.5 = (f32[4,8,1,128]{2,1,3,0:T(8,128)S(1)}, f32[4,8,1,128]{2,1,3,0:T(8,128)}, u32[]{:S(2)}) copy-start(f32[4,8,1,128]{2,1,3,0:T(8,128)} %copy.72) | copy-start | bytes 49156
  93.1 8.4 %collective-permute-start.6 = (f32[4,8,258,1]{2,1,3,0:T(8,128)S(1)}, f32[4,8,258,1]{2,1,3,0:T(8,128)S(1)}, u32[]{:S(2)}, u32[]{:S(2)}) collective-permute-start(f32[4,8,258,1]{2,1,3,0:T(8,128)S(1)} %get-tuple-element.13), channel_id=1, source_target_pairs={{1,0},{2,1},{3,2},{4,3},{5,4},{6,5},{7,6},{8,7},{9,8},{10,9},{11,1... | collective-permute-start | bytes 99080 | tf_op jit(solution)/shard_map/ppermute | solution.py:19
  101.5 7.0 %copy-start.11 = (f32[256,128]{0,1:T(8,128)S(1)}, f32[256,128]{0,1:T(8,128)}, u32[]{:S(2)}) copy-start(f32[256,128]{0,1:T(8,128)} %copy.58) | copy-start | bytes 393220
  101.5 11.0 %copy-start.6 = (f32[4,8,256,128]{2,1,3,0:T(8,128)S(1)}, f32[4,8,256,128]{2,1,3,0:T(8,128)}, u32[]{:S(2)}) copy-start(f32[4,8,256,128]{2,1,3,0:T(8,128)} %get-tuple-element.9) | copy-start | bytes 12582916
  108.5 4.0 %copy-start.3 = (f32[4,8,256,128]{2,1,3,0:T(8,128)S(1)}, f32[4,8,256,128]{2,1,3,0:T(8,128)}, u32[]{:S(2)}) copy-start(f32[4,8,256,128]{2,1,3,0:T(8,128)} %copy.76) | copy-start | bytes 12582916
  108.5 4.0 %copy-start.7 = (f32[4,256,128]{1,2,0:T(8,128)S(1)}, f32[4,256,128]{1,2,0:T(8,128)}, u32[]{:S(2)}) copy-start(f32[4,256,128]{1,2,0:T(8,128)} %copy.61) | copy-start | bytes 1572868
  108.5 4.1 %copy-start.8 = (f32[4,256,128]{1,2,0:T(8,128)S(1)}, f32[4,256,128]{1,2,0:T(8,128)}, u32[]{:S(2)}) copy-start(f32[4,256,128]{1,2,0:T(8,128)} %copy.59) | copy-start | bytes 1572868
where the time goes:
time: 237 us; the launch traced here: 234 us
  blocking collectives  79.9 us (34%)
  local copies, waits for them, and re-layouts  55.8 us (24%)
  other arithmetic  52.7 us (22%)
  starting transfers between devices  26.2 us (11%)
  matrix products  18.1 us (8%)
    psum x1, blocking collectives, local(): lower = jnp.linalg.cholesky(lax.psum(local_gram, ('gx', 'gy')))  79.9 us
    mul x2, other arithmetic, tendency(): grad_x = 0.5 * (east - west)  17.8 us
    ppermute x4, starting transfers between devices, with_halo(): lax.ppermute(head, axis, [((i + 1) % count, i) for i in range(ends)])  13.4 us
    ppermute x4, starting transfers between devices, with_halo(): lax.ppermute(tail, axis, [(i, (i + 1) % count) for i in range(ends)])  12.8 us
    dot_general x1, matrix products, local(): jnp.einsum('vcxy,vdxy->cd', response, response, precision=lax.Precision.H...  12.6 us
    unnamed x30, local copies, waits for them, and re-layouts  12.3 us
    mul x5, local copies, waits for them, and re-layouts, tendency(): mixing = coupling[:, 0][:, None] * center[0][None]  12.1 us
    add x1, other arithmetic, local(): middle = forcing + STEP * first  11.5 us
  transfers between devices with their start and end apart: 8, of which 0 were waited for; matrix products, arithmetic and copies ran while one was open for 15% of the time, Pallas kernels for 0%

commit v1 on v0

--- a/solution.py
+++ b/solution.py
@@ -43,6 +43,16 @@
     return transport + acoustic - mixing
 
 
+def all_sum(value):
+    for axis in ("gy", "gx"):
+        count = lax.axis_size(axis)
+        bit = 1
+        while bit < count:
+            value = value + lax.ppermute(value, axis, [(i, i ^ bit) for i in range(count)])
+            bit *= 2
+    return value
+
+
 def extend(state):
     return with_halo(state, (("gx", 2), ("gy", 3)), 1)
 
@@ -59,7 +69,7 @@
         jnp.einsum("vcxy,vdxy->cd", response, response, precision=lax.Precision.HIGHEST)
         / rows_total
     )
-    lower = jnp.linalg.cholesky(lax.psum(local_gram, ("gx", "gy")))
+    lower = jnp.linalg.cholesky(all_sum(local_gram))
     identity = jnp.eye(lower.shape[0], dtype=lower.dtype)
     inverse = lax.linalg.triangular_solve(lower, identity, left_side=True, lower=True)
     basis = jnp.einsum("cd,vdxy->vcxy", inverse, response, precision=lax.Precision.HIGHEST)

time: 237 us -> 189 us (0.80)
  blocking collectives: 79.9 us -> 0 us
  starting transfers between devices: 26.2 us -> 47.9 us
  waiting for transfers between devices: 0.02 us -> 15.8 us
  matrix products: 18.1 us -> 14.6 us
    psum x1 -> x0, blocking collectives: 79.9 us -> none  [local(): lower = jnp.linalg.cholesky(lax.psum(local_gram, ('gx', 'gy')))]
    ppermute x0 -> x8, starting transfers between devices: none -> 21.7 us  [all_sum(): lax.ppermute(value, axis, [(i, i ^ bit) for i in range(count)])]
    ppermute x0 -> x8, waiting for transfers between devices: none -> 15.8 us  [all_sum(): lax.ppermute(value, axis, [(i, i ^ bit) for i in range(count)])]
    dot_general x1, matrix products: 12.6 us -> 9.03 us  [local(): jnp.einsum('vcxy,vdxy->cd', response, response, precision=lax.Precision.H...]
  transfers between devices with their start and end apart: 8 -> 16, of which waited for: 0 -> 7; matrix products, arithmetic and copies ran while one was open for 15% -> 22% of each run, Pallas kernels for 0% -> 0%
where the time goes in v1:
time: 189 us; the launch traced here: 186 us
  local copies, waits for them, and re-layouts  56 us (30%)
  other arithmetic  51.2 us (27%)
  starting transfers between devices  47.9 us (25%)
  waiting for transfers between devices  15.8 us (8%)
  matrix products  14.6 us (8%)
    ppermute x8, starting transfers between devices, all_sum(): lax.ppermute(value, axis, [(i, i ^ bit) for i in range(count)])  21.7 us
    mul x2, other arithmetic, tendency(): grad_x = 0.5 * (east - west)  17.8 us
    ppermute x8, waiting for transfers between devices, all_sum(): lax.ppermute(value, axis, [(i, i ^ bit) for i in range(count)])  15.8 us
    ppermute x4, starting transfers between devices, with_halo(): lax.ppermute(head, axis, [((i + 1) % count, i) for i in range(ends)])  13.4 us
    ppermute x4, starting transfers between devices, with_halo(): lax.ppermute(tail, axis, [(i, (i + 1) % count) for i in range(ends)])  12.8 us
    unnamed x30, local copies, waits for them, and re-layouts  12.4 us
    mul x5, local copies, waits for them, and re-layouts, tendency(): mixing = coupling[:, 0][:, None] * center[0][None]  12.1 us
    add x1, other arithmetic, local(): middle = forcing + STEP * first  11.5 us
  transfers between devices with their start and end apart: 16, of which 7 were waited for; matrix products, arithmetic and copies ran while one was open for 22% of the time, Pallas kernels for 0%

profile of v1, /device:TPU:2, one launch (start us, length us, event | category | flops | bytes accessed | tf_op | source)
XLA Modules:
  0.0 186.3 jit_solution(12072940917320400074)
XLA Ops:
  2.9 3.2 %collective-permute-start.1 = (f32[4,8,1,128]{3,1,2,0:T(8,128)S(1)}, f32[4,8,1,128]{3,1,2,0:T(8,128)S(1)}, u32[]{:S(2)}, u32[]{:S(2)}) collective-permute-start(f32[4,8,1,128]{3,1,2,0:T(8,128)S(1)} %bitcast.56), channel_id=1, source_target_pairs={{0,16},{16,32},{32,48},{48,64},{64,80},{80,96},{96,112},{112,128},... | collective-permute-start | bytes 49160 | tf_op jit(solution)/shard_map/ppermute | solution.py:17
  6.1 3.8 %slice_bitcast_fusion.7 = (f32[8,256,128]{2,1,0:T(8,128)}, f32[8,256,128]{2,1,0:T(8,128)S(1)}, f32[8,256,128]{2,1,0:T(8,128)}, f32[8,256,128]{2,1,0:T(8,128)}) fusion(f32[4,8,256,128]{3,2,1,0:T(8,128)} %param.5), kind=kLoop, calls=%fused_computation.51 | loop fusion | bytes 8388608 | tf_op jit(solution)/shard_map/mul | solution.py:40
  11.4 5.4 %copy.76 = f32[4,8,256,128]{2,1,3,0:T(8,128)} copy(f32[4,8,256,128]{3,2,1,0:T(8,128)} %param.5) | data formatting | bytes 8388608 | tf_op args[0]
  21.1 3.5 %collective-permute-start.3 = (f32[4,8,258,1]{2,1,3,0:T(8,128)}, f32[4,8,258,1]{2,1,3,0:T(8,128)}, u32[]{:S(2)}, u32[]{:S(2)}) collective-permute-start(f32[4,8,258,1]{2,1,3,0:T(8,128)} %get-tuple-element.16), channel_id=1, source_target_pairs={{0,1},{1,2},{2,3},{3,4},{4,5},{5,6},{6,7},{7,8},{8,9},{9,10},{10,1... | collective-permute-start | bytes 99080 | tf_op jit(solution)/shard_map/ppermute | solution.py:17
  24.6 4.5 %collective-permute-start.2 = (f32[4,8,258,1]{2,1,3,0:T(8,128)}, f32[4,8,258,1]{2,1,3,0:T(8,128)}, u32[]{:S(2)}, u32[]{:S(2)}) collective-permute-start(f32[4,8,258,1]{2,1,3,0:T(8,128)} %get-tuple-element.17), channel_id=1, source_target_pairs={{1,0},{2,1},{3,2},{4,3},{5,4},{6,5},{7,6},{8,7},{9,8},{10,9},{11,1... | collective-permute-start | bytes 99080 | tf_op jit(solution)/shard_map/ppermute | solution.py:19
  48.0 11.0 %fusion.8 = (f32[4,8,256,128]{2,1,3,0:T(8,128)S(1)}, f32[4,8,256,128]{2,1,3,0:T(8,128)S(1)}) fusion(f32[4,8,1,128]{2,1,3,0:T(8,128)S(1)} %copy.48, f32[4,8,256,128]{2,1,3,0:T(8,128)} %copy.76, f32[4,8,1,128]{2,1,3,0:T(8,128)} %copy.50, f32[4,8,258,1]{2,1,3,0:T(8,128)} %collective-permute-done.3, f32[4,8,258,1]{2,1,3,0:T(8,128)} %collective-permute-done.2), kind=kLoop, calls=%fused_computation.27 | loop fusion | flops 12582912 | bytes 12681728 | tf_op jit(solution)/shard_map/mul | solution.py:32
  63.0 11.5 %multiply_add_fusion = (f32[4,8,256,128]{2,1,3,0:T(8,128)S(1)}, f32[4,8,256,128]{2,1,3,0:T(8,128)}) fusion(f32[4,8,256,128]{2,1,3,0:T(8,128)S(1)} %copy-done.2, f32[8,256,128]{1,0,2:T(8,128)} %copy.66, f32[4,256,128]{1,2,0:T(8,128)S(1)} %copy.65, f32[8,256,128]{1,0,2:T(8,128)} %copy.64, f32[4,256,128]{1,2,0:T(8,128)S(1)} %copy.63, f32[8,256,128]{1,0,2:T(8,128)} %copy.62, ...), kind=kLoop, calls=%fused_computation.25 | loop fusion | flops 36700160 | bytes 22512128 | tf_op jit(solution)/shard_map/add | solution.py:62
  81.9 4.1 %collective-permute-start.5 = (f32[4,8,1,128]{3,1,2,0:T(8,128)}, f32[4,8,1,128]{3,1,2,0:T(8,128)}, u32[]{:S(2)}, u32[]{:S(2)}) collective-permute-start(f32[4,8,1,128]{3,1,2,0:T(8,128)} %copy.71), channel_id=1, source_target_pairs={{0,16},{16,32},{32,48},{48,64},{64,80},{80,96},{96,112},{112,128},... | collective-permute-start | bytes 49160 | tf_op jit(solution)/shard_map/ppermute | solution.py:17
  87.5 2.7 %copy.72 = f32[4,8,1,128]{2,1,3,0:T(8,128)} copy(f32[4,8,1,128]{3,1,2,0:T(8,128)} %collective-permute-done.5) | data formatting | bytes 32768 | tf_op jit(solution)/shard_map/ppermute | solution.py:17
  93.3 6.3 %collective-permute-start.6 = (f32[4,8,258,1]{2,1,3,0:T(8,128)S(1)}, f32[4,8,258,1]{2,1,3,0:T(8,128)S(1)}, u32[]{:S(2)}, u32[]{:S(2)}) collective-permute-start(f32[4,8,258,1]{2,1,3,0:T(8,128)S(1)} %get-tuple-element.13), channel_id=1, source_target_pairs={{1,0},{2,1},{3,2},{4,3},{5,4},{6,5},{7,6},{8,7},{9,8},{10,9},{11,1... | collective-permute-start | bytes 99080 | tf_op jit(solution)/shard_map/ppermute | solution.py:19
  101.8 6.8 %fusion.10 = (f32[4,8,256,128]{2,1,3,0:T(8,128)S(1)}, f32[4,8,256,128]{2,1,3,0:T(8,128)}) fusion(f32[4,8,1,128]{2,1,3,0:T(8,128)S(1)} %copy.70, f32[4,8,256,128]{2,1,3,0:T(8,128)S(1)} %copy-done.1, f32[4,8,1,128]{2,1,3,0:T(8,128)S(1)} %copy-done.6, f32[4,8,258,1]{2,1,3,0:T(8,128)S(1)} %collective-permute-done.7, f32[4,8,258,1]{2,1,3,0:T(8,128)S(1)} %collective-permute-done.6), kind=kLoop, calls=%fused_computation.29 | loop fusion | flops 12582912 | bytes 12681728 | tf_op jit(solution)/shard_map/mul | solution.py:32
  108.6 3.4 %slice_multiply_fusion.1 = (f32[1,8,256,128]{2,1,3,0:T(8,128)S(1)}, f32[1,8,256,128]{2,1,3,0:T(8,128)}, f32[1,8,256,128]{2,1,3,0:T(8,128)}) fusion(f32[4,8,256,128]{2,1,3,0:T(8,128)S(1)} %get-tuple-element.10, f32[256,128]{0,1:T(8,128)S(1)} %copy-done.11, f32[4,8,256,128]{2,1,3,0:T(8,128)} %get-tuple-element.11), kind=kLoop, calls=%fused_computation.41 | loop fusion | flops 1048576 | bytes 7471104 | tf_op jit(solution)/shard_map/mul | solution.py:38
  112.1 10.4 %fusion.6 = f32[4,8,256,128]{2,1,3,0:T(8,128)S(1)} fusion(f32[4,8,256,128]{2,1,3,0:T(8,128)S(1)} %copy-done.3, f32[4,8,256,128]{2,1,3,0:T(8,128)} %get-tuple-element.9, f32[1,8,256,128]{2,1,3,0:T(8,128)} %get-tuple-element.19, f32[1,8,256,128]{2,1,3,0:T(8,128)} %get-tuple-element.20, f32[1,8,256,128]{2,1,3,0:T(8,128)S(1)} %get-tuple-element.18, ...), kind=kLoop, calls=%fused_computation.24 | loop fusion | flops 37748736 | bytes 26706432 | tf_op jit(solution)/shard_map/add | solution.py:64
  122.5 9.0 %fusion.11 = f32[8,8]{0,1:T(8,128)S(1)} fusion(f32[4,8,256,128]{2,1,3,0:T(8,128)S(1)} %fusion.6), kind=kOutput, calls=%fused_computation.35 | convolution fusion | flops 100663360 | bytes 4194560 | tf_op jit(solution)/shard_map/vcxy,vdxy->cd/dot_general | solution.py:69
  131.6 3.6 %collective-permute-done.8 = f32[8,8]{0,1:T(8,128)S(1)} collective-permute-done((f32[8,8]{0,1:T(8,128)S(1)}, f32[8,8]{0,1:T(8,128)S(1)}, u32[]{:S(2)}, u32[]{:S(2)}) %collective-permute-start.8) | collective-permute-done | bytes 288 | tf_op jit(solution)/shard_map/ppermute | solution.py:51
  135.2 3.7 %collective-permute-start.9 = (f32[8,8]{0,1:T(8,128)S(1)}, f32[8,8]{0,1:T(8,128)S(1)}, u32[]{:S(2)}, u32[]{:S(2)}) collective-permute-start(f32[8,8]{0,1:T(8,128)S(1)} %add.121), channel_id=1, source_target_pairs={{0,2},{1,3},{2,0},{3,1},{4,6},{5,7},{6,4},{7,5},{8,10},{9,11},{10,... | collective-permute-start | bytes 776 | tf_op jit(solution)/shard_map/ppermute | solution.py:51
  141.1 3.1 %collective-permute-done.10 = f32[8,8]{0,1:T(8,128)S(1)} collective-permute-done((f32[8,8]{0,1:T(8,128)S(1)}, f32[8,8]{0,1:T(8,128)S(1)}, u32[]{:S(2)}, u32[]{:S(2)}) %collective-permute-start.10) | collective-permute-done | bytes 288 | tf_op jit(solution)/shard_map/ppermute | solution.py:51
  146.1 3.2 %collective-permute-done.11 = f32[8,8]{0,1:T(8,128)S(1)} collective-permute-done((f32[8,8]{0,1:T(8,128)S(1)}, f32[8,8]{0,1:T(8,128)S(1)}, u32[]{:S(2)}, u32[]{:S(2)}) %collective-permute-start.11) | collective-permute-done | bytes 288 | tf_op jit(solution)/shard_map/ppermute | solution.py:51
  150.4 2.9 %collective-permute-start.13 = (f32[8,8]{0,1:T(8,128)S(1)}, f32[8,8]{0,1:T(8,128)S(1)}, u32[]{:S(2)}, u32[]{:S(2)}) collective-permute-start(f32[8,8]{0,1:T(8,128)S(1)} %add.125), channel_id=1, source_target_pairs={{0,32},{16,48},{32,0},{48,16},{64,96},{80,112},{96,64},{112,80},{1... | collective-permute-start | bytes 776 | tf_op jit(solution)/shard_map/ppermute | solution.py:51
  154.9 3.4 %collective-permute-start.14 = (f32[8,8]{0,1:T(8,128)S(1)}, f32[8,8]{0,1:T(8,128)S(1)}, u32[]{:S(2)}, u32[]{:S(2)}) collective-permute-start(f32[8,8]{0,1:T(8,128)S(1)} %add.126), channel_id=1, source_target_pairs={{0,64},{16,80},{32,96},{48,112},{64,0},{80,16},{96,32},{112,48},{1... | collective-permute-start | bytes 776 | tf_op jit(solution)/shard_map/ppermute | solution.py:51
  159.8 9.3 %collective-permute-start.15 = (f32[8,8]{0,1:T(8,128)S(1)}, f32[8,8]{0,1:T(8,128)S(1)}, u32[]{:S(2)}, u32[]{:S(2)}) collective-permute-start(f32[8,8]{0,1:T(8,128)S(1)} %add.127), channel_id=1, source_target_pairs={{0,128},{16,144},{32,160},{48,176},{64,192},{80,208},{96,224},{112... | collective-permute-start | bytes 776 | tf_op jit(solution)/shard_map/ppermute | solution.py:51
  169.1 5.5 %copy.80 = f32[4,8,256,128]{3,1,2,0:T(8,128)} copy(f32[4,8,256,128]{2,1,3,0:T(8,128)} %copy-done.4) | data formatting | bytes 8388608 | tf_op jit(solution)/shard_map/add | solution.py:64
  177.6 5.3 %convolution_bitcast_fusion = f32[4,8,256,128]{3,1,2,0:T(8,128)S(1)} fusion(f32[4,8,256,128]{3,1,2,0:T(8,128)} %copy.80, f32[8,8,1,1]{1,0,3,2:T(8,128)S(1)} %convolution_bitcast_fusion.1), kind=kOutput, calls=%fused_computation.30 | convolution fusion | flops 100663296 | bytes 8388864 | tf_op jit(solution)/shard_map/cd,vdxy->vcxy/dot_general | solution.py:75
  182.9 2.8 %copy.81 = f32[4,8,256,128]{3,2,1,0:T(8,128)} copy(f32[4,8,256,128]{3,1,2,0:T(8,128)S(1)} %convolution_bitcast_fusion) | data formatting | bytes 8388608
  (89 shorter events, 57.0 us)
Async XLA Ops:
  1.6 15.2 %collective-permute-start = (f32[4,8,1,128]{3,1,2,0:T(8,128)S(1)}, f32[4,8,1,128]{3,1,2,0:T(8,128)S(1)}, u32[]{:S(2)}, u32[]{:S(2)}) collective-permute-start(f32[4,8,1,128]{3,1,2,0:T(8,128)S(1)} %bitcast.57), channel_id=1, source_target_pairs={{16,0},{32,16},{48,32},{64,48},{80,64},{96,80},{112,96},{128,112},... | collective-permute-start | bytes 49160 | tf_op jit(solution)/shard_map/ppermute | solution.py:19
  2.9 7.0 %copy-start.9 = (f32[4,4,256,128]{3,2,1,0:T(8,128)S(1)}, f32[4,4,256,128]{3,2,1,0:T(8,128)}, u32[]{:S(2)}) copy-start(f32[4,4,256,128]{3,2,1,0:T(8,128)} %param.9) | copy-start | bytes 6291460
  2.9 14.6 %collective-permute-start.1 = (f32[4,8,1,128]{3,1,2,0:T(8,128)S(1)}, f32[4,8,1,128]{3,1,2,0:T(8,128)S(1)}, u32[]{:S(2)}, u32[]{:S(2)}) collective-permute-start(f32[4,8,1,128]{3,1,2,0:T(8,128)S(1)} %bitcast.56), channel_id=1, source_target_pairs={{0,16},{16,32},{32,48},{48,64},{64,80},{80,96},{96,112},{112,128},... | collective-permute-start | bytes 49160 | tf_op jit(solution)/shard_map/ppermute | solution.py:17
  19.6 9.5 %copy-start.12 = (f32[2,256,128]{2,1,0:T(8,128)S(1)}, f32[2,256,128]{2,1,0:T(8,128)}, u32[]{:S(2)}) copy-start(f32[2,256,128]{2,1,0:T(8,128)} %param.6) | copy-start | bytes 786436
  21.1 26.8 %collective-permute-start.3 = (f32[4,8,258,1]{2,1,3,0:T(8,128)}, f32[4,8,258,1]{2,1,3,0:T(8,128)}, u32[]{:S(2)}, u32[]{:S(2)}) collective-permute-start(f32[4,8,258,1]{2,1,3,0:T(8,128)} %get-tuple-element.16), channel_id=1, source_target_pairs={{0,1},{1,2},{2,3},{3,4},{4,5},{5,6},{6,7},{7,8},{8,9},{9,10},{10,1... | collective-permute-start | bytes 99080 | tf_op jit(solution)/shard_map/ppermute | solution.py:17
  24.6 23.4 %collective-permute-start.2 = (f32[4,8,258,1]{2,1,3,0:T(8,128)}, f32[4,8,258,1]{2,1,3,0:T(8,128)}, u32[]{:S(2)}, u32[]{:S(2)}) collective-permute-start(f32[4,8,258,1]{2,1,3,0:T(8,128)} %get-tuple-element.17), channel_id=1, source_target_pairs={{1,0},{2,1},{3,2},{4,3},{5,4},{6,5},{7,6},{8,7},{9,8},{10,9},{11,1... | collective-permute-start | bytes 99080 | tf_op jit(solution)/shard_map/ppermute | solution.py:19
  47.9 11.1 %copy-start.10 = (f32[256,128]{0,1:T(8,128)S(1)}, f32[256,128]{0,1:T(8,128)}, u32[]{:S(2)}) copy-start(f32[256,128]{0,1:T(8,128)} %copy.58) | copy-start | bytes 393220
  59.0 4.0 %copy-start.5 = (f32[4,8,1,128]{2,1,3,0:T(8,128)S(1)}, f32[4,8,1,128]{2,1,3,0:T(8,128)}, u32[]{:S(2)}) copy-start(f32[4,8,1,128]{2,1,3,0:T(8,128)} %copy.50) | copy-start | bytes 49156
  79.4 6.7 %collective-permute-start.4 = (f32[4,8,1,128]{3,1,2,0:T(8,128)S(1)}, f32[4,8,1,128]{3,1,2,0:T(8,128)}, u32[]{:S(2)}, u32[]{:S(2)}) collective-permute-start(f32[4,8,1,128]{3,1,2,0:T(8,128)S(1)} %copy.69), channel_id=1, source_target_pairs={{16,0},{32,16},{48,32},{64,48},{80,64},{96,80},{112,96},{128,112},... | collective-permute-start | bytes 49160 | tf_op jit(solution)/shard_map/ppermute | solution.py:19
  81.9 5.5 %collective-permute-start.5 = (f32[4,8,1,128]{3,1,2,0:T(8,128)}, f32[4,8,1,128]{3,1,2,0:T(8,128)}, u32[]{:S(2)}, u32[]{:S(2)}) collective-permute-start(f32[4,8,1,128]{3,1,2,0:T(8,128)} %copy.71), channel_id=1, source_target_pairs={{0,16},{16,32},{32,48},{48,64},{64,80},{80,96},{96,112},{112,128},... | collective-permute-start | bytes 49160 | tf_op jit(solution)/shard_map/ppermute | solution.py:17
  90.2 9.5 %copy-start.1 = (f32[4,8,256,128]{2,1,3,0:T(8,128)S(1)}, f32[4,8,256,128]{2,1,3,0:T(8,128)}, u32[]{:S(2)}) copy-start(f32[4,8,256,128]{2,1,3,0:T(8,128)} %copy-done) | copy-start | bytes 12582916
  91.2 10.5 %collective-permute-start.7 = (f32[4,8,258,1]{2,1,3,0:T(8,128)S(1)}, f32[4,8,258,1]{2,1,3,0:T(8,128)S(1)}, u32[]{:S(2)}, u32[]{:S(2)}) collective-permute-start(f32[4,8,258,1]{2,1,3,0:T(8,128)S(1)} %get-tuple-element.12), channel_id=1, source_target_pairs={{0,1},{1,2},{2,3},{3,4},{4,5},{5,6},{6,7},{7,8},{8,9},{9,10},{10,1... | collective-permute-start | bytes 99080 | tf_op jit(solution)/shard_map/ppermute | solution.py:17
  93.3 8.5 %copy-start.6 = (f32[4,8,1,128]{2,1,3,0:T(8,128)S(1)}, f32[4,8,1,128]{2,1,3,0:T(8,128)}, u32[]{:S(2)}) copy-start(f32[4,8,1,128]{2,1,3,0:T(8,128)} %copy.72) | copy-start | bytes 49156
  93.3 8.5 %collective-permute-start.6 = (f32[4,8,258,1]{2,1,3,0:T(8,128)S(1)}, f32[4,8,258,1]{2,1,3,0:T(8,128)S(1)}, u32[]{:S(2)}, u32[]{:S(2)}) collective-permute-start(f32[4,8,258,1]{2,1,3,0:T(8,128)S(1)} %get-tuple-element.13), channel_id=1, source_target_pairs={{1,0},{2,1},{3,2},{4,3},{5,4},{6,5},{7,6},{8,7},{9,8},{10,9},{11,1... | collective-permute-start | bytes 99080 | tf_op jit(solution)/shard_map/ppermute | solution.py:19
  101.8 6.8 %copy-start.11 = (f32[256,128]{0,1:T(8,128)S(1)}, f32[256,128]{0,1:T(8,128)}, u32[]{:S(2)}) copy-start(f32[256,128]{0,1:T(8,128)} %copy.58) | copy-start | bytes 393220
  122.5 9.0 %copy-start.4 = (f32[4,8,256,128]{2,1,3,0:T(8,128)}, f32[4,8,256,128]{2,1,3,0:T(8,128)S(1)}, u32[]{:S(2)}) copy-start(f32[4,8,256,128]{2,1,3,0:T(8,128)S(1)} %fusion.6) | copy-start | bytes 12582916
  131.6 3.6 %collective-permute-start.8 = (f32[8,8]{0,1:T(8,128)S(1)}, f32[8,8]{0,1:T(8,128)S(1)}, u32[]{:S(2)}, u32[]{:S(2)}) collective-permute-start(f32[8,8]{0,1:T(8,128)S(1)} %fusion.11), channel_id=1, source_target_pairs={{0,1},{1,0},{2,3},{3,2},{4,5},{5,4},{6,7},{7,6},{8,9},{9,8},{10,11... | collective-permute-start | bytes 776 | tf_op jit(solution)/shard_map/ppermute | solution.py:51
  135.2 5.3 %collective-permute-start.9 = (f32[8,8]{0,1:T(8,128)S(1)}, f32[8,8]{0,1:T(8,128)S(1)}, u32[]{:S(2)}, u32[]{:S(2)}) collective-permute-start(f32[8,8]{0,1:T(8,128)S(1)} %add.121), channel_id=1, source_target_pairs={{0,2},{1,3},{2,0},{3,1},{4,6},{5,7},{6,4},{7,5},{8,10},{9,11},{10,... | collective-permute-start | bytes 776 | tf_op jit(solution)/shard_map/ppermute | solution.py:51
  140.5 3.6 %collective-permute-start.10 = (f32[8,8]{0,1:T(8,128)S(1)}, f32[8,8]{0,1:T(8,128)S(1)}, u32[]{:S(2)}, u32[]{:S(2)}) collective-permute-start(f32[8,8]{0,1:T(8,128)S(1)} %add.122), channel_id=1, source_target_pairs={{0,4},{1,5},{2,6},{3,7},{4,0},{5,1},{6,2},{7,3},{8,12},{9,13},{10,... | collective-permute-start | bytes 776 | tf_op jit(solution)/shard_map/ppermute | solution.py:51
  144.1 5.1 %collective-permute-start.11 = (f32[8,8]{0,1:T(8,128)S(1)}, f32[8,8]{0,1:T(8,128)S(1)}, u32[]{:S(2)}, u32[]{:S(2)}) collective-permute-start(f32[8,8]{0,1:T(8,128)S(1)} %add.123), channel_id=1, source_target_pairs={{0,8},{1,9},{2,10},{3,11},{4,12},{5,13},{6,14},{7,15},{8,0},{9,1},... | collective-permute-start | bytes 776 | tf_op jit(solution)/shard_map/ppermute | solution.py:51
  149.2 1.2 collective-permute-start.12
  150.4 4.5 %collective-permute-start.13 = (f32[8,8]{0,1:T(8,128)S(1)}, f32[8,8]{0,1:T(8,128)S(1)}, u32[]{:S(2)}, u32[]{:S(2)}) collective-permute-start(f32[8,8]{0,1:T(8,128)S(1)} %add.125), channel_id=1, source_target_pairs={{0,32},{16,48},{32,0},{48,16},{64,96},{80,112},{96,64},{112,80},{1... | collective-permute-start | bytes 776 | tf_op jit(solution)/shard_map/ppermute | solution.py:51
  154.9 5.0 %collective-permute-start.14 = (f32[8,8]{0,1:T(8,128)S(1)}, f32[8,8]{0,1:T(8,128)S(1)}, u32[]{:S(2)}, u32[]{:S(2)}) collective-permute-start(f32[8,8]{0,1:T(8,128)S(1)} %add.126), channel_id=1, source_target_pairs={{0,64},{16,80},{32,96},{48,112},{64,0},{80,16},{96,32},{112,48},{1... | collective-permute-start | bytes 776 | tf_op jit(solution)/shard_map/ppermute | solution.py:51
  159.8 14.8 %collective-permute-start.15 = (f32[8,8]{0,1:T(8,128)S(1)}, f32[8,8]{0,1:T(8,128)S(1)}, u32[]{:S(2)}, u32[]{:S(2)}) collective-permute-start(f32[8,8]{0,1:T(8,128)S(1)} %add.127), channel_id=1, source_target_pairs={{0,128},{16,144},{32,160},{48,176},{64,192},{80,208},{96,224},{112... | collective-permute-start | bytes 776 | tf_op jit(solution)/shard_map/ppermute | solution.py:51
  (5 other events, 16.4 us)

commit v2 on v1

v2 whole, which is shorter than its diff:
```python
import jax
import jax.numpy as jnp
from jax import lax
from jax.experimental import pallas as pl
from jax.experimental.pallas import tpu as pltpu
from jax.sharding import PartitionSpec as P

STEP = 0.5
NV = 4


def all_sum(value):
    for axis in ("gy", "gx"):
        count = lax.axis_size(axis)
        bit = 1
        while bit < count:
            value = value + lax.ppermute(value, axis, [(i, i ^ bit) for i in range(count)])
            bit *= 2
    return value


def exchange(low, high, axis):
    count = lax.axis_size(axis)
    from_below = lax.ppermute(high, axis, [(i, i + 1) for i in range(count - 1)])
    from_above = lax.ppermute(low, axis, [(i + 1, i) for i in range(count - 1)])
    return from_below, from_above


def operator(q, west, east, south, north, vel_ref, visc_ref, snd_ref, coup_ref):
    nx, ny = q[0].shape
    rows = lax.broadcasted_iota(jnp.int32, (nx, ny), 0)
    lanes = lax.broadcasted_iota(jnp.int32, (nx, ny), 1)
    half = lax.broadcasted_iota(jnp.int32, (ny, nx), 0) < ny // 2
    vel0 = vel_ref[0]
    vel1 = vel_ref[1]
    visc = visc_ref[...]
    snd = snd_ref[...]
    grad_x, grad_y, transport = [], [], []
    for v in range(NV):
        field = q[v]
        columns = jnp.where(half, south[v], north[v]).T
        e = jnp.where(rows == nx - 1, east[v], pltpu.roll(field, nx - 1, 0))
        w = jnp.where(rows == 0, west[v], pltpu.roll(field, 1, 0))
        n = jnp.where(lanes == ny - 1, columns, pltpu.roll(field, ny - 1, 1))
        s = jnp.where(lanes == 0, columns, pltpu.roll(field, 1, 1))
        gx = 0.5 * (e - w)
        gy = 0.5 * (n - s)
        laplace = e + w + n + s - 4.0 * field
        grad_x.append(gx)
        grad_y.append(gy)
        transport.append(visc * laplace - vel0 * gx - vel1 * gy)
    divergence = grad_x[1] + grad_y[2]
    acoustic = [-snd * divergence, -snd * grad_x[3], -snd * grad_y[3], -snd * divergence]
    out = []
    for w_ in range(NV):
        mixing = coup_ref[w_, 0] * q[0]
        for inner in range(1, NV):
            mixing = mixing + coup_ref[w_, inner] * q[inner]
        out.append(transport[w_] + acoustic[w_] - mixing)
    return out


def stage_one(f_ref, vel_ref, visc_ref, snd_ref, coup_ref, hw_ref, he_ref, hs_ref, hn_ref,
              first_ref, mid_ref, mw_ref, me_ref, ms_ref, mn_ref):
    q = [f_ref[v, 0] for v in range(NV)]
    west = [hw_ref[0, v:v + 1, :] for v in range(NV)]
    east = [he_ref[0, v:v + 1, :] for v in range(NV)]
    south = [hs_ref[0, v:v + 1, :] for v in range(NV)]
    north = [hn_ref[0, v:v + 1, :] for v in range(NV)]
    lq = operator(q, west, east, south, north, vel_ref, visc_ref, snd_ref, coup_ref)
    nx, ny = q[0].shape
    for v in range(NV):
        first = lq[v] + q[v]
        middle = q[v] + STEP * first
        first_ref[v, 0] = first
        mid_ref[v, 0] = middle
        mw_ref[0, v:v + 1, :] = middle[0:1, :]
        me_ref[0, v:v + 1, :] = middle[nx - 1:nx, :]
        flipped = middle.T
        ms_ref[0, v:v + 1, :] = flipped[0:1, :]
        mn_ref[0, v:v + 1, :] = flipped[ny - 1:ny, :]


def stage_two(f_ref, first_ref, mid_ref, vel_ref, visc_ref, snd_ref, coup_ref, hw_ref, he_ref, hs_ref, hn_ref,
              resp_ref, gram_ref):
    c = pl.program_id(0)
    ncol = resp_ref.shape[1]
    nx, ny = f_ref.shape[2], f_ref.shape[3]
    q = [mid_ref[v, 0] for v in range(NV)]
    west = [hw_ref[0, v:v + 1, :] for v in range(NV)]
    east = [he_ref[0, v:v + 1, :] for v in range(NV)]
    south = [hs_ref[0, v:v + 1, :] for v in range(NV)]
    north = [hn_ref[0, v:v + 1, :] for v in range(NV)]
    lq = operator(q, west, east, south, north, vel_ref, visc_ref, snd_ref, coup_ref)
    resp = []
    for v in range(NV):
        forcing = f_ref[v, 0]
        second = lq[v] + forcing
        r = forcing + 0.5 * STEP * (first_ref[v, 0] + second)
        resp_ref[v, pl.ds(c, 1)] = r[None]
        resp.append(r)
    for d in range(ncol):
        @pl.when(d <= c)
        def _():
            acc = None
            for v in range(NV):
                prod = (resp_ref[v, d] * resp[v]).reshape(nx // 8, 8, ny).sum(axis=0)
                acc = prod if acc is None else acc + prod
            gram_ref[c * ncol + d] = acc
            gram_ref[d * ncol + c] = acc


def combine(inv_ref, r_ref, out_ref):
    ncol = r_ref.shape[1]
    rs = [r_ref[0, d] for d in range(ncol)]
    for c in range(ncol):
        acc = inv_ref[c, 0] * rs[0]
        for d in range(1, ncol):
            acc = acc + inv_ref[c, d] * rs[d]
        out_ref[0, c] = acc


def local(forcing, velocity, viscosity, sound, coupling):
    nv, ncol, nx, ny = forcing.shape
    f32 = jnp.float32
    whole = lambda shape: pl.BlockSpec(shape, lambda c: (0,) * len(shape))
    column = pl.BlockSpec((nv, 1, nx, ny), lambda c: (0, c, 0, 0))
    edge_x = pl.BlockSpec((1, nv, ny), lambda c: (c, 0, 0))
    edge_y = pl.BlockSpec((1, nv, nx), lambda c: (c, 0, 0))
    coef_specs = [whole((2, nx, ny)), whole((nx, ny)), whole((nx, ny)), whole((nv, nv, nx, ny))]
    params = pltpu.CompilerParams(vmem_limit_bytes=60 * 1024 * 1024)

    def by_column(a):
        return jnp.transpose(a, (1, 0, 2))

    hw, he = exchange(by_column(forcing[:, :, 0, :]), by_column(forcing[:, :, nx - 1, :]), "gx")
    hs, hn = exchange(by_column(forcing[:, :, :, 0]), by_column(forcing[:, :, :, ny - 1]), "gy")

    first, middle, mw, me, ms, mn = pl.pallas_call(
        stage_one,
        grid=(ncol,),
        in_specs=[column] + coef_specs + [edge_x, edge_x, edge_y, edge_y],
        out_specs=[column, column, edge_x, edge_x, edge_y, edge_y],
        out_shape=[
            jax.ShapeDtypeStruct(forcing.shape, f32),
            jax.ShapeDtypeStruct(forcing.shape, f32),
            jax.ShapeDtypeStruct((ncol, nv, ny), f32),
            jax.ShapeDtypeStruct((ncol, nv, ny), f32),
            jax.ShapeDtypeStruct((ncol, nv, nx), f32),
            jax.ShapeDtypeStruct((ncol, nv, nx), f32),
        ],
        compiler_params=params,
    )(forcing, velocity, viscosity, sound, coupling, hw, he, hs, hn)

    hw2, he2 = exchange(mw, me, "gx")
    hs2, hn2 = exchange(ms, mn, "gy")

    response, partial = pl.pallas_call(
        stage_two,
        grid=(ncol,),
        in_specs=[column, column, column] + coef_specs + [edge_x, edge_x, edge_y, edge_y],
        out_specs=[whole(forcing.shape), whole((ncol * ncol, 8, ny))],
        out_shape=[
            jax.ShapeDtypeStruct(forcing.shape, f32),
            jax.ShapeDtypeStruct((ncol * ncol, 8, ny), f32),
        ],
        compiler_params=pltpu.CompilerParams(
            vmem_limit_bytes=60 * 1024 * 1024, dimension_semantics=("arbitrary",)
        ),
    )(forcing, first, middle, velocity, viscosity, sound, coupling, hw2, he2, hs2, hn2)

    rows_total = float(nv * nx * ny * lax.axis_size("gx") * lax.axis_size("gy"))
    local_gram = jnp.sum(partial, axis=(1, 2)).reshape(ncol, ncol) / rows_total
    lower = jnp.linalg.cholesky(all_sum(local_gram))
    identity = jnp.eye(lower.shape[0], dtype=lower.dtype)
    inverse = lax.linalg.triangular_solve(lower, identity, left_side=True, lower=True)

    basis = pl.pallas_call(
        combine,
        grid=(nv,),
        in_specs=[
            pl.BlockSpec(memory_space=pltpu.SMEM),
            pl.BlockSpec((1, ncol, nx, ny), lambda v: (v, 0, 0, 0)),
        ],
        out_specs=pl.BlockSpec((1, ncol, nx, ny), lambda v: (v, 0, 0, 0)),
        out_shape=jax.ShapeDtypeStruct(forcing.shape, f32),
        compiler_params=params,
    )(inverse, response)
    return (basis, lower.T)


def solution(mesh):
    in_specs = (
        P(None, None, "gx", "gy"),
        P(None, "gx", "gy"),
        P("gx", "gy"),
        P("gx", "gy"),
        P(None, None, "gx", "gy"),
    )
    out_specs = (P(None, None, "gx", "gy"), P())
    return jax.shard_map(local, mesh=mesh, in_specs=in_specs, out_specs=out_specs, check_vma=False)
```

time: 189 us -> 125 us (0.66)
  other arithmetic: 51.2 us -> 4.21 us
  local copies, waits for them, and re-layouts: 56 us -> 17.5 us
  Pallas kernels: 0 us -> 32.6 us
  matrix products: 14.6 us -> 0.79 us
  waiting for transfers between devices: 15.8 us -> 27.2 us
  starting transfers between devices: 47.9 us -> 40.8 us
    pallas_call x0 -> x3, Pallas kernels: none -> 32.6 us  [the longest x1 14.3 us: local(): pl.pallas_call(stage_two, grid=(ncol,), in_specs=[column, column, column]...]
    mul x13 -> x0, local copies, waits for them, and re-layouts: 23.5 us -> none  [the longest x5 12.1 us: tendency(): mixing = coupling[:, 0][:, None] * center[0][None]]
    mul x5 -> x0, other arithmetic: 23.1 us -> none  [the longest x2 17.8 us: tendency(): grad_x = 0.5 * (east - west)]
    add x2 -> x0, other arithmetic: 21.9 us -> none  [the longest x1 11.5 us: local(): middle = forcing + STEP * first]
    dot_general x2 -> x0, matrix products: 14.4 us -> none  [the longest x1 9.03 us: local(): jnp.einsum('vcxy,vdxy->cd', response, response, precision=lax.Precision.H...]
    ppermute x4 -> x0, local copies, waits for them, and re-layouts: 6.85 us -> none  [the longest x2 4.74 us: with_halo(): lax.ppermute(tail, axis, [(i, (i + 1) % count) for i in range(ends)])]
    ppermute x8, waiting for transfers between devices: 0.02 us -> 5.98 us  [the longest x4 5.97 us: exchange(): from_above = lax.ppermute(low, axis, [(i + 1, i) for i in range(count - 1)])]
    add x1 -> x0, local copies, waits for them, and re-layouts: 5.52 us -> none  [local(): response = forcing + 0.5 * STEP * (first + second)]
  transfers between devices with their start and end apart: 16 -> 16, of which waited for: 7 -> 10; matrix products, arithmetic and copies ran while one was open for 22% -> 3% of each run, Pallas kernels for 0% -> 0%
where the time goes in v2:
time: 125 us; the launch traced here: 124 us
  starting transfers between devices  40.8 us (33%)
  Pallas kernels  32.6 us (26%)
  waiting for transfers between devices  27.2 us (22%)
  local copies, waits for them, and re-layouts  17.5 us (14%)
  other arithmetic  4.21 us (3%)
    ppermute x8, waiting for transfers between devices, all_sum(): lax.ppermute(value, axis, [(i, i ^ bit) for i in range(count)])  21.2 us
    ppermute x8, starting transfers between devices, all_sum(): lax.ppermute(value, axis, [(i, i ^ bit) for i in range(count)])  17.2 us
    pallas_call x1, Pallas kernels, local(): pl.pallas_call(stage_two, grid=(ncol,), in_specs=[column, column, column]...  14.3 us
    ppermute x4, starting transfers between devices, exchange(): from_above = lax.ppermute(low, axis, [(i + 1, i) for i in range(count - 1)])  13.1 us
    pallas_call x1, Pallas kernels, local(): pl.pallas_call(stage_one, grid=(ncol,), in_specs=[column] + coef_specs +...  12.5 us
    ppermute x4, starting transfers between devices, exchange(): lax.ppermute(high, axis, [(i, i + 1) for i in range(count - 1)])  10.5 us
    unnamed x21, local copies, waits for them, and re-layouts  8.2 us
    slice x1, local copies, waits for them, and re-layouts, local(): forcing[:, :, :, 0]  8.1 us
  transfers between devices with their start and end apart: 16, of which 10 were waited for; matrix products, arithmetic and copies ran while one was open for 3% of the time, Pallas kernels for 0%

profile of v2, /device:TPU:2, one launch (start us, length us, event | category | flops | bytes accessed | tf_op | source)
XLA Modules:
  0.0 123.9 jit_solution(10521897492455451188)
XLA Ops:
  0.6 8.1 %fusion.4 = (f32[4,8,256,1]{3,2,1,0:T(8,128)}, f32[4,8,256,1]{3,2,1,0:T(8,128)}) fusion(f32[4,8,256,128]{3,2,1,0:T(8,128)} %f_ref.3), kind=kLoop, calls=%fused_computation.14 | loop fusion | bytes 131072 | tf_op jit(solution)/shard_map/slice | solution.py:137
  8.7 2.8 %copy.18 = f32[4,8,256,1]{2,0,1,3:T(4,128)S(1)} copy(f32[4,8,256,1]{3,2,1,0:T(8,128)} %get-tuple-element.21) | data formatting | bytes 65536
  11.6 3.5 %collective-permute-start.2 = (f32[8,4,256]{2,1,0:T(4,128)S(1)}, f32[8,4,256]{2,1,0:T(4,128)S(1)}, u32[]{:S(2)}, u32[]{:S(2)}) collective-permute-start(f32[8,4,256]{2,1,0:T(4,128)S(1)} %bitcast.28), channel_id=1, source_target_pairs={{0,1},{1,2},{2,3},{3,4},{4,5},{5,6},{6,7},{7,8},{8,9},{9,10},{10,1... | collective-permute-start | bytes 98312 | tf_op jit(solution)/shard_map/ppermute | solution.py:24
  15.1 2.9 %copy.19 = f32[4,8,256,1]{2,0,1,3:T(4,128)S(1)} copy(f32[4,8,256,1]{3,2,1,0:T(8,128)} %get-tuple-element.20) | data formatting | bytes 65536
  17.9 4.5 %collective-permute-start.3 = (f32[8,4,256]{2,1,0:T(4,128)S(1)}, f32[8,4,256]{2,1,0:T(4,128)S(1)}, u32[]{:S(2)}, u32[]{:S(2)}) collective-permute-start(f32[8,4,256]{2,1,0:T(4,128)S(1)} %bitcast.29), channel_id=1, source_target_pairs={{1,0},{2,1},{3,2},{4,3},{5,4},{6,5},{7,6},{8,7},{9,8},{10,9},{11,1... | collective-permute-start | bytes 98312 | tf_op jit(solution)/shard_map/ppermute | solution.py:25
  26.0 3.9 %collective-permute-done.1.he_ref = f32[8,4,128]{2,1,0:T(4,128)S(1)} collective-permute-done((f32[8,4,128]{2,1,0:T(4,128)S(1)}, f32[8,4,128]{2,1,0:T(4,128)S(1)}, u32[]{:S(2)}, u32[]{:S(2)}) %collective-permute-start.1) | collective-permute-done | bytes 16416 | tf_op jit(solution)/shard_map/ppermute | solution.py:25
  31.2 12.5 %shard_map.68 = (f32[4,8,256,128]{3,2,1,0:T(8,128)}, f32[4,8,256,128]{3,2,1,0:T(8,128)}, f32[8,4,128]{2,1,0:T(4,128)}, f32[8,4,128]{2,1,0:T(4,128)}, f32[8,4,256]{2,1,0:T(4,128)}, /*index=5*/f32[8,4,256]{2,1,0:T(4,128)}) custom-call(f32[4,8,256,128]{3,2,1,0:T(8,128)} %f_ref.3, f32[2,256,128]{2,1,0:T(8,128)} %vel_ref.3, f32[256,128]{1,0:T(8,128)} %visc_ref.3, ...), custom_call_target="tpu_custom_call" | custom-call | tf_op jit(solution)/shard_map/pallas_call | solution.py:139
  43.7 1.9 %collective-permute-start.6 = (f32[8,4,256]{2,1,0:T(4,128)}, f32[8,4,256]{2,1,0:T(4,128)S(1)}, u32[]{:S(2)}, u32[]{:S(2)}) collective-permute-start(f32[8,4,256]{2,1,0:T(4,128)} %get-tuple-element.14), channel_id=1, source_target_pairs={{0,1},{1,2},{2,3},{3,4},{4,5},{5,6},{6,7},{7,8},{8,9},{9,10},{10,1... | collective-permute-start | bytes 98312 | tf_op jit(solution)/shard_map/ppermute | solution.py:24
  45.7 6.0 %collective-permute-start.7 = (f32[8,4,256]{2,1,0:T(4,128)}, f32[8,4,256]{2,1,0:T(4,128)S(1)}, u32[]{:S(2)}, u32[]{:S(2)}) collective-permute-start(f32[8,4,256]{2,1,0:T(4,128)} %get-tuple-element.15), channel_id=1, source_target_pairs={{1,0},{2,1},{3,2},{4,3},{5,4},{6,5},{7,6},{8,7},{9,8},{10,9},{11,1... | collective-permute-start | bytes 98312 | tf_op jit(solution)/shard_map/ppermute | solution.py:25
  51.7 3.8 %collective-permute-start.4 = (f32[8,4,128]{2,1,0:T(4,128)}, f32[8,4,128]{2,1,0:T(4,128)S(1)}, u32[]{:S(2)}, u32[]{:S(2)}) collective-permute-start(f32[8,4,128]{2,1,0:T(4,128)} %get-tuple-element.12), channel_id=1, source_target_pairs={{0,16},{16,32},{32,48},{48,64},{64,80},{80,96},{96,112},{112,128},... | collective-permute-start | bytes 49160 | tf_op jit(solution)/shard_map/ppermute | solution.py:24
  56.9 2.1 %collective-permute-done.5.he_ref = f32[8,4,128]{2,1,0:T(4,128)S(1)} collective-permute-done((f32[8,4,128]{2,1,0:T(4,128)}, f32[8,4,128]{2,1,0:T(4,128)S(1)}, u32[]{:S(2)}, u32[]{:S(2)}) %collective-permute-start.5) | collective-permute-done | bytes 16416 | tf_op jit(solution)/shard_map/ppermute | solution.py:25
  59.5 14.3 %shard_map.69 = (f32[4,8,256,128]{3,2,1,0:T(8,128)}, f32[64,8,128]{2,1,0:T(8,128)}) custom-call(f32[4,8,256,128]{3,2,1,0:T(8,128)} %f_ref.3, f32[4,8,256,128]{3,2,1,0:T(8,128)} %get-tuple-element.10.first_ref, f32[4,8,256,128]{3,2,1,0:T(8,128)} %get-tuple-element.11.mid_ref, f32[2,256,128]{2,1,0:T(8,128)} %vel_ref.3, f32[256,128]{1,0:T(8,128)} %visc_ref.3, ...), custom_call_target="tpu_custom_call" | custom-call | tf_op jit(solution)/shard_map/pallas_call | solution.py:158
  75.5 3.6 %collective-permute-done.8 = f32[8,8]{0,1:T(8,128)S(1)} collective-permute-done((f32[8,8]{0,1:T(8,128)S(1)}, f32[8,8]{0,1:T(8,128)S(1)}, u32[]{:S(2)}, u32[]{:S(2)}) %collective-permute-start.8) | collective-permute-done | bytes 288 | tf_op jit(solution)/shard_map/ppermute | solution.py:17
  79.1 5.1 %collective-permute-done.9 = f32[8,8]{0,1:T(8,128)S(1)} collective-permute-done((f32[8,8]{0,1:T(8,128)S(1)}, f32[8,8]{0,1:T(8,128)S(1)}, u32[]{:S(2)}, u32[]{:S(2)}) %collective-permute-start.9) | collective-permute-done | bytes 288 | tf_op jit(solution)/shard_map/ppermute | solution.py:17
  84.2 3.6 %collective-permute-done.10 = f32[8,8]{0,1:T(8,128)S(1)} collective-permute-done((f32[8,8]{0,1:T(8,128)S(1)}, f32[8,8]{0,1:T(8,128)S(1)}, u32[]{:S(2)}, u32[]{:S(2)}) %collective-permute-start.10) | collective-permute-done | bytes 288 | tf_op jit(solution)/shard_map/ppermute | solution.py:17
  87.8 2.1 %collective-permute-start.11 = (f32[8,8]{0,1:T(8,128)S(1)}, f32[8,8]{0,1:T(8,128)S(1)}, u32[]{:S(2)}, u32[]{:S(2)}) collective-permute-start(f32[8,8]{0,1:T(8,128)S(1)} %add.37), channel_id=1, source_target_pairs={{0,8},{1,9},{2,10},{3,11},{4,12},{5,13},{6,14},{7,15},{8,0},{9,1},... | collective-permute-start | bytes 776 | tf_op jit(solution)/shard_map/ppermute | solution.py:17
  89.9 3.0 %collective-permute-done.11 = f32[8,8]{0,1:T(8,128)S(1)} collective-permute-done((f32[8,8]{0,1:T(8,128)S(1)}, f32[8,8]{0,1:T(8,128)S(1)}, u32[]{:S(2)}, u32[]{:S(2)}) %collective-permute-start.11) | collective-permute-done | bytes 288 | tf_op jit(solution)/shard_map/ppermute | solution.py:17
  94.1 2.4 %collective-permute-start.13 = (f32[8,8]{0,1:T(8,128)S(1)}, f32[8,8]{0,1:T(8,128)S(1)}, u32[]{:S(2)}, u32[]{:S(2)}) collective-permute-start(f32[8,8]{0,1:T(8,128)S(1)} %add.39), channel_id=1, source_target_pairs={{0,32},{16,48},{32,0},{48,16},{64,96},{80,112},{96,64},{112,80},{1... | collective-permute-start | bytes 776 | tf_op jit(solution)/shard_map/ppermute | solution.py:17
  96.5 1.6 %collective-permute-done.13 = f32[8,8]{0,1:T(8,128)S(1)} collective-permute-done((f32[8,8]{0,1:T(8,128)S(1)}, f32[8,8]{0,1:T(8,128)S(1)}, u32[]{:S(2)}, u32[]{:S(2)}) %collective-permute-start.13) | collective-permute-done | bytes 288 | tf_op jit(solution)/shard_map/ppermute | solution.py:17
  98.1 5.4 %collective-permute-start.14 = (f32[8,8]{0,1:T(8,128)S(1)}, f32[8,8]{0,1:T(8,128)S(1)}, u32[]{:S(2)}, u32[]{:S(2)}) collective-permute-start(f32[8,8]{0,1:T(8,128)S(1)} %add.40), channel_id=1, source_target_pairs={{0,64},{16,80},{32,96},{48,112},{64,0},{80,16},{96,32},{112,48},{1... | collective-permute-start | bytes 776 | tf_op jit(solution)/shard_map/ppermute | solution.py:17
  103.5 1.6 %collective-permute-done.14 = f32[8,8]{0,1:T(8,128)S(1)} collective-permute-done((f32[8,8]{0,1:T(8,128)S(1)}, f32[8,8]{0,1:T(8,128)S(1)}, u32[]{:S(2)}, u32[]{:S(2)}) %collective-permute-start.14) | collective-permute-done | bytes 288 | tf_op jit(solution)/shard_map/ppermute | solution.py:17
  105.1 7.2 %collective-permute-start.15 = (f32[8,8]{0,1:T(8,128)S(1)}, f32[8,8]{0,1:T(8,128)S(1)}, u32[]{:S(2)}, u32[]{:S(2)}) collective-permute-start(f32[8,8]{0,1:T(8,128)S(1)} %add.41), channel_id=1, source_target_pairs={{0,128},{16,144},{32,160},{48,176},{64,192},{80,208},{96,224},{112... | collective-permute-start | bytes 776 | tf_op jit(solution)/shard_map/ppermute | solution.py:17
  112.3 1.6 %collective-permute-done.15 = f32[8,8]{0,1:T(8,128)S(1)} collective-permute-done((f32[8,8]{0,1:T(8,128)S(1)}, f32[8,8]{0,1:T(8,128)S(1)}, u32[]{:S(2)}, u32[]{:S(2)}) %collective-permute-start.15) | collective-permute-done | bytes 288 | tf_op jit(solution)/shard_map/ppermute | solution.py:17
  118.1 5.8 %shard_map.70 = f32[4,8,256,128]{3,2,1,0:T(8,128)} custom-call(f32[8,8]{1,0:T(8,128)} %fusion.inv_ref, f32[4,8,256,128]{3,2,1,0:T(8,128)} %get-tuple-element.17.r_ref), custom_call_target="tpu_custom_call" | custom-call | tf_op jit(solution)/shard_map/pallas_call | solution.py:178
  (54 shorter events, 13.8 us)
Async XLA Ops:
  11.6 18.4 %collective-permute-start.2 = (f32[8,4,256]{2,1,0:T(4,128)S(1)}, f32[8,4,256]{2,1,0:T(4,128)S(1)}, u32[]{:S(2)}, u32[]{:S(2)}) collective-permute-start(f32[8,4,256]{2,1,0:T(4,128)S(1)} %bitcast.28), channel_id=1, source_target_pairs={{0,1},{1,2},{2,3},{3,4},{4,5},{5,6},{6,7},{7,8},{8,9},{9,10},{10,1... | collective-permute-start | bytes 98312 | tf_op jit(solution)/shard_map/ppermute | solution.py:24
  17.9 12.0 %collective-permute-start.3 = (f32[8,4,256]{2,1,0:T(4,128)S(1)}, f32[8,4,256]{2,1,0:T(4,128)S(1)}, u32[]{:S(2)}, u32[]{:S(2)}) collective-permute-start(f32[8,4,256]{2,1,0:T(4,128)S(1)} %bitcast.29), channel_id=1, source_target_pairs={{1,0},{2,1},{3,2},{4,3},{5,4},{6,5},{7,6},{8,7},{9,8},{10,9},{11,1... | collective-permute-start | bytes 98312 | tf_op jit(solution)/shard_map/ppermute | solution.py:25
  23.4 2.6 %collective-permute-start = (f32[8,4,128]{2,1,0:T(4,128)S(1)}, f32[8,4,128]{2,1,0:T(4,128)S(1)}, u32[]{:S(2)}, u32[]{:S(2)}) collective-permute-start(f32[8,4,128]{2,1,0:T(4,128)S(1)} %bitcast.30), channel_id=1, source_target_pairs={{0,16},{16,32},{32,48},{48,64},{64,80},{80,96},{96,112},{112,128},... | collective-permute-start | bytes 49160 | tf_op jit(solution)/shard_map/ppermute | solution.py:24
  24.7 5.2 %collective-permute-start.1 = (f32[8,4,128]{2,1,0:T(4,128)S(1)}, f32[8,4,128]{2,1,0:T(4,128)S(1)}, u32[]{:S(2)}, u32[]{:S(2)}) collective-permute-start(f32[8,4,128]{2,1,0:T(4,128)S(1)} %bitcast.31), channel_id=1, source_target_pairs={{16,0},{32,16},{48,32},{64,48},{80,64},{96,80},{112,96},{128,112},... | collective-permute-start | bytes 49160 | tf_op jit(solution)/shard_map/ppermute | solution.py:25
  26.0 3.9 %copy-start.4 = (f32[8,4,128]{2,1,0:T(4,128)}, f32[8,4,128]{2,1,0:T(4,128)S(1)}, u32[]{:S(2)}) copy-start(f32[8,4,128]{2,1,0:T(4,128)S(1)} %collective-permute-done.hw_ref) | copy-start | bytes 49156
  29.9 0.6 copy-start.5
  29.9 0.6 copy-start
  30.6 0.6 copy-start.1
  43.7 15.2 %collective-permute-start.6 = (f32[8,4,256]{2,1,0:T(4,128)}, f32[8,4,256]{2,1,0:T(4,128)S(1)}, u32[]{:S(2)}, u32[]{:S(2)}) collective-permute-start(f32[8,4,256]{2,1,0:T(4,128)} %get-tuple-element.14), channel_id=1, source_target_pairs={{0,1},{1,2},{2,3},{3,4},{4,5},{5,6},{6,7},{7,8},{8,9},{9,10},{10,1... | collective-permute-start | bytes 98312 | tf_op jit(solution)/shard_map/ppermute | solution.py:24
  45.7 13.3 %collective-permute-start.7 = (f32[8,4,256]{2,1,0:T(4,128)}, f32[8,4,256]{2,1,0:T(4,128)S(1)}, u32[]{:S(2)}, u32[]{:S(2)}) collective-permute-start(f32[8,4,256]{2,1,0:T(4,128)} %get-tuple-element.15), channel_id=1, source_target_pairs={{1,0},{2,1},{3,2},{4,3},{5,4},{6,5},{7,6},{8,7},{9,8},{10,9},{11,1... | collective-permute-start | bytes 98312 | tf_op jit(solution)/shard_map/ppermute | solution.py:25
  51.7 5.1 %collective-permute-start.4 = (f32[8,4,128]{2,1,0:T(4,128)}, f32[8,4,128]{2,1,0:T(4,128)S(1)}, u32[]{:S(2)}, u32[]{:S(2)}) collective-permute-start(f32[8,4,128]{2,1,0:T(4,128)} %get-tuple-element.12), channel_id=1, source_target_pairs={{0,16},{16,32},{32,48},{48,64},{64,80},{80,96},{96,112},{112,128},... | collective-permute-start | bytes 49160 | tf_op jit(solution)/shard_map/ppermute | solution.py:24
  55.5 3.4 %collective-permute-start.5 = (f32[8,4,128]{2,1,0:T(4,128)}, f32[8,4,128]{2,1,0:T(4,128)S(1)}, u32[]{:S(2)}, u32[]{:S(2)}) collective-permute-start(f32[8,4,128]{2,1,0:T(4,128)} %get-tuple-element.13), channel_id=1, source_target_pairs={{16,0},{32,16},{48,32},{64,48},{80,64},{96,80},{112,96},{128,112},... | collective-permute-start | bytes 49160 | tf_op jit(solution)/shard_map/ppermute | solution.py:25
  56.8 2.1 %copy-start.6 = (f32[8,4,128]{2,1,0:T(4,128)}, f32[8,4,128]{2,1,0:T(4,128)S(1)}, u32[]{:S(2)}) copy-start(f32[8,4,128]{2,1,0:T(4,128)S(1)} %collective-permute-done.4.hw_ref) | copy-start | bytes 49156
  58.9 0.6 copy-start.7
  58.9 0.6 copy-start.2
  58.9 0.6 copy-start.3
  75.5 3.6 %collective-permute-start.8 = (f32[8,8]{0,1:T(8,128)S(1)}, f32[8,8]{0,1:T(8,128)S(1)}, u32[]{:S(2)}, u32[]{:S(2)}) collective-permute-start(f32[8,8]{0,1:T(8,128)S(1)} %copy.12), channel_id=1, source_target_pairs={{0,1},{1,0},{2,3},{3,2},{4,5},{5,4},{6,7},{7,6},{8,9},{9,8},{10,11... | collective-permute-start | bytes 776 | tf_op jit(solution)/shard_map/ppermute | solution.py:17
  79.1 5.1 %collective-permute-start.9 = (f32[8,8]{0,1:T(8,128)S(1)}, f32[8,8]{0,1:T(8,128)S(1)}, u32[]{:S(2)}, u32[]{:S(2)}) collective-permute-start(f32[8,8]{0,1:T(8,128)S(1)} %add.35), channel_id=1, source_target_pairs={{0,2},{1,3},{2,0},{3,1},{4,6},{5,7},{6,4},{7,5},{8,10},{9,11},{10,... | collective-permute-start | bytes 776 | tf_op jit(solution)/shard_map/ppermute | solution.py:17
  84.2 3.6 %collective-permute-start.10 = (f32[8,8]{0,1:T(8,128)S(1)}, f32[8,8]{0,1:T(8,128)S(1)}, u32[]{:S(2)}, u32[]{:S(2)}) collective-permute-start(f32[8,8]{0,1:T(8,128)S(1)} %add.36), channel_id=1, source_target_pairs={{0,4},{1,5},{2,6},{3,7},{4,0},{5,1},{6,2},{7,3},{8,12},{9,13},{10,... | collective-permute-start | bytes 776 | tf_op jit(solution)/shard_map/ppermute | solution.py:17
  87.8 5.1 %collective-permute-start.11 = (f32[8,8]{0,1:T(8,128)S(1)}, f32[8,8]{0,1:T(8,128)S(1)}, u32[]{:S(2)}, u32[]{:S(2)}) collective-permute-start(f32[8,8]{0,1:T(8,128)S(1)} %add.37), channel_id=1, source_target_pairs={{0,8},{1,9},{2,10},{3,11},{4,12},{5,13},{6,14},{7,15},{8,0},{9,1},... | collective-permute-start | bytes 776 | tf_op jit(solution)/shard_map/ppermute | solution.py:17
  92.9 1.2 collective-permute-start.12
  94.1 4.0 %collective-permute-start.13 = (f32[8,8]{0,1:T(8,128)S(1)}, f32[8,8]{0,1:T(8,128)S(1)}, u32[]{:S(2)}, u32[]{:S(2)}) collective-permute-start(f32[8,8]{0,1:T(8,128)S(1)} %add.39), channel_id=1, source_target_pairs={{0,32},{16,48},{32,0},{48,16},{64,96},{80,112},{96,64},{112,80},{1... | collective-permute-start | bytes 776 | tf_op jit(solution)/shard_map/ppermute | solution.py:17
  98.1 7.0 %collective-permute-start.14 = (f32[8,8]{0,1:T(8,128)S(1)}, f32[8,8]{0,1:T(8,128)S(1)}, u32[]{:S(2)}, u32[]{:S(2)}) collective-permute-start(f32[8,8]{0,1:T(8,128)S(1)} %add.40), channel_id=1, source_target_pairs={{0,64},{16,80},{32,96},{48,112},{64,0},{80,16},{96,32},{112,48},{1... | collective-permute-start | bytes 776 | tf_op jit(solution)/shard_map/ppermute | solution.py:17
  105.1 8.8 %collective-permute-start.15 = (f32[8,8]{0,1:T(8,128)S(1)}, f32[8,8]{0,1:T(8,128)S(1)}, u32[]{:S(2)}, u32[]{:S(2)}) collective-permute-start(f32[8,8]{0,1:T(8,128)S(1)} %add.41), channel_id=1, source_target_pairs={{0,128},{16,144},{32,160},{48,176},{64,192},{80,208},{96,224},{112... | collective-permute-start | bytes 776 | tf_op jit(solution)/shard_map/ppermute | solution.py:17

commit v3 on v2

--- a/solution.py
+++ b/solution.py
@@ -106,8 +106,20 @@
             for v in range(NV):
                 prod = (resp_ref[v, d] * resp[v]).reshape(nx // 8, 8, ny).sum(axis=0)
                 acc = prod if acc is None else acc + prod
-            gram_ref[c * ncol + d] = acc
-            gram_ref[d * ncol + c] = acc
+            total = jnp.sum(acc)
+            gram_ref[c * ncol + d] = total
+            gram_ref[d * ncol + c] = total
+
+
+def edges(f_ref, w_ref, e_ref, s_ref, n_ref):
+    nx, ny = f_ref.shape[2], f_ref.shape[3]
+    for v in range(NV):
+        field = f_ref[v, 0]
+        w_ref[0, v:v + 1, :] = field[0:1, :]
+        e_ref[0, v:v + 1, :] = field[nx - 1:nx, :]
+        flipped = field.T
+        s_ref[0, v:v + 1, :] = flipped[0:1, :]
+        n_ref[0, v:v + 1, :] = flipped[ny - 1:ny, :]
 
 
 def combine(inv_ref, r_ref, out_ref):
@@ -130,11 +142,21 @@
     coef_specs = [whole((2, nx, ny)), whole((nx, ny)), whole((nx, ny)), whole((nv, nv, nx, ny))]
     params = pltpu.CompilerParams(vmem_limit_bytes=60 * 1024 * 1024)
 
-    def by_column(a):
-        return jnp.transpose(a, (1, 0, 2))
-
-    hw, he = exchange(by_column(forcing[:, :, 0, :]), by_column(forcing[:, :, nx - 1, :]), "gx")
-    hs, hn = exchange(by_column(forcing[:, :, :, 0]), by_column(forcing[:, :, :, ny - 1]), "gy")
+    fw, fe, fs, fn = pl.pallas_call(
+        edges,
+        grid=(ncol,),
+        in_specs=[column],
+        out_specs=[edge_x, edge_x, edge_y, edge_y],
+        out_shape=[
+            jax.ShapeDtypeStruct((ncol, nv, ny), f32),
+            jax.ShapeDtypeStruct((ncol, nv, ny), f32),
+            jax.ShapeDtypeStruct((ncol, nv, nx), f32),
+            jax.ShapeDtypeStruct((ncol, nv, nx), f32),
+        ],
+        compiler_params=params,
+    )(forcing)
+    hw, he = exchange(fw, fe, "gx")
+    hs, hn = exchange(fs, fn, "gy")
 
     first, middle, mw, me, ms, mn = pl.pallas_call(
         stage_one,
@@ -159,10 +181,10 @@
         stage_two,
         grid=(ncol,),
         in_specs=[column, column, column] + coef_specs + [edge_x, edge_x, edge_y, edge_y],
-        out_specs=[whole(forcing.shape), whole((ncol * ncol, 8, ny))],
+        out_specs=[whole(forcing.shape), pl.BlockSpec(memory_space=pltpu.SMEM)],
         out_shape=[
             jax.ShapeDtypeStruct(forcing.shape, f32),
-            jax.ShapeDtypeStruct((ncol * ncol, 8, ny), f32),
+            jax.ShapeDtypeStruct((ncol * ncol,), f32),
         ],
         compiler_params=pltpu.CompilerParams(
             vmem_limit_bytes=60 * 1024 * 1024, dimension_semantics=("arbitrary",)
@@ -170,7 +192,7 @@
     )(forcing, first, middle, velocity, viscosity, sound, coupling, hw2, he2, hs2, hn2)
 
     rows_total = float(nv * nx * ny * lax.axis_size("gx") * lax.axis_size("gy"))
-    local_gram = jnp.sum(partial, axis=(1, 2)).reshape(ncol, ncol) / rows_total
+    local_gram = partial.reshape(ncol, ncol) / rows_total
     lower = jnp.linalg.cholesky(all_sum(local_gram))
     identity = jnp.eye(lower.shape[0], dtype=lower.dtype)
     inverse = lax.linalg.triangular_solve(lower, identity, left_side=True, lower=True)

time: 125 us -> 119 us (0.952)
  local copies, waits for them, and re-layouts: 17.5 us -> 2.73 us
  Pallas kernels: 32.6 us -> 42.7 us
    slice x2 -> x0, local copies, waits for them, and re-layouts: 9.09 us -> none  [the longest x1 8.1 us: local(): forcing[:, :, :, 0]]
    pallas_call x0 -> x1, Pallas kernels: none -> 6.34 us  [local(): pl.pallas_call(edges, grid=(ncol,), in_specs=[column], out_specs=[edge_x,...]
    unnamed x21 -> x17, local copies, waits for them, and re-layouts: 8.2 us -> 2.51 us
    pallas_call x1, Pallas kernels: 14.3 us -> 18 us  [local(): pl.pallas_call(stage_two, grid=(ncol,), in_specs=[column, column, column]...]
    reduce_sum x1 -> x0, other arithmetic: 1.5 us -> none  [local(): local_gram = jnp.sum(partial, axis=(1, 2)).reshape(ncol, ncol) / rows_total]
  transfers between devices with their start and end apart: 16 -> 16, of which waited for: 10 -> 10; matrix products, arithmetic and copies ran while one was open for 3% -> 0% of each run, Pallas kernels for 0% -> 0%
where the time goes in v3:
time: 119 us
  Pallas kernels  42.7 us (36%)
  starting transfers between devices  40.7 us (34%)
  waiting for transfers between devices  27.4 us (23%)
  other arithmetic  3.36 us (3%)
  local copies, waits for them, and re-layouts  2.73 us (2%)
    ppermute x8, waiting for transfers between devices, all_sum(): lax.ppermute(value, axis, [(i, i ^ bit) for i in range(count)])  21.2 us
    pallas_call x1, Pallas kernels, local(): pl.pallas_call(stage_two, grid=(ncol,), in_specs=[column, column, column]...  18 us
    ppermute x8, starting transfers between devices, all_sum(): lax.ppermute(value, axis, [(i, i ^ bit) for i in range(count)])  17.2 us
    ppermute x4, starting transfers between devices, exchange(): from_above = lax.ppermute(low, axis, [(i + 1, i) for i in range(count - 1)])  13.1 us
    pallas_call x1, Pallas kernels, local(): pl.pallas_call(stage_one, grid=(ncol,), in_specs=[column] + coef_specs +...  12.5 us
    ppermute x4, starting transfers between devices, exchange(): lax.ppermute(high, axis, [(i, i + 1) for i in range(count - 1)])  10.5 us
    pallas_call x1, Pallas kernels, local(): pl.pallas_call(edges, grid=(ncol,), in_specs=[column], out_specs=[edge_x,...  6.34 us
    ppermute x4, waiting for transfers between devices, exchange(): from_above = lax.ppermute(low, axis, [(i + 1, i) for i in range(count - 1)])  6.18 us
  transfers between devices with their start and end apart: 16, of which 10 were waited for; matrix products, arithmetic and copies ran while one was open for 0% of the time, Pallas kernels for 0%

profile of v3, /device:TPU:2, one launch (start us, length us, event | category | flops | bytes accessed | tf_op | source)
XLA Modules:
  0.0 118.5 jit_solution(11687507664457692662)
XLA Ops:
  0.6 6.3 %shard_map.68 = (f32[8,4,128]{2,1,0:T(4,128)}, f32[8,4,128]{2,1,0:T(4,128)}, f32[8,4,256]{2,1,0:T(4,128)}, f32[8,4,256]{2,1,0:T(4,128)}) custom-call(f32[4,8,256,128]{3,2,1,0:T(8,128)} %f_ref.5), custom_call_target="tpu_custom_call" | custom-call | tf_op jit(solution)/shard_map/pallas_call | solution.py:145
  7.0 3.5 %collective-permute-start.2 = (f32[8,4,256]{2,1,0:T(4,128)}, f32[8,4,256]{2,1,0:T(4,128)S(1)}, u32[]{:S(2)}, u32[]{:S(2)}) collective-permute-start(f32[8,4,256]{2,1,0:T(4,128)} %get-tuple-element.16), channel_id=1, source_target_pairs={{0,1},{1,2},{2,3},{3,4},{4,5},{5,6},{6,7},{7,8},{8,9},{9,10},{10,1... | collective-permute-start | bytes 98312 | tf_op jit(solution)/shard_map/ppermute | solution.py:24
  10.4 4.5 %collective-permute-start.3 = (f32[8,4,256]{2,1,0:T(4,128)}, f32[8,4,256]{2,1,0:T(4,128)S(1)}, u32[]{:S(2)}, u32[]{:S(2)}) collective-permute-start(f32[8,4,256]{2,1,0:T(4,128)} %get-tuple-element.17), channel_id=1, source_target_pairs={{1,0},{2,1},{3,2},{4,3},{5,4},{6,5},{7,6},{8,7},{9,8},{10,9},{11,1... | collective-permute-start | bytes 98312 | tf_op jit(solution)/shard_map/ppermute | solution.py:25
  16.2 1.3 %collective-permute-start.1 = (f32[8,4,128]{2,1,0:T(4,128)}, f32[8,4,128]{2,1,0:T(4,128)S(1)}, u32[]{:S(2)}, u32[]{:S(2)}) collective-permute-start(f32[8,4,128]{2,1,0:T(4,128)} %get-tuple-element.15), channel_id=1, source_target_pairs={{16,0},{32,16},{48,32},{64,48},{80,64},{96,80},{112,96},{128,112},... | collective-permute-start | bytes 49160 | tf_op jit(solution)/shard_map/ppermute | solution.py:25
  17.5 4.1 %collective-permute-done.1.he_ref = f32[8,4,128]{2,1,0:T(4,128)S(1)} collective-permute-done((f32[8,4,128]{2,1,0:T(4,128)}, f32[8,4,128]{2,1,0:T(4,128)S(1)}, u32[]{:S(2)}, u32[]{:S(2)}) %collective-permute-start.1) | collective-permute-done | bytes 16416 | tf_op jit(solution)/shard_map/ppermute | solution.py:25
  22.9 12.5 %shard_map.69 = (f32[4,8,256,128]{3,2,1,0:T(8,128)}, f32[4,8,256,128]{3,2,1,0:T(8,128)}, f32[8,4,128]{2,1,0:T(4,128)}, f32[8,4,128]{2,1,0:T(4,128)}, f32[8,4,256]{2,1,0:T(4,128)}, /*index=5*/f32[8,4,256]{2,1,0:T(4,128)}) custom-call(f32[4,8,256,128]{3,2,1,0:T(8,128)} %f_ref.5, f32[2,256,128]{2,1,0:T(8,128)} %vel_ref.3, f32[256,128]{1,0:T(8,128)} %visc_ref.3, ...), custom_call_target="tpu_custom_call" | custom-call | tf_op jit(solution)/shard_map/pallas_call | solution.py:161
  35.4 1.9 %collective-permute-start.6 = (f32[8,4,256]{2,1,0:T(4,128)}, f32[8,4,256]{2,1,0:T(4,128)S(1)}, u32[]{:S(2)}, u32[]{:S(2)}) collective-permute-start(f32[8,4,256]{2,1,0:T(4,128)} %get-tuple-element.22), channel_id=1, source_target_pairs={{0,1},{1,2},{2,3},{3,4},{4,5},{5,6},{6,7},{7,8},{8,9},{9,10},{10,1... | collective-permute-start | bytes 98312 | tf_op jit(solution)/shard_map/ppermute | solution.py:24
  37.4 6.0 %collective-permute-start.7 = (f32[8,4,256]{2,1,0:T(4,128)}, f32[8,4,256]{2,1,0:T(4,128)S(1)}, u32[]{:S(2)}, u32[]{:S(2)}) collective-permute-start(f32[8,4,256]{2,1,0:T(4,128)} %get-tuple-element.23), channel_id=1, source_target_pairs={{1,0},{2,1},{3,2},{4,3},{5,4},{6,5},{7,6},{8,7},{9,8},{10,9},{11,1... | collective-permute-start | bytes 98312 | tf_op jit(solution)/shard_map/ppermute | solution.py:25
  43.4 3.8 %collective-permute-start.4 = (f32[8,4,128]{2,1,0:T(4,128)}, f32[8,4,128]{2,1,0:T(4,128)S(1)}, u32[]{:S(2)}, u32[]{:S(2)}) collective-permute-start(f32[8,4,128]{2,1,0:T(4,128)} %get-tuple-element.20), channel_id=1, source_target_pairs={{0,16},{16,32},{32,48},{48,64},{64,80},{80,96},{96,112},{112,128},... | collective-permute-start | bytes 49160 | tf_op jit(solution)/shard_map/ppermute | solution.py:24
  47.2 1.3 %collective-permute-start.5 = (f32[8,4,128]{2,1,0:T(4,128)}, f32[8,4,128]{2,1,0:T(4,128)S(1)}, u32[]{:S(2)}, u32[]{:S(2)}) collective-permute-start(f32[8,4,128]{2,1,0:T(4,128)} %get-tuple-element.21), channel_id=1, source_target_pairs={{16,0},{32,16},{48,32},{64,48},{80,64},{96,80},{112,96},{128,112},... | collective-permute-start | bytes 49160 | tf_op jit(solution)/shard_map/ppermute | solution.py:25
  48.5 2.1 %collective-permute-done.5.he_ref = f32[8,4,128]{2,1,0:T(4,128)S(1)} collective-permute-done((f32[8,4,128]{2,1,0:T(4,128)}, f32[8,4,128]{2,1,0:T(4,128)S(1)}, u32[]{:S(2)}, u32[]{:S(2)}) %collective-permute-start.5) | collective-permute-done | bytes 16416 | tf_op jit(solution)/shard_map/ppermute | solution.py:25
  51.3 18.0 %shard_map.70 = (f32[4,8,256,128]{3,2,1,0:T(8,128)}, f32[64]{0:T(128)}) custom-call(f32[4,8,256,128]{3,2,1,0:T(8,128)} %f_ref.5, f32[4,8,256,128]{3,2,1,0:T(8,128)} %get-tuple-element.18.first_ref, f32[4,8,256,128]{3,2,1,0:T(8,128)} %get-tuple-element.19.mid_ref, f32[2,256,128]{2,1,0:T(8,128)} %vel_ref.3, f32[256,128]{1,0:T(8,128)} %visc_ref.3, ...), custom_call_target="tpu_custom_call" | custom-call | tf_op jit(solution)/shard_map/pallas_call | solution.py:180
  70.1 3.6 %collective-permute-done.8 = f32[8,8]{0,1:T(8,128)S(1)} collective-permute-done((f32[8,8]{0,1:T(8,128)S(1)}, f32[8,8]{0,1:T(8,128)S(1)}, u32[]{:S(2)}, u32[]{:S(2)}) %collective-permute-start.8) | collective-permute-done | bytes 288 | tf_op jit(solution)/shard_map/ppermute | solution.py:17
  73.7 5.1 %collective-permute-done.9 = f32[8,8]{0,1:T(8,128)S(1)} collective-permute-done((f32[8,8]{0,1:T(8,128)S(1)}, f32[8,8]{0,1:T(8,128)S(1)}, u32[]{:S(2)}, u32[]{:S(2)}) %collective-permute-start.9) | collective-permute-done | bytes 288 | tf_op jit(solution)/shard_map/ppermute | solution.py:17
  78.9 3.6 %collective-permute-done.10 = f32[8,8]{0,1:T(8,128)S(1)} collective-permute-done((f32[8,8]{0,1:T(8,128)S(1)}, f32[8,8]{0,1:T(8,128)S(1)}, u32[]{:S(2)}, u32[]{:S(2)}) %collective-permute-start.10) | collective-permute-done | bytes 288 | tf_op jit(solution)/shard_map/ppermute | solution.py:17
  82.5 2.1 %collective-permute-start.11 = (f32[8,8]{0,1:T(8,128)S(1)}, f32[8,8]{0,1:T(8,128)S(1)}, u32[]{:S(2)}, u32[]{:S(2)}) collective-permute-start(f32[8,8]{0,1:T(8,128)S(1)} %add.37), channel_id=1, source_target_pairs={{0,8},{1,9},{2,10},{3,11},{4,12},{5,13},{6,14},{7,15},{8,0},{9,1},... | collective-permute-start | bytes 776 | tf_op jit(solution)/shard_map/ppermute | solution.py:17
  84.6 3.0 %collective-permute-done.11 = f32[8,8]{0,1:T(8,128)S(1)} collective-permute-done((f32[8,8]{0,1:T(8,128)S(1)}, f32[8,8]{0,1:T(8,128)S(1)}, u32[]{:S(2)}, u32[]{:S(2)}) %collective-permute-start.11) | collective-permute-done | bytes 288 | tf_op jit(solution)/shard_map/ppermute | solution.py:17
  88.8 2.4 %collective-permute-start.13 = (f32[8,8]{0,1:T(8,128)S(1)}, f32[8,8]{0,1:T(8,128)S(1)}, u32[]{:S(2)}, u32[]{:S(2)}) collective-permute-start(f32[8,8]{0,1:T(8,128)S(1)} %add.39), channel_id=1, source_target_pairs={{0,32},{16,48},{32,0},{48,16},{64,96},{80,112},{96,64},{112,80},{1... | collective-permute-start | bytes 776 | tf_op jit(solution)/shard_map/ppermute | solution.py:17
  91.1 1.6 %collective-permute-done.13 = f32[8,8]{0,1:T(8,128)S(1)} collective-permute-done((f32[8,8]{0,1:T(8,128)S(1)}, f32[8,8]{0,1:T(8,128)S(1)}, u32[]{:S(2)}, u32[]{:S(2)}) %collective-permute-start.13) | collective-permute-done | bytes 288 | tf_op jit(solution)/shard_map/ppermute | solution.py:17
  92.7 5.4 %collective-permute-start.14 = (f32[8,8]{0,1:T(8,128)S(1)}, f32[8,8]{0,1:T(8,128)S(1)}, u32[]{:S(2)}, u32[]{:S(2)}) collective-permute-start(f32[8,8]{0,1:T(8,128)S(1)} %add.40), channel_id=1, source_target_pairs={{0,64},{16,80},{32,96},{48,112},{64,0},{80,16},{96,32},{112,48},{1... | collective-permute-start | bytes 776 | tf_op jit(solution)/shard_map/ppermute | solution.py:17
  98.1 1.6 %collective-permute-done.14 = f32[8,8]{0,1:T(8,128)S(1)} collective-permute-done((f32[8,8]{0,1:T(8,128)S(1)}, f32[8,8]{0,1:T(8,128)S(1)}, u32[]{:S(2)}, u32[]{:S(2)}) %collective-permute-start.14) | collective-permute-done | bytes 288 | tf_op jit(solution)/shard_map/ppermute | solution.py:17
  99.7 7.2 %collective-permute-start.15 = (f32[8,8]{0,1:T(8,128)S(1)}, f32[8,8]{0,1:T(8,128)S(1)}, u32[]{:S(2)}, u32[]{:S(2)}) collective-permute-start(f32[8,8]{0,1:T(8,128)S(1)} %add.41), channel_id=1, source_target_pairs={{0,128},{16,144},{32,160},{48,176},{64,192},{80,208},{96,224},{112... | collective-permute-start | bytes 776 | tf_op jit(solution)/shard_map/ppermute | solution.py:17
  107.0 1.6 %collective-permute-done.15 = f32[8,8]{0,1:T(8,128)S(1)} collective-permute-done((f32[8,8]{0,1:T(8,128)S(1)}, f32[8,8]{0,1:T(8,128)S(1)}, u32[]{:S(2)}, u32[]{:S(2)}) %collective-permute-start.15) | collective-permute-done | bytes 288 | tf_op jit(solution)/shard_map/ppermute | solution.py:17
  112.8 5.8 %shard_map.71 = f32[4,8,256,128]{3,2,1,0:T(8,128)} custom-call(f32[8,8]{1,0:T(8,128)} %fusion.inv_ref, f32[4,8,256,128]{3,2,1,0:T(8,128)} %get-tuple-element.25.r_ref), custom_call_target="tpu_custom_call" | custom-call | tf_op jit(solution)/shard_map/pallas_call | solution.py:200
  (48 shorter events, 9.4 us)
Async XLA Ops:
  7.0 14.7 %collective-permute-start.2 = (f32[8,4,256]{2,1,0:T(4,128)}, f32[8,4,256]{2,1,0:T(4,128)S(1)}, u32[]{:S(2)}, u32[]{:S(2)}) collective-permute-start(f32[8,4,256]{2,1,0:T(4,128)} %get-tuple-element.16), channel_id=1, source_target_pairs={{0,1},{1,2},{2,3},{3,4},{4,5},{5,6},{6,7},{7,8},{8,9},{9,10},{10,1... | collective-permute-start | bytes 98312 | tf_op jit(solution)/shard_map/ppermute | solution.py:24
  10.4 11.2 %collective-permute-start.3 = (f32[8,4,256]{2,1,0:T(4,128)}, f32[8,4,256]{2,1,0:T(4,128)S(1)}, u32[]{:S(2)}, u32[]{:S(2)}) collective-permute-start(f32[8,4,256]{2,1,0:T(4,128)} %get-tuple-element.17), channel_id=1, source_target_pairs={{1,0},{2,1},{3,2},{4,3},{5,4},{6,5},{7,6},{8,7},{9,8},{10,9},{11,1... | collective-permute-start | bytes 98312 | tf_op jit(solution)/shard_map/ppermute | solution.py:25
  14.9 2.6 %collective-permute-start = (f32[8,4,128]{2,1,0:T(4,128)}, f32[8,4,128]{2,1,0:T(4,128)S(1)}, u32[]{:S(2)}, u32[]{:S(2)}) collective-permute-start(f32[8,4,128]{2,1,0:T(4,128)} %get-tuple-element.14), channel_id=1, source_target_pairs={{0,16},{16,32},{32,48},{48,64},{64,80},{80,96},{96,112},{112,128},... | collective-permute-start | bytes 49160 | tf_op jit(solution)/shard_map/ppermute | solution.py:24
  16.2 5.4 %collective-permute-start.1 = (f32[8,4,128]{2,1,0:T(4,128)}, f32[8,4,128]{2,1,0:T(4,128)S(1)}, u32[]{:S(2)}, u32[]{:S(2)}) collective-permute-start(f32[8,4,128]{2,1,0:T(4,128)} %get-tuple-element.15), channel_id=1, source_target_pairs={{16,0},{32,16},{48,32},{64,48},{80,64},{96,80},{112,96},{128,112},... | collective-permute-start | bytes 49160 | tf_op jit(solution)/shard_map/ppermute | solution.py:25
  17.5 4.1 %copy-start.4 = (f32[8,4,128]{2,1,0:T(4,128)}, f32[8,4,128]{2,1,0:T(4,128)S(1)}, u32[]{:S(2)}) copy-start(f32[8,4,128]{2,1,0:T(4,128)S(1)} %collective-permute-done.hw_ref) | copy-start | bytes 49156
  21.7 0.6 copy-start.5
  21.7 0.6 copy-start
  22.3 0.6 copy-start.2
  35.4 15.2 %collective-permute-start.6 = (f32[8,4,256]{2,1,0:T(4,128)}, f32[8,4,256]{2,1,0:T(4,128)S(1)}, u32[]{:S(2)}, u32[]{:S(2)}) collective-permute-start(f32[8,4,256]{2,1,0:T(4,128)} %get-tuple-element.22), channel_id=1, source_target_pairs={{0,1},{1,2},{2,3},{3,4},{4,5},{5,6},{6,7},{7,8},{8,9},{9,10},{10,1... | collective-permute-start | bytes 98312 | tf_op jit(solution)/shard_map/ppermute | solution.py:24
  37.4 13.3 %collective-permute-start.7 = (f32[8,4,256]{2,1,0:T(4,128)}, f32[8,4,256]{2,1,0:T(4,128)S(1)}, u32[]{:S(2)}, u32[]{:S(2)}) collective-permute-start(f32[8,4,256]{2,1,0:T(4,128)} %get-tuple-element.23), channel_id=1, source_target_pairs={{1,0},{2,1},{3,2},{4,3},{5,4},{6,5},{7,6},{8,7},{9,8},{10,9},{11,1... | collective-permute-start | bytes 98312 | tf_op jit(solution)/shard_map/ppermute | solution.py:25
  43.4 5.1 %collective-permute-start.4 = (f32[8,4,128]{2,1,0:T(4,128)}, f32[8,4,128]{2,1,0:T(4,128)S(1)}, u32[]{:S(2)}, u32[]{:S(2)}) collective-permute-start(f32[8,4,128]{2,1,0:T(4,128)} %get-tuple-element.20), channel_id=1, source_target_pairs={{0,16},{16,32},{32,48},{48,64},{64,80},{80,96},{96,112},{112,128},... | collective-permute-start | bytes 49160 | tf_op jit(solution)/shard_map/ppermute | solution.py:24
  47.2 3.4 %collective-permute-start.5 = (f32[8,4,128]{2,1,0:T(4,128)}, f32[8,4,128]{2,1,0:T(4,128)S(1)}, u32[]{:S(2)}, u32[]{:S(2)}) collective-permute-start(f32[8,4,128]{2,1,0:T(4,128)} %get-tuple-element.21), channel_id=1, source_target_pairs={{16,0},{32,16},{48,32},{64,48},{80,64},{96,80},{112,96},{128,112},... | collective-permute-start | bytes 49160 | tf_op jit(solution)/shard_map/ppermute | solution.py:25
  48.5 2.1 %copy-start.6 = (f32[8,4,128]{2,1,0:T(4,128)}, f32[8,4,128]{2,1,0:T(4,128)S(1)}, u32[]{:S(2)}) copy-start(f32[8,4,128]{2,1,0:T(4,128)S(1)} %collective-permute-done.4.hw_ref) | copy-start | bytes 49156
  50.6 0.6 copy-start.7
  50.6 0.6 copy-start.1
  50.6 0.6 copy-start.3
  70.1 3.6 %collective-permute-start.8 = (f32[8,8]{0,1:T(8,128)S(1)}, f32[8,8]{0,1:T(8,128)S(1)}, u32[]{:S(2)}, u32[]{:S(2)}) collective-permute-start(f32[8,8]{0,1:T(8,128)S(1)} %copy.8), channel_id=1, source_target_pairs={{0,1},{1,0},{2,3},{3,2},{4,5},{5,4},{6,7},{7,6},{8,9},{9,8},{10,11... | collective-permute-start | bytes 776 | tf_op jit(solution)/shard_map/ppermute | solution.py:17
  73.7 5.1 %collective-permute-start.9 = (f32[8,8]{0,1:T(8,128)S(1)}, f32[8,8]{0,1:T(8,128)S(1)}, u32[]{:S(2)}, u32[]{:S(2)}) collective-permute-start(f32[8,8]{0,1:T(8,128)S(1)} %add.35), channel_id=1, source_target_pairs={{0,2},{1,3},{2,0},{3,1},{4,6},{5,7},{6,4},{7,5},{8,10},{9,11},{10,... | collective-permute-start | bytes 776 | tf_op jit(solution)/shard_map/ppermute | solution.py:17
  78.9 3.6 %collective-permute-start.10 = (f32[8,8]{0,1:T(8,128)S(1)}, f32[8,8]{0,1:T(8,128)S(1)}, u32[]{:S(2)}, u32[]{:S(2)}) collective-permute-start(f32[8,8]{0,1:T(8,128)S(1)} %add.36), channel_id=1, source_target_pairs={{0,4},{1,5},{2,6},{3,7},{4,0},{5,1},{6,2},{7,3},{8,12},{9,13},{10,... | collective-permute-start | bytes 776 | tf_op jit(solution)/shard_map/ppermute | solution.py:17
  82.5 5.1 %collective-permute-start.11 = (f32[8,8]{0,1:T(8,128)S(1)}, f32[8,8]{0,1:T(8,128)S(1)}, u32[]{:S(2)}, u32[]{:S(2)}) collective-permute-start(f32[8,8]{0,1:T(8,128)S(1)} %add.37), channel_id=1, source_target_pairs={{0,8},{1,9},{2,10},{3,11},{4,12},{5,13},{6,14},{7,15},{8,0},{9,1},... | collective-permute-start | bytes 776 | tf_op jit(solution)/shard_map/ppermute | solution.py:17
  87.6 1.2 collective-permute-start.12
  88.8 4.0 %collective-permute-start.13 = (f32[8,8]{0,1:T(8,128)S(1)}, f32[8,8]{0,1:T(8,128)S(1)}, u32[]{:S(2)}, u32[]{:S(2)}) collective-permute-start(f32[8,8]{0,1:T(8,128)S(1)} %add.39), channel_id=1, source_target_pairs={{0,32},{16,48},{32,0},{48,16},{64,96},{80,112},{96,64},{112,80},{1... | collective-permute-start | bytes 776 | tf_op jit(solution)/shard_map/ppermute | solution.py:17
  92.7 7.0 %collective-permute-start.14 = (f32[8,8]{0,1:T(8,128)S(1)}, f32[8,8]{0,1:T(8,128)S(1)}, u32[]{:S(2)}, u32[]{:S(2)}) collective-permute-start(f32[8,8]{0,1:T(8,128)S(1)} %add.40), channel_id=1, source_target_pairs={{0,64},{16,80},{32,96},{48,112},{64,0},{80,16},{96,32},{112,48},{1... | collective-permute-start | bytes 776 | tf_op jit(solution)/shard_map/ppermute | solution.py:17
  99.7 8.8 %collective-permute-start.15 = (f32[8,8]{0,1:T(8,128)S(1)}, f32[8,8]{0,1:T(8,128)S(1)}, u32[]{:S(2)}, u32[]{:S(2)}) collective-permute-start(f32[8,8]{0,1:T(8,128)S(1)} %add.41), channel_id=1, source_target_pairs={{0,128},{16,144},{32,160},{48,176},{64,192},{80,208},{96,224},{112... | collective-permute-start | bytes 776 | tf_op jit(solution)/shard_map/ppermute | solution.py:17

commit v4 on v3

--- a/solution.py
+++ b/solution.py
@@ -26,11 +26,30 @@
     return from_below, from_above
 
 
+def selector(ny):
+    r = lax.broadcasted_iota(jnp.int32, (8, ny), 0)
+    y = lax.broadcasted_iota(jnp.int32, (8, ny), 1)
+    return jnp.where(((r == 0) & (y == 0)) | ((r == 1) & (y == ny - 1)), 1.0, 0.0).astype(jnp.float32)
+
+
+def pick_columns(field, sel):
+    return lax.dot_general(sel, field, (((1,), (1,)), ((), ())), precision=lax.Precision.HIGHEST,
+                           preferred_element_type=jnp.float32)
+
+
+def place_columns(low, high, sel):
+    nx = low.shape[1]
+    r = lax.broadcasted_iota(jnp.int32, (8, nx), 0)
+    h = jnp.where(r == 0, low, jnp.where(r == 1, high, 0.0))
+    return lax.dot_general(h, sel, (((0,), (0,)), ((), ())), precision=lax.Precision.HIGHEST,
+                           preferred_element_type=jnp.float32)
+
+
 def operator(q, west, east, south, north, vel_ref, visc_ref, snd_ref, coup_ref):
     nx, ny = q[0].shape
     rows = lax.broadcasted_iota(jnp.int32, (nx, ny), 0)
     lanes = lax.broadcasted_iota(jnp.int32, (nx, ny), 1)
-    half = lax.broadcasted_iota(jnp.int32, (ny, nx), 0) < ny // 2
+    sel = selector(ny)
     vel0 = vel_ref[0]
     vel1 = vel_ref[1]
     visc = visc_ref[...]
@@ -38,7 +57,7 @@
     grad_x, grad_y, transport = [], [], []
     for v in range(NV):
         field = q[v]
-        columns = jnp.where(half, south[v], north[v]).T
+        columns = place_columns(south[v], north[v], sel)
         e = jnp.where(rows == nx - 1, east[v], pltpu.roll(field, nx - 1, 0))
         w = jnp.where(rows == 0, west[v], pltpu.roll(field, 1, 0))
         n = jnp.where(lanes == ny - 1, columns, pltpu.roll(field, ny - 1, 1))
@@ -76,9 +95,9 @@
         mid_ref[v, 0] = middle
         mw_ref[0, v:v + 1, :] = middle[0:1, :]
         me_ref[0, v:v + 1, :] = middle[nx - 1:nx, :]
-        flipped = middle.T
-        ms_ref[0, v:v + 1, :] = flipped[0:1, :]
-        mn_ref[0, v:v + 1, :] = flipped[ny - 1:ny, :]
+        picked = pick_columns(middle, selector(ny))
+        ms_ref[0, v:v + 1, :] = picked[0:1, :]
+        mn_ref[0, v:v + 1, :] = picked[1:2, :]
 
 
 def stage_two(f_ref, first_ref, mid_ref, vel_ref, visc_ref, snd_ref, coup_ref, hw_ref, he_ref, hs_ref, hn_ref,
@@ -106,9 +125,9 @@
             for v in range(NV):
                 prod = (resp_ref[v, d] * resp[v]).reshape(nx // 8, 8, ny).sum(axis=0)
                 acc = prod if acc is None else acc + prod
-            total = jnp.sum(acc)
-            gram_ref[c * ncol + d] = total
-            gram_ref[d * ncol + c] = total
+            row = jnp.sum(acc, axis=0, keepdims=True)
+            gram_ref[pl.ds(c * ncol + d, 1), :] = row
+            gram_ref[pl.ds(d * ncol + c, 1), :] = row
 
 
 def edges(f_ref, w_ref, e_ref, s_ref, n_ref):
@@ -117,9 +136,9 @@
         field = f_ref[v, 0]
         w_ref[0, v:v + 1, :] = field[0:1, :]
         e_ref[0, v:v + 1, :] = field[nx - 1:nx, :]
-        flipped = field.T
-        s_ref[0, v:v + 1, :] = flipped[0:1, :]
-        n_ref[0, v:v + 1, :] = flipped[ny - 1:ny, :]
+        picked = pick_columns(field, selector(ny))
+        s_ref[0, v:v + 1, :] = picked[0:1, :]
+        n_ref[0, v:v + 1, :] = picked[1:2, :]
 
 
 def combine(inv_ref, r_ref, out_ref):
@@ -181,10 +200,10 @@
         stage_two,
         grid=(ncol,),
         in_specs=[column, column, column] + coef_specs + [edge_x, edge_x, edge_y, edge_y],
-        out_specs=[whole(forcing.shape), pl.BlockSpec(memory_space=pltpu.SMEM)],
+        out_specs=[whole(forcing.shape), whole((ncol * ncol, ny))],
         out_shape=[
             jax.ShapeDtypeStruct(forcing.shape, f32),
-            jax.ShapeDtypeStruct((ncol * ncol,), f32),
+            jax.ShapeDtypeStruct((ncol * ncol, ny), f32),
         ],
         compiler_params=pltpu.CompilerParams(
             vmem_limit_bytes=60 * 1024 * 1024, dimension_semantics=("arbitrary",)
@@ -192,7 +211,7 @@
     )(forcing, first, middle, velocity, viscosity, sound, coupling, hw2, he2, hs2, hn2)
 
     rows_total = float(nv * nx * ny * lax.axis_size("gx") * lax.axis_size("gy"))
-    local_gram = partial.reshape(ncol, ncol) / rows_total
+    local_gram = jnp.sum(partial, axis=1).reshape(ncol, ncol) / rows_total
     lower = jnp.linalg.cholesky(all_sum(local_gram))
     identity = jnp.eye(lower.shape[0], dtype=lower.dtype)
     inverse = lax.linalg.triangular_solve(lower, identity, left_side=True, lower=True)

time: 119 us -> 121 us (1.017)
  Pallas kernels: 42.7 us -> 44.3 us
    pallas_call x1, Pallas kernels: 12.5 us -> 15.6 us  [local(): pl.pallas_call(stage_one, grid=(ncol,), in_specs=[column] + coef_specs +...]
    pallas_call x1, Pallas kernels: 18 us -> 15.3 us  [local(): pl.pallas_call(stage_two, grid=(ncol,), in_specs=[column, column, column]...]
    pallas_call x1, Pallas kernels: 6.34 us -> 7.65 us  [local(): pl.pallas_call(edges, grid=(ncol,), in_specs=[column], out_specs=[edge_x,...]
where the time goes in v4:
time: 121 us; the launch traced here: 120 us
  Pallas kernels  44.3 us (37%)
  starting transfers between devices  40.7 us (34%)
  waiting for transfers between devices  27.4 us (23%)
  other arithmetic  3.56 us (3%)
  local copies, waits for them, and re-layouts  2.68 us (2%)
    ppermute x8, waiting for transfers between devices, all_sum(): lax.ppermute(value, axis, [(i, i ^ bit) for i in range(count)])  21.2 us
    ppermute x8, starting transfers between devices, all_sum(): lax.ppermute(value, axis, [(i, i ^ bit) for i in range(count)])  17.2 us
    pallas_call x1, Pallas kernels, local(): pl.pallas_call(stage_one, grid=(ncol,), in_specs=[column] + coef_specs +...  15.6 us
    pallas_call x1, Pallas kernels, local(): pl.pallas_call(stage_two, grid=(ncol,), in_specs=[column, column, column]...  15.3 us
    ppermute x4, starting transfers between devices, exchange(): from_above = lax.ppermute(low, axis, [(i + 1, i) for i in range(count - 1)])  13.1 us
    ppermute x4, starting transfers between devices, exchange(): lax.ppermute(high, axis, [(i, i + 1) for i in range(count - 1)])  10.5 us
    pallas_call x1, Pallas kernels, local(): pl.pallas_call(edges, grid=(ncol,), in_specs=[column], out_specs=[edge_x,...  7.65 us
    ppermute x4, waiting for transfers between devices, exchange(): from_above = lax.ppermute(low, axis, [(i + 1, i) for i in range(count - 1)])  6.18 us
  transfers between devices with their start and end apart: 16, of which 10 were waited for; matrix products, arithmetic and copies ran while one was open for 0% of the time, Pallas kernels for 0%

profile of v4, /device:TPU:2, one launch (start us, length us, event | category | flops | bytes accessed | tf_op | source)
XLA Modules:
  0.0 120.3 jit_solution(13531345129531266443)
XLA Ops:
  0.6 7.6 %shard_map.68 = (f32[8,4,128]{2,1,0:T(4,128)}, f32[8,4,128]{2,1,0:T(4,128)}, f32[8,4,256]{2,1,0:T(4,128)}, f32[8,4,256]{2,1,0:T(4,128)}) custom-call(f32[4,8,256,128]{3,2,1,0:T(8,128)} %f_ref.5), custom_call_target="tpu_custom_call" | custom-call | tf_op jit(solution)/shard_map/pallas_call | solution.py:164
  8.3 3.5 %collective-permute-start.2 = (f32[8,4,256]{2,1,0:T(4,128)}, f32[8,4,256]{2,1,0:T(4,128)S(1)}, u32[]{:S(2)}, u32[]{:S(2)}) collective-permute-start(f32[8,4,256]{2,1,0:T(4,128)} %get-tuple-element.16), channel_id=1, source_target_pairs={{0,1},{1,2},{2,3},{3,4},{4,5},{5,6},{6,7},{7,8},{8,9},{9,10},{10,1... | collective-permute-start | bytes 98312 | tf_op jit(solution)/shard_map/ppermute | solution.py:24
  11.8 4.5 %collective-permute-start.3 = (f32[8,4,256]{2,1,0:T(4,128)}, f32[8,4,256]{2,1,0:T(4,128)S(1)}, u32[]{:S(2)}, u32[]{:S(2)}) collective-permute-start(f32[8,4,256]{2,1,0:T(4,128)} %get-tuple-element.17), channel_id=1, source_target_pairs={{1,0},{2,1},{3,2},{4,3},{5,4},{6,5},{7,6},{8,7},{9,8},{10,9},{11,1... | collective-permute-start | bytes 98312 | tf_op jit(solution)/shard_map/ppermute | solution.py:25
  17.5 1.3 %collective-permute-start.1 = (f32[8,4,128]{2,1,0:T(4,128)}, f32[8,4,128]{2,1,0:T(4,128)S(1)}, u32[]{:S(2)}, u32[]{:S(2)}) collective-permute-start(f32[8,4,128]{2,1,0:T(4,128)} %get-tuple-element.15), channel_id=1, source_target_pairs={{16,0},{32,16},{48,32},{64,48},{80,64},{96,80},{112,96},{128,112},... | collective-permute-start | bytes 49160 | tf_op jit(solution)/shard_map/ppermute | solution.py:25
  18.9 4.1 %collective-permute-done.1.he_ref = f32[8,4,128]{2,1,0:T(4,128)S(1)} collective-permute-done((f32[8,4,128]{2,1,0:T(4,128)}, f32[8,4,128]{2,1,0:T(4,128)S(1)}, u32[]{:S(2)}, u32[]{:S(2)}) %collective-permute-start.1) | collective-permute-done | bytes 16416 | tf_op jit(solution)/shard_map/ppermute | solution.py:25
  24.2 15.6 %shard_map.69 = (f32[4,8,256,128]{3,2,1,0:T(8,128)}, f32[4,8,256,128]{3,2,1,0:T(8,128)}, f32[8,4,128]{2,1,0:T(4,128)}, f32[8,4,128]{2,1,0:T(4,128)}, f32[8,4,256]{2,1,0:T(4,128)}, /*index=5*/f32[8,4,256]{2,1,0:T(4,128)}) custom-call(f32[4,8,256,128]{3,2,1,0:T(8,128)} %f_ref.5, f32[2,256,128]{2,1,0:T(8,128)} %vel_ref.3, f32[256,128]{1,0:T(8,128)} %visc_ref.3, ...), custom_call_target="tpu_custom_call" | custom-call | tf_op jit(solution)/shard_map/pallas_call | solution.py:180
  39.8 1.9 %collective-permute-start.6 = (f32[8,4,256]{2,1,0:T(4,128)}, f32[8,4,256]{2,1,0:T(4,128)S(1)}, u32[]{:S(2)}, u32[]{:S(2)}) collective-permute-start(f32[8,4,256]{2,1,0:T(4,128)} %get-tuple-element.22), channel_id=1, source_target_pairs={{0,1},{1,2},{2,3},{3,4},{4,5},{5,6},{6,7},{7,8},{8,9},{9,10},{10,1... | collective-permute-start | bytes 98312 | tf_op jit(solution)/shard_map/ppermute | solution.py:24
  41.7 6.0 %collective-permute-start.7 = (f32[8,4,256]{2,1,0:T(4,128)}, f32[8,4,256]{2,1,0:T(4,128)S(1)}, u32[]{:S(2)}, u32[]{:S(2)}) collective-permute-start(f32[8,4,256]{2,1,0:T(4,128)} %get-tuple-element.23), channel_id=1, source_target_pairs={{1,0},{2,1},{3,2},{4,3},{5,4},{6,5},{7,6},{8,7},{9,8},{10,9},{11,1... | collective-permute-start | bytes 98312 | tf_op jit(solution)/shard_map/ppermute | solution.py:25
  47.8 3.8 %collective-permute-start.4 = (f32[8,4,128]{2,1,0:T(4,128)}, f32[8,4,128]{2,1,0:T(4,128)S(1)}, u32[]{:S(2)}, u32[]{:S(2)}) collective-permute-start(f32[8,4,128]{2,1,0:T(4,128)} %get-tuple-element.20), channel_id=1, source_target_pairs={{0,16},{16,32},{32,48},{48,64},{64,80},{80,96},{96,112},{112,128},... | collective-permute-start | bytes 49160 | tf_op jit(solution)/shard_map/ppermute | solution.py:24
  51.6 1.3 %collective-permute-start.5 = (f32[8,4,128]{2,1,0:T(4,128)}, f32[8,4,128]{2,1,0:T(4,128)S(1)}, u32[]{:S(2)}, u32[]{:S(2)}) collective-permute-start(f32[8,4,128]{2,1,0:T(4,128)} %get-tuple-element.21), channel_id=1, source_target_pairs={{16,0},{32,16},{48,32},{64,48},{80,64},{96,80},{112,96},{128,112},... | collective-permute-start | bytes 49160 | tf_op jit(solution)/shard_map/ppermute | solution.py:25
  52.9 2.1 %collective-permute-done.5.he_ref = f32[8,4,128]{2,1,0:T(4,128)S(1)} collective-permute-done((f32[8,4,128]{2,1,0:T(4,128)}, f32[8,4,128]{2,1,0:T(4,128)S(1)}, u32[]{:S(2)}, u32[]{:S(2)}) %collective-permute-start.5) | collective-permute-done | bytes 16416 | tf_op jit(solution)/shard_map/ppermute | solution.py:25
  55.6 15.3 %shard_map.70 = (f32[4,8,256,128]{3,2,1,0:T(8,128)}, f32[64,128]{1,0:T(8,128)}) custom-call(f32[4,8,256,128]{3,2,1,0:T(8,128)} %f_ref.5, f32[4,8,256,128]{3,2,1,0:T(8,128)} %get-tuple-element.18.first_ref, f32[4,8,256,128]{3,2,1,0:T(8,128)} %get-tuple-element.19.mid_ref, f32[2,256,128]{2,1,0:T(8,128)} %vel_ref.3, f32[256,128]{1,0:T(8,128)} %visc_ref.3, ...), custom_call_target="tpu_custom_call" | custom-call | tf_op jit(solution)/shard_map/pallas_call | solution.py:199
  71.9 3.6 %collective-permute-done.8 = f32[8,8]{0,1:T(8,128)S(1)} collective-permute-done((f32[8,8]{0,1:T(8,128)S(1)}, f32[8,8]{0,1:T(8,128)S(1)}, u32[]{:S(2)}, u32[]{:S(2)}) %collective-permute-start.8) | collective-permute-done | bytes 288 | tf_op jit(solution)/shard_map/ppermute | solution.py:17
  75.6 5.1 %collective-permute-done.9 = f32[8,8]{0,1:T(8,128)S(1)} collective-permute-done((f32[8,8]{0,1:T(8,128)S(1)}, f32[8,8]{0,1:T(8,128)S(1)}, u32[]{:S(2)}, u32[]{:S(2)}) %collective-permute-start.9) | collective-permute-done | bytes 288 | tf_op jit(solution)/shard_map/ppermute | solution.py:17
  80.7 3.6 %collective-permute-done.10 = f32[8,8]{0,1:T(8,128)S(1)} collective-permute-done((f32[8,8]{0,1:T(8,128)S(1)}, f32[8,8]{0,1:T(8,128)S(1)}, u32[]{:S(2)}, u32[]{:S(2)}) %collective-permute-start.10) | collective-permute-done | bytes 288 | tf_op jit(solution)/shard_map/ppermute | solution.py:17
  84.3 2.1 %collective-permute-start.11 = (f32[8,8]{0,1:T(8,128)S(1)}, f32[8,8]{0,1:T(8,128)S(1)}, u32[]{:S(2)}, u32[]{:S(2)}) collective-permute-start(f32[8,8]{0,1:T(8,128)S(1)} %add.37), channel_id=1, source_target_pairs={{0,8},{1,9},{2,10},{3,11},{4,12},{5,13},{6,14},{7,15},{8,0},{9,1},... | collective-permute-start | bytes 776 | tf_op jit(solution)/shard_map/ppermute | solution.py:17
  86.4 3.0 %collective-permute-done.11 = f32[8,8]{0,1:T(8,128)S(1)} collective-permute-done((f32[8,8]{0,1:T(8,128)S(1)}, f32[8,8]{0,1:T(8,128)S(1)}, u32[]{:S(2)}, u32[]{:S(2)}) %collective-permute-start.11) | collective-permute-done | bytes 288 | tf_op jit(solution)/shard_map/ppermute | solution.py:17
  90.6 2.4 %collective-permute-start.13 = (f32[8,8]{0,1:T(8,128)S(1)}, f32[8,8]{0,1:T(8,128)S(1)}, u32[]{:S(2)}, u32[]{:S(2)}) collective-permute-start(f32[8,8]{0,1:T(8,128)S(1)} %add.39), channel_id=1, source_target_pairs={{0,32},{16,48},{32,0},{48,16},{64,96},{80,112},{96,64},{112,80},{1... | collective-permute-start | bytes 776 | tf_op jit(solution)/shard_map/ppermute | solution.py:17
  93.0 1.6 %collective-permute-done.13 = f32[8,8]{0,1:T(8,128)S(1)} collective-permute-done((f32[8,8]{0,1:T(8,128)S(1)}, f32[8,8]{0,1:T(8,128)S(1)}, u32[]{:S(2)}, u32[]{:S(2)}) %collective-permute-start.13) | collective-permute-done | bytes 288 | tf_op jit(solution)/shard_map/ppermute | solution.py:17
  94.5 5.4 %collective-permute-start.14 = (f32[8,8]{0,1:T(8,128)S(1)}, f32[8,8]{0,1:T(8,128)S(1)}, u32[]{:S(2)}, u32[]{:S(2)}) collective-permute-start(f32[8,8]{0,1:T(8,128)S(1)} %add.40), channel_id=1, source_target_pairs={{0,64},{16,80},{32,96},{48,112},{64,0},{80,16},{96,32},{112,48},{1... | collective-permute-start | bytes 776 | tf_op jit(solution)/shard_map/ppermute | solution.py:17
  99.9 1.6 %collective-permute-done.14 = f32[8,8]{0,1:T(8,128)S(1)} collective-permute-done((f32[8,8]{0,1:T(8,128)S(1)}, f32[8,8]{0,1:T(8,128)S(1)}, u32[]{:S(2)}, u32[]{:S(2)}) %collective-permute-start.14) | collective-permute-done | bytes 288 | tf_op jit(solution)/shard_map/ppermute | solution.py:17
  101.5 7.2 %collective-permute-start.15 = (f32[8,8]{0,1:T(8,128)S(1)}, f32[8,8]{0,1:T(8,128)S(1)}, u32[]{:S(2)}, u32[]{:S(2)}) collective-permute-start(f32[8,8]{0,1:T(8,128)S(1)} %add.41), channel_id=1, source_target_pairs={{0,128},{16,144},{32,160},{48,176},{64,192},{80,208},{96,224},{112... | collective-permute-start | bytes 776 | tf_op jit(solution)/shard_map/ppermute | solution.py:17
  108.8 1.6 %collective-permute-done.15 = f32[8,8]{0,1:T(8,128)S(1)} collective-permute-done((f32[8,8]{0,1:T(8,128)S(1)}, f32[8,8]{0,1:T(8,128)S(1)}, u32[]{:S(2)}, u32[]{:S(2)}) %collective-permute-start.15) | collective-permute-done | bytes 288 | tf_op jit(solution)/shard_map/ppermute | solution.py:17
  114.6 5.8 %shard_map.71 = f32[4,8,256,128]{3,2,1,0:T(8,128)} custom-call(f32[8,8]{1,0:T(8,128)} %fusion.inv_ref, f32[4,8,256,128]{3,2,1,0:T(8,128)} %get-tuple-element.25.r_ref), custom_call_target="tpu_custom_call" | custom-call | tf_op jit(solution)/shard_map/pallas_call | solution.py:219
  (49 shorter events, 9.5 us)
Async XLA Ops:
  8.3 14.7 %collective-permute-start.2 = (f32[8,4,256]{2,1,0:T(4,128)}, f32[8,4,256]{2,1,0:T(4,128)S(1)}, u32[]{:S(2)}, u32[]{:S(2)}) collective-permute-start(f32[8,4,256]{2,1,0:T(4,128)} %get-tuple-element.16), channel_id=1, source_target_pairs={{0,1},{1,2},{2,3},{3,4},{4,5},{5,6},{6,7},{7,8},{8,9},{9,10},{10,1... | collective-permute-start | bytes 98312 | tf_op jit(solution)/shard_map/ppermute | solution.py:24
  11.8 11.2 %collective-permute-start.3 = (f32[8,4,256]{2,1,0:T(4,128)}, f32[8,4,256]{2,1,0:T(4,128)S(1)}, u32[]{:S(2)}, u32[]{:S(2)}) collective-permute-start(f32[8,4,256]{2,1,0:T(4,128)} %get-tuple-element.17), channel_id=1, source_target_pairs={{1,0},{2,1},{3,2},{4,3},{5,4},{6,5},{7,6},{8,7},{9,8},{10,9},{11,1... | collective-permute-start | bytes 98312 | tf_op jit(solution)/shard_map/ppermute | solution.py:25
  16.2 2.6 %collective-permute-start = (f32[8,4,128]{2,1,0:T(4,128)}, f32[8,4,128]{2,1,0:T(4,128)S(1)}, u32[]{:S(2)}, u32[]{:S(2)}) collective-permute-start(f32[8,4,128]{2,1,0:T(4,128)} %get-tuple-element.14), channel_id=1, source_target_pairs={{0,16},{16,32},{32,48},{48,64},{64,80},{80,96},{96,112},{112,128},... | collective-permute-start | bytes 49160 | tf_op jit(solution)/shard_map/ppermute | solution.py:24
  17.5 5.4 %collective-permute-start.1 = (f32[8,4,128]{2,1,0:T(4,128)}, f32[8,4,128]{2,1,0:T(4,128)S(1)}, u32[]{:S(2)}, u32[]{:S(2)}) collective-permute-start(f32[8,4,128]{2,1,0:T(4,128)} %get-tuple-element.15), channel_id=1, source_target_pairs={{16,0},{32,16},{48,32},{64,48},{80,64},{96,80},{112,96},{128,112},... | collective-permute-start | bytes 49160 | tf_op jit(solution)/shard_map/ppermute | solution.py:25
  18.8 4.1 %copy-start.4 = (f32[8,4,128]{2,1,0:T(4,128)}, f32[8,4,128]{2,1,0:T(4,128)S(1)}, u32[]{:S(2)}) copy-start(f32[8,4,128]{2,1,0:T(4,128)S(1)} %collective-permute-done.hw_ref) | copy-start | bytes 49156
  23.0 0.6 copy-start.5
  23.0 0.6 copy-start
  23.6 0.6 copy-start.2
  39.8 15.2 %collective-permute-start.6 = (f32[8,4,256]{2,1,0:T(4,128)}, f32[8,4,256]{2,1,0:T(4,128)S(1)}, u32[]{:S(2)}, u32[]{:S(2)}) collective-permute-start(f32[8,4,256]{2,1,0:T(4,128)} %get-tuple-element.22), channel_id=1, source_target_pairs={{0,1},{1,2},{2,3},{3,4},{4,5},{5,6},{6,7},{7,8},{8,9},{9,10},{10,1... | collective-permute-start | bytes 98312 | tf_op jit(solution)/shard_map/ppermute | solution.py:24
  41.7 13.3 %collective-permute-start.7 = (f32[8,4,256]{2,1,0:T(4,128)}, f32[8,4,256]{2,1,0:T(4,128)S(1)}, u32[]{:S(2)}, u32[]{:S(2)}) collective-permute-start(f32[8,4,256]{2,1,0:T(4,128)} %get-tuple-element.23), channel_id=1, source_target_pairs={{1,0},{2,1},{3,2},{4,3},{5,4},{6,5},{7,6},{8,7},{9,8},{10,9},{11,1... | collective-permute-start | bytes 98312 | tf_op jit(solution)/shard_map/ppermute | solution.py:25
  47.8 5.1 %collective-permute-start.4 = (f32[8,4,128]{2,1,0:T(4,128)}, f32[8,4,128]{2,1,0:T(4,128)S(1)}, u32[]{:S(2)}, u32[]{:S(2)}) collective-permute-start(f32[8,4,128]{2,1,0:T(4,128)} %get-tuple-element.20), channel_id=1, source_target_pairs={{0,16},{16,32},{32,48},{48,64},{64,80},{80,96},{96,112},{112,128},... | collective-permute-start | bytes 49160 | tf_op jit(solution)/shard_map/ppermute | solution.py:24
  51.6 3.4 %collective-permute-start.5 = (f32[8,4,128]{2,1,0:T(4,128)}, f32[8,4,128]{2,1,0:T(4,128)S(1)}, u32[]{:S(2)}, u32[]{:S(2)}) collective-permute-start(f32[8,4,128]{2,1,0:T(4,128)} %get-tuple-element.21), channel_id=1, source_target_pairs={{16,0},{32,16},{48,32},{64,48},{80,64},{96,80},{112,96},{128,112},... | collective-permute-start | bytes 49160 | tf_op jit(solution)/shard_map/ppermute | solution.py:25
  52.9 2.1 %copy-start.6 = (f32[8,4,128]{2,1,0:T(4,128)}, f32[8,4,128]{2,1,0:T(4,128)S(1)}, u32[]{:S(2)}) copy-start(f32[8,4,128]{2,1,0:T(4,128)S(1)} %collective-permute-done.4.hw_ref) | copy-start | bytes 49156
  55.0 0.6 copy-start.7
  55.0 0.6 copy-start.1
  55.0 0.6 copy-start.3
  71.9 3.6 %collective-permute-start.8 = (f32[8,8]{0,1:T(8,128)S(1)}, f32[8,8]{0,1:T(8,128)S(1)}, u32[]{:S(2)}, u32[]{:S(2)}) collective-permute-start(f32[8,8]{0,1:T(8,128)S(1)} %copy.8), channel_id=1, source_target_pairs={{0,1},{1,0},{2,3},{3,2},{4,5},{5,4},{6,7},{7,6},{8,9},{9,8},{10,11... | collective-permute-start | bytes 776 | tf_op jit(solution)/shard_map/ppermute | solution.py:17
  75.5 5.1 %collective-permute-start.9 = (f32[8,8]{0,1:T(8,128)S(1)}, f32[8,8]{0,1:T(8,128)S(1)}, u32[]{:S(2)}, u32[]{:S(2)}) collective-permute-start(f32[8,8]{0,1:T(8,128)S(1)} %add.35), channel_id=1, source_target_pairs={{0,2},{1,3},{2,0},{3,1},{4,6},{5,7},{6,4},{7,5},{8,10},{9,11},{10,... | collective-permute-start | bytes 776 | tf_op jit(solution)/shard_map/ppermute | solution.py:17
  80.7 3.6 %collective-permute-start.10 = (f32[8,8]{0,1:T(8,128)S(1)}, f32[8,8]{0,1:T(8,128)S(1)}, u32[]{:S(2)}, u32[]{:S(2)}) collective-permute-start(f32[8,8]{0,1:T(8,128)S(1)} %add.36), channel_id=1, source_target_pairs={{0,4},{1,5},{2,6},{3,7},{4,0},{5,1},{6,2},{7,3},{8,12},{9,13},{10,... | collective-permute-start | bytes 776 | tf_op jit(solution)/shard_map/ppermute | solution.py:17
  84.3 5.1 %collective-permute-start.11 = (f32[8,8]{0,1:T(8,128)S(1)}, f32[8,8]{0,1:T(8,128)S(1)}, u32[]{:S(2)}, u32[]{:S(2)}) collective-permute-start(f32[8,8]{0,1:T(8,128)S(1)} %add.37), channel_id=1, source_target_pairs={{0,8},{1,9},{2,10},{3,11},{4,12},{5,13},{6,14},{7,15},{8,0},{9,1},... | collective-permute-start | bytes 776 | tf_op jit(solution)/shard_map/ppermute | solution.py:17
  89.4 1.2 collective-permute-start.12
  90.6 4.0 %collective-permute-start.13 = (f32[8,8]{0,1:T(8,128)S(1)}, f32[8,8]{0,1:T(8,128)S(1)}, u32[]{:S(2)}, u32[]{:S(2)}) collective-permute-start(f32[8,8]{0,1:T(8,128)S(1)} %add.39), channel_id=1, source_target_pairs={{0,32},{16,48},{32,0},{48,16},{64,96},{80,112},{96,64},{112,80},{1... | collective-permute-start | bytes 776 | tf_op jit(solution)/shard_map/ppermute | solution.py:17
  94.5 7.0 %collective-permute-start.14 = (f32[8,8]{0,1:T(8,128)S(1)}, f32[8,8]{0,1:T(8,128)S(1)}, u32[]{:S(2)}, u32[]{:S(2)}) collective-permute-start(f32[8,8]{0,1:T(8,128)S(1)} %add.40), channel_id=1, source_target_pairs={{0,64},{16,80},{32,96},{48,112},{64,0},{80,16},{96,32},{112,48},{1... | collective-permute-start | bytes 776 | tf_op jit(solution)/shard_map/ppermute | solution.py:17
  101.5 8.8 %collective-permute-start.15 = (f32[8,8]{0,1:T(8,128)S(1)}, f32[8,8]{0,1:T(8,128)S(1)}, u32[]{:S(2)}, u32[]{:S(2)}) collective-permute-start(f32[8,8]{0,1:T(8,128)S(1)} %add.41), channel_id=1, source_target_pairs={{0,128},{16,144},{32,160},{48,176},{64,192},{80,208},{96,224},{112... | collective-permute-start | bytes 776 | tf_op jit(solution)/shard_map/ppermute | solution.py:17

commit v5 on v3

v5 whole, which is shorter than its diff:
```python
import jax
import jax.numpy as jnp
from jax import lax
from jax.experimental import pallas as pl
from jax.experimental.pallas import tpu as pltpu
from jax.sharding import PartitionSpec as P

STEP = 0.5
NV = 4


def all_sum(value):
    for axis in ("gy", "gx"):
        count = lax.axis_size(axis)
        bit = 1
        while bit < count:
            value = value + lax.ppermute(value, axis, [(i, i ^ bit) for i in range(count)])
            bit *= 2
    return value


def exchange(low, high, axis):
    count = lax.axis_size(axis)
    from_below = lax.ppermute(high, axis, [(i, i + 1) for i in range(count - 1)])
    from_above = lax.ppermute(low, axis, [(i + 1, i) for i in range(count - 1)])
    return from_below, from_above


def pack(pack_ref, fields, c):
    nx, ny = fields[0].shape
    lanes = lax.broadcasted_iota(jnp.int32, (nx, ny), 1)
    cur = pack_ref[...]
    for v, field in enumerate(fields):
        lo = 2 * NV * c + 2 * v
        cur = jnp.where(lanes == lo, pltpu.roll(field, lo, 1), cur)
        cur = jnp.where(lanes == lo + 1, pltpu.roll(field, lo + 2, 1), cur)
    pack_ref[...] = cur


def send_packed(pack_ref, g_ref):
    g_ref[...] = pack_ref[...].T[0:g_ref.shape[0], :]


def unpack(g_ref, ny):
    width, nx = g_ref.shape
    return jnp.concatenate([g_ref[...], jnp.zeros((ny - width, nx), jnp.float32)], axis=0).T


def operator(q, west, east, below_ref, above_ref, c, vel_ref, visc_ref, snd_ref, coup_ref):
    nx, ny = q[0].shape
    rows = lax.broadcasted_iota(jnp.int32, (nx, ny), 0)
    lanes = lax.broadcasted_iota(jnp.int32, (nx, ny), 1)
    vel0 = vel_ref[0]
    vel1 = vel_ref[1]
    visc = visc_ref[...]
    snd = snd_ref[...]
    grad_x, grad_y, transport = [], [], []
    for v in range(NV):
        field = q[v]
        lo = 2 * NV * c + 2 * v
        north = pltpu.roll(above_ref[...], ny - 1 - lo, 1)
        south = pltpu.roll(below_ref[...], ny - 1 - lo, 1)
        e = jnp.where(rows == nx - 1, east[v], pltpu.roll(field, nx - 1, 0))
        w = jnp.where(rows == 0, west[v], pltpu.roll(field, 1, 0))
        n = jnp.where(lanes == ny - 1, north, pltpu.roll(field, ny - 1, 1))
        s = jnp.where(lanes == 0, south, pltpu.roll(field, 1, 1))
        gx = 0.5 * (e - w)
        gy = 0.5 * (n - s)
        laplace = e + w + n + s - 4.0 * field
        grad_x.append(gx)
        grad_y.append(gy)
        transport.append(visc * laplace - vel0 * gx - vel1 * gy)
    divergence = grad_x[1] + grad_y[2]
    acoustic = [-snd * divergence, -snd * grad_x[3], -snd * grad_y[3], -snd * divergence]
    out = []
    for w_ in range(NV):
        mixing = coup_ref[w_, 0] * q[0]
        for inner in range(1, NV):
            mixing = mixing + coup_ref[w_, inner] * q[inner]
        out.append(transport[w_] + acoustic[w_] - mixing)
    return out


def receive(c, gb_ref, ga_ref, below_ref, above_ref, ny):
    @pl.when(c == 0)
    def _():
        below_ref[...] = unpack(gb_ref, ny)
        above_ref[...] = unpack(ga_ref, ny)


def stage_one(f_ref, vel_ref, visc_ref, snd_ref, coup_ref, hw_ref, he_ref, gb_ref, ga_ref,
              first_ref, mid_ref, mw_ref, me_ref, g_ref, below_ref, above_ref, pack_ref):
    c = pl.program_id(0)
    nx, ny = f_ref.shape[2], f_ref.shape[3]
    receive(c, gb_ref, ga_ref, below_ref, above_ref, ny)
    q = [f_ref[v, 0] for v in range(NV)]
    west = [hw_ref[0, v:v + 1, :] for v in range(NV)]
    east = [he_ref[0, v:v + 1, :] for v in range(NV)]
    lq = operator(q, west, east, below_ref, above_ref, c, vel_ref, visc_ref, snd_ref, coup_ref)
    mids = []
    for v in range(NV):
        first = lq[v] + q[v]
        middle = q[v] + STEP * first
        first_ref[v, 0] = first
        mid_ref[v, 0] = middle
        mw_ref[0, v:v + 1, :] = middle[0:1, :]
        me_ref[0, v:v + 1, :] = middle[nx - 1:nx, :]
        mids.append(middle)
    pack(pack_ref, mids, c)

    @pl.when(c == pl.num_programs(0) - 1)
    def _():
        send_packed(pack_ref, g_ref)


def stage_two(f_ref, first_ref, mid_ref, vel_ref, visc_ref, snd_ref, coup_ref, hw_ref, he_ref, gb_ref, ga_ref,
              resp_ref, gram_ref, below_ref, above_ref):
    c = pl.program_id(0)
    ncol = resp_ref.shape[1]
    nx, ny = f_ref.shape[2], f_ref.shape[3]
    receive(c, gb_ref, ga_ref, below_ref, above_ref, ny)
    q = [mid_ref[v, 0] for v in range(NV)]
    west = [hw_ref[0, v:v + 1, :] for v in range(NV)]
    east = [he_ref[0, v:v + 1, :] for v in range(NV)]
    lq = operator(q, west, east, below_ref, above_ref, c, vel_ref, visc_ref, snd_ref, coup_ref)
    resp = []
    for v in range(NV):
        forcing = f_ref[v, 0]
        second = lq[v] + forcing
        r = forcing + 0.5 * STEP * (first_ref[v, 0] + second)
        resp_ref[v, pl.ds(c, 1)] = r[None]
        resp.append(r)
    for d in range(ncol):
        @pl.when(d <= c)
        def _():
            acc = None
            for v in range(NV):
                prod = (resp_ref[v, d] * resp[v]).reshape(nx // 8, 8, ny).sum(axis=0)
                acc = prod if acc is None else acc + prod
            row = jnp.sum(acc, axis=0, keepdims=True)
            gram_ref[pl.ds(c * ncol + d, 1), :] = row
            gram_ref[pl.ds(d * ncol + c, 1), :] = row


def edges(f_ref, w_ref, e_ref, g_ref, pack_ref):
    c = pl.program_id(0)
    nx = f_ref.shape[2]
    fields = [f_ref[v, 0] for v in range(NV)]
    for v in range(NV):
        w_ref[0, v:v + 1, :] = fields[v][0:1, :]
        e_ref[0, v:v + 1, :] = fields[v][nx - 1:nx, :]
    pack(pack_ref, fields, c)

    @pl.when(c == pl.num_programs(0) - 1)
    def _():
        send_packed(pack_ref, g_ref)


def combine(inv_ref, r_ref, out_ref):
    ncol = r_ref.shape[1]
    rs = [r_ref[0, d] for d in range(ncol)]
    for c in range(ncol):
        acc = inv_ref[c, 0] * rs[0]
        for d in range(1, ncol):
            acc = acc + inv_ref[c, d] * rs[d]
        out_ref[0, c] = acc


def local(forcing, velocity, viscosity, sound, coupling):
    nv, ncol, nx, ny = forcing.shape
    f32 = jnp.float32
    whole = lambda shape: pl.BlockSpec(shape, lambda c: (0,) * len(shape))
    column = pl.BlockSpec((nv, 1, nx, ny), lambda c: (0, c, 0, 0))
    edge_x = pl.BlockSpec((1, nv, ny), lambda c: (c, 0, 0))
    coef_specs = [whole((2, nx, ny)), whole((nx, ny)), whole((nx, ny)), whole((nv, nv, nx, ny))]
    params = pltpu.CompilerParams(vmem_limit_bytes=60 * 1024 * 1024)

    width = 2 * nv * ncol
    packed = whole((width, nx))
    packed_shape = jax.ShapeDtypeStruct((width, nx), f32)
    tile = pltpu.VMEM((nx, ny), f32)
    fw, fe, fg = pl.pallas_call(
        edges,
        grid=(ncol,),
        in_specs=[column],
        out_specs=[edge_x, edge_x, packed],
        out_shape=[
            jax.ShapeDtypeStruct((ncol, nv, ny), f32),
            jax.ShapeDtypeStruct((ncol, nv, ny), f32),
            packed_shape,
        ],
        scratch_shapes=[tile],
        compiler_params=params,
    )(forcing)
    hw, he = exchange(fw, fe, "gx")
    gb, ga = exchange(fg, fg, "gy")

    first, middle, mw, me, mg = pl.pallas_call(
        stage_one,
        grid=(ncol,),
        in_specs=[column] + coef_specs + [edge_x, edge_x, packed, packed],
        out_specs=[column, column, edge_x, edge_x, packed],
        out_shape=[
            jax.ShapeDtypeStruct(forcing.shape, f32),
            jax.ShapeDtypeStruct(forcing.shape, f32),
            jax.ShapeDtypeStruct((ncol, nv, ny), f32),
            jax.ShapeDtypeStruct((ncol, nv, ny), f32),
            packed_shape,
        ],
        scratch_shapes=[tile, tile, tile],
        compiler_params=params,
    )(forcing, velocity, viscosity, sound, coupling, hw, he, gb, ga)

    hw2, he2 = exchange(mw, me, "gx")
    gb2, ga2 = exchange(mg, mg, "gy")

    response, partial = pl.pallas_call(
        stage_two,
        grid=(ncol,),
        in_specs=[column, column, column] + coef_specs + [edge_x, edge_x, packed, packed],
        out_specs=[whole(forcing.shape), whole((ncol * ncol, ny))],
        out_shape=[
            jax.ShapeDtypeStruct(forcing.shape, f32),
            jax.ShapeDtypeStruct((ncol * ncol, ny), f32),
        ],
        compiler_params=pltpu.CompilerParams(
            vmem_limit_bytes=60 * 1024 * 1024, dimension_semantics=("arbitrary",)
        ),
        scratch_shapes=[tile, tile],
    )(forcing, first, middle, velocity, viscosity, sound, coupling, hw2, he2, gb2, ga2)

    rows_total = float(nv * nx * ny * lax.axis_size("gx") * lax.axis_size("gy"))
    local_gram = jnp.sum(partial, axis=1).reshape(ncol, ncol) / rows_total
    lower = jnp.linalg.cholesky(all_sum(local_gram))
    identity = jnp.eye(lower.shape[0], dtype=lower.dtype)
    inverse = lax.linalg.triangular_solve(lower, identity, left_side=True, lower=True)

    basis = pl.pallas_call(
        combine,
        grid=(nv,),
        in_specs=[
            pl.BlockSpec(memory_space=pltpu.SMEM),
            pl.BlockSpec((1, ncol, nx, ny), lambda v: (v, 0, 0, 0)),
        ],
        out_specs=pl.BlockSpec((1, ncol, nx, ny), lambda v: (v, 0, 0, 0)),
        out_shape=jax.ShapeDtypeStruct(forcing.shape, f32),
        compiler_params=params,
    )(inverse, response)
    return (basis, lower.T)


def solution(mesh):
    in_specs = (
        P(None, None, "gx", "gy"),
        P(None, "gx", "gy"),
        P("gx", "gy"),
        P("gx", "gy"),
        P(None, None, "gx", "gy"),
    )
    out_specs = (P(None, None, "gx", "gy"), P())
    return jax.shard_map(local, mesh=mesh, in_specs=in_specs, out_specs=out_specs, check_vma=False)
```

time: 119 us -> 117 us (0.983)
  waiting for transfers between devices: 27.4 us -> 23.1 us
  starting transfers between devices: 40.7 us -> 44 us
  Pallas kernels: 42.7 us -> 40.5 us
    ppermute x8, waiting for transfers between devices: 21.2 us -> 17.1 us  [all_sum(): lax.ppermute(value, axis, [(i, i ^ bit) for i in range(count)])]
    ppermute x8, starting transfers between devices: 17.2 us -> 21.1 us  [all_sum(): lax.ppermute(value, axis, [(i, i ^ bit) for i in range(count)])]
    pallas_call x1, Pallas kernels: 18 us -> 14.6 us  [local(): pl.pallas_call(stage_two, grid=(ncol,), in_specs=[column, column, column]...]
where the time goes in v5:
time: 117 us; the launch traced here: 116 us
  starting transfers between devices  44 us (38%)
  Pallas kernels  40.5 us (35%)
  waiting for transfers between devices  23.1 us (20%)
  other arithmetic  3.56 us (3%)
  local copies, waits for them, and re-layouts  2.75 us (2%)
    ppermute x8, starting transfers between devices, all_sum(): lax.ppermute(value, axis, [(i, i ^ bit) for i in range(count)])  21.1 us
    ppermute x8, waiting for transfers between devices, all_sum(): lax.ppermute(value, axis, [(i, i ^ bit) for i in range(count)])  17.1 us
    pallas_call x1, Pallas kernels, local(): pl.pallas_call(stage_two, grid=(ncol,), in_specs=[column, column, column]...  14.6 us
    ppermute x4, starting transfers between devices, exchange(): from_above = lax.ppermute(low, axis, [(i + 1, i) for i in range(count - 1)])  13.5 us
    pallas_call x1, Pallas kernels, local(): pl.pallas_call(stage_one, grid=(ncol,), in_specs=[column] + coef_specs +...  13.1 us
    ppermute x4, starting transfers between devices, exchange(): lax.ppermute(high, axis, [(i, i + 1) for i in range(count - 1)])  9.4 us
    pallas_call x1, Pallas kernels, local(): pl.pallas_call(edges, grid=(ncol,), in_specs=[column], out_specs=[edge_x,...  7.02 us
    ppermute x4, waiting for transfers between devices, exchange(): from_above = lax.ppermute(low, axis, [(i + 1, i) for i in range(count - 1)])  5.92 us
  transfers between devices with their start and end apart: 16, of which 10 were waited for; matrix products, arithmetic and copies ran while one was open for 0% of the time, Pallas kernels for 0%

profile of v5, /device:TPU:2, one launch (start us, length us, event | category | flops | bytes accessed | tf_op | source)
XLA Modules:
  0.0 115.5 jit_solution(8410363250629701353)
XLA Ops:
  0.6 7.0 %shard_map.68 = (f32[8,4,128]{2,1,0:T(4,128)}, f32[8,4,128]{2,1,0:T(4,128)}, f32[64,256]{1,0:T(8,128)}) custom-call(f32[4,8,256,128]{3,2,1,0:T(8,128)} %f_ref.5), custom_call_target="tpu_custom_call" | custom-call | tf_op jit(solution)/shard_map/pallas_call | solution.py:182
  7.6 4.9 %collective-permute-start.3 = (f32[64,256]{1,0:T(8,128)}, f32[64,256]{1,0:T(8,128)S(1)}, u32[]{:S(2)}, u32[]{:S(2)}) collective-permute-start(f32[64,256]{1,0:T(8,128)} %get-tuple-element.14), channel_id=1, source_target_pairs={{1,0},{2,1},{3,2},{4,3},{5,4},{6,5},{7,6},{8,7},{9,8},{10,9},{11,1... | collective-permute-start | bytes 196616 | tf_op jit(solution)/shard_map/ppermute | solution.py:25
  12.5 1.9 %collective-permute-start.2 = (f32[64,256]{1,0:T(8,128)}, f32[64,256]{1,0:T(8,128)S(1)}, u32[]{:S(2)}, u32[]{:S(2)}) collective-permute-start(f32[64,256]{1,0:T(8,128)} %get-tuple-element.14), channel_id=1, source_target_pairs={{0,1},{1,2},{2,3},{3,4},{4,5},{5,6},{6,7},{7,8},{8,9},{9,10},{10,1... | collective-permute-start | bytes 196616 | tf_op jit(solution)/shard_map/ppermute | solution.py:24
  14.5 1.5 %collective-permute-start = (f32[8,4,128]{2,1,0:T(4,128)}, f32[8,4,128]{2,1,0:T(4,128)S(1)}, u32[]{:S(2)}, u32[]{:S(2)}) collective-permute-start(f32[8,4,128]{2,1,0:T(4,128)} %get-tuple-element.12), channel_id=1, source_target_pairs={{0,16},{16,32},{32,48},{48,64},{64,80},{80,96},{96,112},{112,128},... | collective-permute-start | bytes 49160 | tf_op jit(solution)/shard_map/ppermute | solution.py:24
  17.3 4.0 %collective-permute-done.1.he_ref = f32[8,4,128]{2,1,0:T(4,128)S(1)} collective-permute-done((f32[8,4,128]{2,1,0:T(4,128)}, f32[8,4,128]{2,1,0:T(4,128)S(1)}, u32[]{:S(2)}, u32[]{:S(2)}) %collective-permute-start.1) | collective-permute-done | bytes 16416 | tf_op jit(solution)/shard_map/ppermute | solution.py:25
  22.5 13.1 %shard_map.69 = (f32[4,8,256,128]{3,2,1,0:T(8,128)}, f32[4,8,256,128]{3,2,1,0:T(8,128)}, f32[8,4,128]{2,1,0:T(4,128)}, f32[8,4,128]{2,1,0:T(4,128)}, f32[64,256]{1,0:T(8,128)}) custom-call(f32[4,8,256,128]{3,2,1,0:T(8,128)} %f_ref.5, f32[2,256,128]{2,1,0:T(8,128)} %vel_ref.3, f32[256,128]{1,0:T(8,128)} %visc_ref.3, f32[256,128]{1,0:T(8,128)} %snd_ref.3, ...), custom_call_target="tpu_custom_call" | custom-call | tf_op jit(solution)/shard_map/pallas_call | solution.py:198
  35.6 6.0 %collective-permute-start.7 = (f32[64,256]{1,0:T(8,128)}, f32[64,256]{1,0:T(8,128)S(1)}, u32[]{:S(2)}, u32[]{:S(2)}) collective-permute-start(f32[64,256]{1,0:T(8,128)} %get-tuple-element.19), channel_id=1, source_target_pairs={{1,0},{2,1},{3,2},{4,3},{5,4},{6,5},{7,6},{8,7},{9,8},{10,9},{11,1... | collective-permute-start | bytes 196616 | tf_op jit(solution)/shard_map/ppermute | solution.py:25
  41.6 1.9 %collective-permute-start.6 = (f32[64,256]{1,0:T(8,128)}, f32[64,256]{1,0:T(8,128)S(1)}, u32[]{:S(2)}, u32[]{:S(2)}) collective-permute-start(f32[64,256]{1,0:T(8,128)} %get-tuple-element.19), channel_id=1, source_target_pairs={{0,1},{1,2},{2,3},{3,4},{4,5},{5,6},{6,7},{7,8},{8,9},{9,10},{10,1... | collective-permute-start | bytes 196616 | tf_op jit(solution)/shard_map/ppermute | solution.py:24
  43.5 4.1 %collective-permute-start.4 = (f32[8,4,128]{2,1,0:T(4,128)}, f32[8,4,128]{2,1,0:T(4,128)S(1)}, u32[]{:S(2)}, u32[]{:S(2)}) collective-permute-start(f32[8,4,128]{2,1,0:T(4,128)} %get-tuple-element.17), channel_id=1, source_target_pairs={{0,16},{16,32},{32,48},{48,64},{64,80},{80,96},{96,112},{112,128},... | collective-permute-start | bytes 49160 | tf_op jit(solution)/shard_map/ppermute | solution.py:24
  49.0 2.0 %collective-permute-done.5.he_ref = f32[8,4,128]{2,1,0:T(4,128)S(1)} collective-permute-done((f32[8,4,128]{2,1,0:T(4,128)}, f32[8,4,128]{2,1,0:T(4,128)S(1)}, u32[]{:S(2)}, u32[]{:S(2)}) %collective-permute-start.5) | collective-permute-done | bytes 16416 | tf_op jit(solution)/shard_map/ppermute | solution.py:25
  51.6 14.6 %shard_map.70 = (f32[4,8,256,128]{3,2,1,0:T(8,128)}, f32[64,128]{1,0:T(8,128)}) custom-call(f32[4,8,256,128]{3,2,1,0:T(8,128)} %f_ref.5, f32[4,8,256,128]{3,2,1,0:T(8,128)} %get-tuple-element.15.first_ref, f32[4,8,256,128]{3,2,1,0:T(8,128)} %get-tuple-element.16.mid_ref, f32[2,256,128]{2,1,0:T(8,128)} %vel_ref.3, f32[256,128]{1,0:T(8,128)} %visc_ref.3, ...), custom_call_target="tpu_custom_call" | custom-call | tf_op jit(solution)/shard_map/pallas_call | solution.py:217
  67.2 3.6 %collective-permute-done.8 = f32[8,8]{0,1:T(8,128)S(1)} collective-permute-done((f32[8,8]{0,1:T(8,128)S(1)}, f32[8,8]{0,1:T(8,128)S(1)}, u32[]{:S(2)}, u32[]{:S(2)}) %collective-permute-start.8) | collective-permute-done | bytes 288 | tf_op jit(solution)/shard_map/ppermute | solution.py:17
  70.8 3.4 %collective-permute-start.9 = (f32[8,8]{0,1:T(8,128)S(1)}, f32[8,8]{0,1:T(8,128)S(1)}, u32[]{:S(2)}, u32[]{:S(2)}) collective-permute-start(f32[8,8]{0,1:T(8,128)S(1)} %add.35), channel_id=1, source_target_pairs={{0,2},{1,3},{2,0},{3,1},{4,6},{5,7},{6,4},{7,5},{8,10},{9,11},{10,... | collective-permute-start | bytes 776 | tf_op jit(solution)/shard_map/ppermute | solution.py:17
  74.3 1.7 %collective-permute-done.9 = f32[8,8]{0,1:T(8,128)S(1)} collective-permute-done((f32[8,8]{0,1:T(8,128)S(1)}, f32[8,8]{0,1:T(8,128)S(1)}, u32[]{:S(2)}, u32[]{:S(2)}) %collective-permute-start.9) | collective-permute-done | bytes 288 | tf_op jit(solution)/shard_map/ppermute | solution.py:17
  76.4 3.2 %collective-permute-done.10 = f32[8,8]{0,1:T(8,128)S(1)} collective-permute-done((f32[8,8]{0,1:T(8,128)S(1)}, f32[8,8]{0,1:T(8,128)S(1)}, u32[]{:S(2)}, u32[]{:S(2)}) %collective-permute-start.10) | collective-permute-done | bytes 288 | tf_op jit(solution)/shard_map/ppermute | solution.py:17
  79.6 2.4 %collective-permute-start.11 = (f32[8,8]{0,1:T(8,128)S(1)}, f32[8,8]{0,1:T(8,128)S(1)}, u32[]{:S(2)}, u32[]{:S(2)}) collective-permute-start(f32[8,8]{0,1:T(8,128)S(1)} %add.37), channel_id=1, source_target_pairs={{0,8},{1,9},{2,10},{3,11},{4,12},{5,13},{6,14},{7,15},{8,0},{9,1},... | collective-permute-start | bytes 776 | tf_op jit(solution)/shard_map/ppermute | solution.py:17
  82.0 2.7 %collective-permute-done.11 = f32[8,8]{0,1:T(8,128)S(1)} collective-permute-done((f32[8,8]{0,1:T(8,128)S(1)}, f32[8,8]{0,1:T(8,128)S(1)}, u32[]{:S(2)}, u32[]{:S(2)}) %collective-permute-start.11) | collective-permute-done | bytes 288 | tf_op jit(solution)/shard_map/ppermute | solution.py:17
  85.9 2.3 %collective-permute-start.13 = (f32[8,8]{0,1:T(8,128)S(1)}, f32[8,8]{0,1:T(8,128)S(1)}, u32[]{:S(2)}, u32[]{:S(2)}) collective-permute-start(f32[8,8]{0,1:T(8,128)S(1)} %add.39), channel_id=1, source_target_pairs={{0,32},{16,48},{32,0},{48,16},{64,96},{80,112},{96,64},{112,80},{1... | collective-permute-start | bytes 776 | tf_op jit(solution)/shard_map/ppermute | solution.py:17
  88.1 1.6 %collective-permute-done.13 = f32[8,8]{0,1:T(8,128)S(1)} collective-permute-done((f32[8,8]{0,1:T(8,128)S(1)}, f32[8,8]{0,1:T(8,128)S(1)}, u32[]{:S(2)}, u32[]{:S(2)}) %collective-permute-start.13) | collective-permute-done | bytes 288 | tf_op jit(solution)/shard_map/ppermute | solution.py:17
  89.7 5.6 %collective-permute-start.14 = (f32[8,8]{0,1:T(8,128)S(1)}, f32[8,8]{0,1:T(8,128)S(1)}, u32[]{:S(2)}, u32[]{:S(2)}) collective-permute-start(f32[8,8]{0,1:T(8,128)S(1)} %add.40), channel_id=1, source_target_pairs={{0,64},{16,80},{32,96},{48,112},{64,0},{80,16},{96,32},{112,48},{1... | collective-permute-start | bytes 776 | tf_op jit(solution)/shard_map/ppermute | solution.py:17
  95.3 1.6 %collective-permute-done.14 = f32[8,8]{0,1:T(8,128)S(1)} collective-permute-done((f32[8,8]{0,1:T(8,128)S(1)}, f32[8,8]{0,1:T(8,128)S(1)}, u32[]{:S(2)}, u32[]{:S(2)}) %collective-permute-start.14) | collective-permute-done | bytes 288 | tf_op jit(solution)/shard_map/ppermute | solution.py:17
  96.9 7.0 %collective-permute-start.15 = (f32[8,8]{0,1:T(8,128)S(1)}, f32[8,8]{0,1:T(8,128)S(1)}, u32[]{:S(2)}, u32[]{:S(2)}) collective-permute-start(f32[8,8]{0,1:T(8,128)S(1)} %add.41), channel_id=1, source_target_pairs={{0,128},{16,144},{32,160},{48,176},{64,192},{80,208},{96,224},{112... | collective-permute-start | bytes 776 | tf_op jit(solution)/shard_map/ppermute | solution.py:17
  103.9 1.6 %collective-permute-done.15 = f32[8,8]{0,1:T(8,128)S(1)} collective-permute-done((f32[8,8]{0,1:T(8,128)S(1)}, f32[8,8]{0,1:T(8,128)S(1)}, u32[]{:S(2)}, u32[]{:S(2)}) %collective-permute-start.15) | collective-permute-done | bytes 288 | tf_op jit(solution)/shard_map/ppermute | solution.py:17
  109.7 5.8 %shard_map.71 = f32[4,8,256,128]{3,2,1,0:T(8,128)} custom-call(f32[8,8]{1,0:T(8,128)} %fusion.inv_ref, f32[4,8,256,128]{3,2,1,0:T(8,128)} %get-tuple-element.21.r_ref), custom_call_target="tpu_custom_call" | custom-call | tf_op jit(solution)/shard_map/pallas_call | solution.py:238
  (49 shorter events, 11.3 us)
Async XLA Ops:
  7.6 13.6 %collective-permute-start.3 = (f32[64,256]{1,0:T(8,128)}, f32[64,256]{1,0:T(8,128)S(1)}, u32[]{:S(2)}, u32[]{:S(2)}) collective-permute-start(f32[64,256]{1,0:T(8,128)} %get-tuple-element.14), channel_id=1, source_target_pairs={{1,0},{2,1},{3,2},{4,3},{5,4},{6,5},{7,6},{8,7},{9,8},{10,9},{11,1... | collective-permute-start | bytes 196616 | tf_op jit(solution)/shard_map/ppermute | solution.py:25
  12.5 8.7 %collective-permute-start.2 = (f32[64,256]{1,0:T(8,128)}, f32[64,256]{1,0:T(8,128)S(1)}, u32[]{:S(2)}, u32[]{:S(2)}) collective-permute-start(f32[64,256]{1,0:T(8,128)} %get-tuple-element.14), channel_id=1, source_target_pairs={{0,1},{1,2},{2,3},{3,4},{4,5},{5,6},{6,7},{7,8},{8,9},{9,10},{10,1... | collective-permute-start | bytes 196616 | tf_op jit(solution)/shard_map/ppermute | solution.py:24
  14.5 2.8 %collective-permute-start = (f32[8,4,128]{2,1,0:T(4,128)}, f32[8,4,128]{2,1,0:T(4,128)S(1)}, u32[]{:S(2)}, u32[]{:S(2)}) collective-permute-start(f32[8,4,128]{2,1,0:T(4,128)} %get-tuple-element.12), channel_id=1, source_target_pairs={{0,16},{16,32},{32,48},{48,64},{64,80},{80,96},{96,112},{112,128},... | collective-permute-start | bytes 49160 | tf_op jit(solution)/shard_map/ppermute | solution.py:24
  15.9 5.3 %collective-permute-start.1 = (f32[8,4,128]{2,1,0:T(4,128)}, f32[8,4,128]{2,1,0:T(4,128)S(1)}, u32[]{:S(2)}, u32[]{:S(2)}) collective-permute-start(f32[8,4,128]{2,1,0:T(4,128)} %get-tuple-element.13), channel_id=1, source_target_pairs={{16,0},{32,16},{48,32},{64,48},{80,64},{96,80},{112,96},{128,112},... | collective-permute-start | bytes 49160 | tf_op jit(solution)/shard_map/ppermute | solution.py:25
  17.2 4.0 %copy-start.4 = (f32[8,4,128]{2,1,0:T(4,128)}, f32[8,4,128]{2,1,0:T(4,128)S(1)}, u32[]{:S(2)}) copy-start(f32[8,4,128]{2,1,0:T(4,128)S(1)} %collective-permute-done.hw_ref) | copy-start | bytes 49156
  21.2 0.6 copy-start.5
  21.2 0.6 copy-start
  21.8 0.6 copy-start.2
  35.6 15.4 %collective-permute-start.7 = (f32[64,256]{1,0:T(8,128)}, f32[64,256]{1,0:T(8,128)S(1)}, u32[]{:S(2)}, u32[]{:S(2)}) collective-permute-start(f32[64,256]{1,0:T(8,128)} %get-tuple-element.19), channel_id=1, source_target_pairs={{1,0},{2,1},{3,2},{4,3},{5,4},{6,5},{7,6},{8,7},{9,8},{10,9},{11,1... | collective-permute-start | bytes 196616 | tf_op jit(solution)/shard_map/ppermute | solution.py:25
  41.6 9.3 %collective-permute-start.6 = (f32[64,256]{1,0:T(8,128)}, f32[64,256]{1,0:T(8,128)S(1)}, u32[]{:S(2)}, u32[]{:S(2)}) collective-permute-start(f32[64,256]{1,0:T(8,128)} %get-tuple-element.19), channel_id=1, source_target_pairs={{0,1},{1,2},{2,3},{3,4},{4,5},{5,6},{6,7},{7,8},{8,9},{9,10},{10,1... | collective-permute-start | bytes 196616 | tf_op jit(solution)/shard_map/ppermute | solution.py:24
  43.5 5.4 %collective-permute-start.4 = (f32[8,4,128]{2,1,0:T(4,128)}, f32[8,4,128]{2,1,0:T(4,128)S(1)}, u32[]{:S(2)}, u32[]{:S(2)}) collective-permute-start(f32[8,4,128]{2,1,0:T(4,128)} %get-tuple-element.17), channel_id=1, source_target_pairs={{0,16},{16,32},{32,48},{48,64},{64,80},{80,96},{96,112},{112,128},... | collective-permute-start | bytes 49160 | tf_op jit(solution)/shard_map/ppermute | solution.py:24
  47.7 3.3 %collective-permute-start.5 = (f32[8,4,128]{2,1,0:T(4,128)}, f32[8,4,128]{2,1,0:T(4,128)S(1)}, u32[]{:S(2)}, u32[]{:S(2)}) collective-permute-start(f32[8,4,128]{2,1,0:T(4,128)} %get-tuple-element.18), channel_id=1, source_target_pairs={{16,0},{32,16},{48,32},{64,48},{80,64},{96,80},{112,96},{128,112},... | collective-permute-start | bytes 49160 | tf_op jit(solution)/shard_map/ppermute | solution.py:25
  49.0 2.0 %copy-start.6 = (f32[8,4,128]{2,1,0:T(4,128)}, f32[8,4,128]{2,1,0:T(4,128)S(1)}, u32[]{:S(2)}) copy-start(f32[8,4,128]{2,1,0:T(4,128)S(1)} %collective-permute-done.4.hw_ref) | copy-start | bytes 49156
  50.9 0.6 copy-start.7
  50.9 0.6 copy-start.1
  51.0 0.6 copy-start.3
  67.2 3.6 %collective-permute-start.8 = (f32[8,8]{0,1:T(8,128)S(1)}, f32[8,8]{0,1:T(8,128)S(1)}, u32[]{:S(2)}, u32[]{:S(2)}) collective-permute-start(f32[8,8]{0,1:T(8,128)S(1)} %copy.8), channel_id=1, source_target_pairs={{0,1},{1,0},{2,3},{3,2},{4,5},{5,4},{6,7},{7,6},{8,9},{9,8},{10,11... | collective-permute-start | bytes 776 | tf_op jit(solution)/shard_map/ppermute | solution.py:17
  70.8 5.1 %collective-permute-start.9 = (f32[8,8]{0,1:T(8,128)S(1)}, f32[8,8]{0,1:T(8,128)S(1)}, u32[]{:S(2)}, u32[]{:S(2)}) collective-permute-start(f32[8,8]{0,1:T(8,128)S(1)} %add.35), channel_id=1, source_target_pairs={{0,2},{1,3},{2,0},{3,1},{4,6},{5,7},{6,4},{7,5},{8,10},{9,11},{10,... | collective-permute-start | bytes 776 | tf_op jit(solution)/shard_map/ppermute | solution.py:17
  76.0 3.6 %collective-permute-start.10 = (f32[8,8]{0,1:T(8,128)S(1)}, f32[8,8]{0,1:T(8,128)S(1)}, u32[]{:S(2)}, u32[]{:S(2)}) collective-permute-start(f32[8,8]{0,1:T(8,128)S(1)} %add.36), channel_id=1, source_target_pairs={{0,4},{1,5},{2,6},{3,7},{4,0},{5,1},{6,2},{7,3},{8,12},{9,13},{10,... | collective-permute-start | bytes 776 | tf_op jit(solution)/shard_map/ppermute | solution.py:17
  79.6 5.1 %collective-permute-start.11 = (f32[8,8]{0,1:T(8,128)S(1)}, f32[8,8]{0,1:T(8,128)S(1)}, u32[]{:S(2)}, u32[]{:S(2)}) collective-permute-start(f32[8,8]{0,1:T(8,128)S(1)} %add.37), channel_id=1, source_target_pairs={{0,8},{1,9},{2,10},{3,11},{4,12},{5,13},{6,14},{7,15},{8,0},{9,1},... | collective-permute-start | bytes 776 | tf_op jit(solution)/shard_map/ppermute | solution.py:17
  84.7 1.2 %collective-permute-start.12 = (f32[8,8]{0,1:T(8,128)S(1)}, f32[8,8]{0,1:T(8,128)S(1)}, u32[]{:S(2)}, u32[]{:S(2)}) collective-permute-start(f32[8,8]{0,1:T(8,128)S(1)} %add.38), channel_id=1, source_target_pairs={{0,16},{16,0},{32,48},{48,32},{64,80},{80,64},{96,112},{112,96},{1... | collective-permute-start | bytes 776 | tf_op jit(solution)/shard_map/ppermute | solution.py:17
  85.9 3.8 %collective-permute-start.13 = (f32[8,8]{0,1:T(8,128)S(1)}, f32[8,8]{0,1:T(8,128)S(1)}, u32[]{:S(2)}, u32[]{:S(2)}) collective-permute-start(f32[8,8]{0,1:T(8,128)S(1)} %add.39), channel_id=1, source_target_pairs={{0,32},{16,48},{32,0},{48,16},{64,96},{80,112},{96,64},{112,80},{1... | collective-permute-start | bytes 776 | tf_op jit(solution)/shard_map/ppermute | solution.py:17
  89.7 7.2 %collective-permute-start.14 = (f32[8,8]{0,1:T(8,128)S(1)}, f32[8,8]{0,1:T(8,128)S(1)}, u32[]{:S(2)}, u32[]{:S(2)}) collective-permute-start(f32[8,8]{0,1:T(8,128)S(1)} %add.40), channel_id=1, source_target_pairs={{0,64},{16,80},{32,96},{48,112},{64,0},{80,16},{96,32},{112,48},{1... | collective-permute-start | bytes 776 | tf_op jit(solution)/shard_map/ppermute | solution.py:17
  96.9 8.6 %collective-permute-start.15 = (f32[8,8]{0,1:T(8,128)S(1)}, f32[8,8]{0,1:T(8,128)S(1)}, u32[]{:S(2)}, u32[]{:S(2)}) collective-permute-start(f32[8,8]{0,1:T(8,128)S(1)} %add.41), channel_id=1, source_target_pairs={{0,128},{16,144},{32,160},{48,176},{64,192},{80,208},{96,224},{112... | collective-permute-start | bytes 776 | tf_op jit(solution)/shard_map/ppermute | solution.py:17

commit v6 on v5

--- a/solution.py
+++ b/solution.py
@@ -143,17 +143,14 @@
 
 
 def edges(f_ref, w_ref, e_ref, g_ref, pack_ref):
-    c = pl.program_id(0)
-    nx = f_ref.shape[2]
-    fields = [f_ref[v, 0] for v in range(NV)]
-    for v in range(NV):
-        w_ref[0, v:v + 1, :] = fields[v][0:1, :]
-        e_ref[0, v:v + 1, :] = fields[v][nx - 1:nx, :]
-    pack(pack_ref, fields, c)
-
-    @pl.when(c == pl.num_programs(0) - 1)
-    def _():
-        send_packed(pack_ref, g_ref)
+    ncol, nx = f_ref.shape[1], f_ref.shape[2]
+    for c in range(ncol):
+        fields = [f_ref[v, c] for v in range(NV)]
+        for v in range(NV):
+            w_ref[c, v:v + 1, :] = fields[v][0:1, :]
+            e_ref[c, v:v + 1, :] = fields[v][nx - 1:nx, :]
+        pack(pack_ref, fields, c)
+    send_packed(pack_ref, g_ref)
 
 
 def combine(inv_ref, r_ref, out_ref):
@@ -181,9 +178,8 @@
     tile = pltpu.VMEM((nx, ny), f32)
     fw, fe, fg = pl.pallas_call(
         edges,
-        grid=(ncol,),
-        in_specs=[column],
-        out_specs=[edge_x, edge_x, packed],
+        in_specs=[pl.BlockSpec(memory_space=pltpu.VMEM)],
+        out_specs=[pl.BlockSpec(memory_space=pltpu.VMEM)] * 3,
         out_shape=[
             jax.ShapeDtypeStruct((ncol, nv, ny), f32),
             jax.ShapeDtypeStruct((ncol, nv, ny), f32),

time: 117 us -> 116 us (level)
  Pallas kernels: 40.5 us -> 38.9 us
    pallas_call x1, Pallas kernels: 7.02 us -> 5.43 us  [local(): pl.pallas_call(edges, in_specs=[pl.BlockSpec(memory_space=pltpu.VMEM)], o...]
where the time goes in v6:
time: 116 us; the launch traced here: 114 us
  starting transfers between devices  44 us (38%)
  Pallas kernels  38.9 us (34%)
  waiting for transfers between devices  23.1 us (20%)
  other arithmetic  3.56 us (3%)
  local copies, waits for them, and re-layouts  2.75 us (2%)
    ppermute x8, starting transfers between devices, all_sum(): lax.ppermute(value, axis, [(i, i ^ bit) for i in range(count)])  21.1 us
    ppermute x8, waiting for transfers between devices, all_sum(): lax.ppermute(value, axis, [(i, i ^ bit) for i in range(count)])  17.1 us
    pallas_call x1, Pallas kernels, local(): pl.pallas_call(stage_two, grid=(ncol,), in_specs=[column, column, column]...  14.6 us
    ppermute x4, starting transfers between devices, exchange(): from_above = lax.ppermute(low, axis, [(i + 1, i) for i in range(count - 1)])  13.5 us
    pallas_call x1, Pallas kernels, local(): pl.pallas_call(stage_one, grid=(ncol,), in_specs=[column] + coef_specs +...  13.1 us
    ppermute x4, starting transfers between devices, exchange(): lax.ppermute(high, axis, [(i, i + 1) for i in range(count - 1)])  9.4 us
    ppermute x4, waiting for transfers between devices, exchange(): from_above = lax.ppermute(low, axis, [(i + 1, i) for i in range(count - 1)])  5.92 us
    pallas_call x1, Pallas kernels, local(): pl.pallas_call(combine, grid=(nv,), in_specs=[pl.BlockSpec(memory_space=p...  5.78 us
  transfers between devices with their start and end apart: 16, of which 10 were waited for; matrix products, arithmetic and copies ran while one was open for 0% of the time, Pallas kernels for 0%

profile of v6, /device:TPU:2, one launch (start us, length us, event | category | flops | bytes accessed | tf_op | source)
XLA Modules:
  0.0 113.9 jit_solution(8709533388291038131)
XLA Ops:
  0.6 5.4 %shard_map.68 = (f32[8,4,128]{2,1,0:T(4,128)}, f32[8,4,128]{2,1,0:T(4,128)}, f32[64,256]{1,0:T(8,128)}) custom-call(f32[4,8,256,128]{3,2,1,0:T(8,128)} %f_ref.5), custom_call_target="tpu_custom_call" | custom-call | tf_op jit(solution)/shard_map/pallas_call | solution.py:179
  6.1 4.9 %collective-permute-start.3 = (f32[64,256]{1,0:T(8,128)}, f32[64,256]{1,0:T(8,128)S(1)}, u32[]{:S(2)}, u32[]{:S(2)}) collective-permute-start(f32[64,256]{1,0:T(8,128)} %get-tuple-element.14), channel_id=1, source_target_pairs={{1,0},{2,1},{3,2},{4,3},{5,4},{6,5},{7,6},{8,7},{9,8},{10,9},{11,1... | collective-permute-start | bytes 196616 | tf_op jit(solution)/shard_map/ppermute | solution.py:25
  10.9 1.9 %collective-permute-start.2 = (f32[64,256]{1,0:T(8,128)}, f32[64,256]{1,0:T(8,128)S(1)}, u32[]{:S(2)}, u32[]{:S(2)}) collective-permute-start(f32[64,256]{1,0:T(8,128)} %get-tuple-element.14), channel_id=1, source_target_pairs={{0,1},{1,2},{2,3},{3,4},{4,5},{5,6},{6,7},{7,8},{8,9},{9,10},{10,1... | collective-permute-start | bytes 196616 | tf_op jit(solution)/shard_map/ppermute | solution.py:24
  12.9 1.5 %collective-permute-start = (f32[8,4,128]{2,1,0:T(4,128)}, f32[8,4,128]{2,1,0:T(4,128)S(1)}, u32[]{:S(2)}, u32[]{:S(2)}) collective-permute-start(f32[8,4,128]{2,1,0:T(4,128)} %get-tuple-element.12), channel_id=1, source_target_pairs={{0,16},{16,32},{32,48},{48,64},{64,80},{80,96},{96,112},{112,128},... | collective-permute-start | bytes 49160 | tf_op jit(solution)/shard_map/ppermute | solution.py:24
  15.7 4.0 %collective-permute-done.1.he_ref = f32[8,4,128]{2,1,0:T(4,128)S(1)} collective-permute-done((f32[8,4,128]{2,1,0:T(4,128)}, f32[8,4,128]{2,1,0:T(4,128)S(1)}, u32[]{:S(2)}, u32[]{:S(2)}) %collective-permute-start.1) | collective-permute-done | bytes 16416 | tf_op jit(solution)/shard_map/ppermute | solution.py:25
  20.9 13.1 %shard_map.69 = (f32[4,8,256,128]{3,2,1,0:T(8,128)}, f32[4,8,256,128]{3,2,1,0:T(8,128)}, f32[8,4,128]{2,1,0:T(4,128)}, f32[8,4,128]{2,1,0:T(4,128)}, f32[64,256]{1,0:T(8,128)}) custom-call(f32[4,8,256,128]{3,2,1,0:T(8,128)} %f_ref.5, f32[2,256,128]{2,1,0:T(8,128)} %vel_ref.3, f32[256,128]{1,0:T(8,128)} %visc_ref.3, f32[256,128]{1,0:T(8,128)} %snd_ref.3, ...), custom_call_target="tpu_custom_call" | custom-call | tf_op jit(solution)/shard_map/pallas_call | solution.py:194
  34.0 6.0 %collective-permute-start.7 = (f32[64,256]{1,0:T(8,128)}, f32[64,256]{1,0:T(8,128)S(1)}, u32[]{:S(2)}, u32[]{:S(2)}) collective-permute-start(f32[64,256]{1,0:T(8,128)} %get-tuple-element.19), channel_id=1, source_target_pairs={{1,0},{2,1},{3,2},{4,3},{5,4},{6,5},{7,6},{8,7},{9,8},{10,9},{11,1... | collective-permute-start | bytes 196616 | tf_op jit(solution)/shard_map/ppermute | solution.py:25
  40.0 1.9 %collective-permute-start.6 = (f32[64,256]{1,0:T(8,128)}, f32[64,256]{1,0:T(8,128)S(1)}, u32[]{:S(2)}, u32[]{:S(2)}) collective-permute-start(f32[64,256]{1,0:T(8,128)} %get-tuple-element.19), channel_id=1, source_target_pairs={{0,1},{1,2},{2,3},{3,4},{4,5},{5,6},{6,7},{7,8},{8,9},{9,10},{10,1... | collective-permute-start | bytes 196616 | tf_op jit(solution)/shard_map/ppermute | solution.py:24
  42.0 4.1 %collective-permute-start.4 = (f32[8,4,128]{2,1,0:T(4,128)}, f32[8,4,128]{2,1,0:T(4,128)S(1)}, u32[]{:S(2)}, u32[]{:S(2)}) collective-permute-start(f32[8,4,128]{2,1,0:T(4,128)} %get-tuple-element.17), channel_id=1, source_target_pairs={{0,16},{16,32},{32,48},{48,64},{64,80},{80,96},{96,112},{112,128},... | collective-permute-start | bytes 49160 | tf_op jit(solution)/shard_map/ppermute | solution.py:24
  47.4 2.0 %collective-permute-done.5.he_ref = f32[8,4,128]{2,1,0:T(4,128)S(1)} collective-permute-done((f32[8,4,128]{2,1,0:T(4,128)}, f32[8,4,128]{2,1,0:T(4,128)S(1)}, u32[]{:S(2)}, u32[]{:S(2)}) %collective-permute-start.5) | collective-permute-done | bytes 16416 | tf_op jit(solution)/shard_map/ppermute | solution.py:25
  50.0 14.6 %shard_map.70 = (f32[4,8,256,128]{3,2,1,0:T(8,128)}, f32[64,128]{1,0:T(8,128)}) custom-call(f32[4,8,256,128]{3,2,1,0:T(8,128)} %f_ref.5, f32[4,8,256,128]{3,2,1,0:T(8,128)} %get-tuple-element.15.first_ref, f32[4,8,256,128]{3,2,1,0:T(8,128)} %get-tuple-element.16.mid_ref, f32[2,256,128]{2,1,0:T(8,128)} %vel_ref.3, f32[256,128]{1,0:T(8,128)} %visc_ref.3, ...), custom_call_target="tpu_custom_call" | custom-call | tf_op jit(solution)/shard_map/pallas_call | solution.py:213
  65.6 3.6 %collective-permute-done.8 = f32[8,8]{0,1:T(8,128)S(1)} collective-permute-done((f32[8,8]{0,1:T(8,128)S(1)}, f32[8,8]{0,1:T(8,128)S(1)}, u32[]{:S(2)}, u32[]{:S(2)}) %collective-permute-start.8) | collective-permute-done | bytes 288 | tf_op jit(solution)/shard_map/ppermute | solution.py:17
  69.3 3.4 %collective-permute-start.9 = (f32[8,8]{0,1:T(8,128)S(1)}, f32[8,8]{0,1:T(8,128)S(1)}, u32[]{:S(2)}, u32[]{:S(2)}) collective-permute-start(f32[8,8]{0,1:T(8,128)S(1)} %add.35), channel_id=1, source_target_pairs={{0,2},{1,3},{2,0},{3,1},{4,6},{5,7},{6,4},{7,5},{8,10},{9,11},{10,... | collective-permute-start | bytes 776 | tf_op jit(solution)/shard_map/ppermute | solution.py:17
  72.7 1.7 %collective-permute-done.9 = f32[8,8]{0,1:T(8,128)S(1)} collective-permute-done((f32[8,8]{0,1:T(8,128)S(1)}, f32[8,8]{0,1:T(8,128)S(1)}, u32[]{:S(2)}, u32[]{:S(2)}) %collective-permute-start.9) | collective-permute-done | bytes 288 | tf_op jit(solution)/shard_map/ppermute | solution.py:17
  74.8 3.2 %collective-permute-done.10 = f32[8,8]{0,1:T(8,128)S(1)} collective-permute-done((f32[8,8]{0,1:T(8,128)S(1)}, f32[8,8]{0,1:T(8,128)S(1)}, u32[]{:S(2)}, u32[]{:S(2)}) %collective-permute-start.10) | collective-permute-done | bytes 288 | tf_op jit(solution)/shard_map/ppermute | solution.py:17
  78.0 2.4 %collective-permute-start.11 = (f32[8,8]{0,1:T(8,128)S(1)}, f32[8,8]{0,1:T(8,128)S(1)}, u32[]{:S(2)}, u32[]{:S(2)}) collective-permute-start(f32[8,8]{0,1:T(8,128)S(1)} %add.37), channel_id=1, source_target_pairs={{0,8},{1,9},{2,10},{3,11},{4,12},{5,13},{6,14},{7,15},{8,0},{9,1},... | collective-permute-start | bytes 776 | tf_op jit(solution)/shard_map/ppermute | solution.py:17
  80.4 2.7 %collective-permute-done.11 = f32[8,8]{0,1:T(8,128)S(1)} collective-permute-done((f32[8,8]{0,1:T(8,128)S(1)}, f32[8,8]{0,1:T(8,128)S(1)}, u32[]{:S(2)}, u32[]{:S(2)}) %collective-permute-start.11) | collective-permute-done | bytes 288 | tf_op jit(solution)/shard_map/ppermute | solution.py:17
  84.3 2.3 %collective-permute-start.13 = (f32[8,8]{0,1:T(8,128)S(1)}, f32[8,8]{0,1:T(8,128)S(1)}, u32[]{:S(2)}, u32[]{:S(2)}) collective-permute-start(f32[8,8]{0,1:T(8,128)S(1)} %add.39), channel_id=1, source_target_pairs={{0,32},{16,48},{32,0},{48,16},{64,96},{80,112},{96,64},{112,80},{1... | collective-permute-start | bytes 776 | tf_op jit(solution)/shard_map/ppermute | solution.py:17
  86.5 1.6 %collective-permute-done.13 = f32[8,8]{0,1:T(8,128)S(1)} collective-permute-done((f32[8,8]{0,1:T(8,128)S(1)}, f32[8,8]{0,1:T(8,128)S(1)}, u32[]{:S(2)}, u32[]{:S(2)}) %collective-permute-start.13) | collective-permute-done | bytes 288 | tf_op jit(solution)/shard_map/ppermute | solution.py:17
  88.1 5.6 %collective-permute-start.14 = (f32[8,8]{0,1:T(8,128)S(1)}, f32[8,8]{0,1:T(8,128)S(1)}, u32[]{:S(2)}, u32[]{:S(2)}) collective-permute-start(f32[8,8]{0,1:T(8,128)S(1)} %add.40), channel_id=1, source_target_pairs={{0,64},{16,80},{32,96},{48,112},{64,0},{80,16},{96,32},{112,48},{1... | collective-permute-start | bytes 776 | tf_op jit(solution)/shard_map/ppermute | solution.py:17
  93.7 1.6 %collective-permute-done.14 = f32[8,8]{0,1:T(8,128)S(1)} collective-permute-done((f32[8,8]{0,1:T(8,128)S(1)}, f32[8,8]{0,1:T(8,128)S(1)}, u32[]{:S(2)}, u32[]{:S(2)}) %collective-permute-start.14) | collective-permute-done | bytes 288 | tf_op jit(solution)/shard_map/ppermute | solution.py:17
  95.3 7.0 %collective-permute-start.15 = (f32[8,8]{0,1:T(8,128)S(1)}, f32[8,8]{0,1:T(8,128)S(1)}, u32[]{:S(2)}, u32[]{:S(2)}) collective-permute-start(f32[8,8]{0,1:T(8,128)S(1)} %add.41), channel_id=1, source_target_pairs={{0,128},{16,144},{32,160},{48,176},{64,192},{80,208},{96,224},{112... | collective-permute-start | bytes 776 | tf_op jit(solution)/shard_map/ppermute | solution.py:17
  102.4 1.6 %collective-permute-done.15 = f32[8,8]{0,1:T(8,128)S(1)} collective-permute-done((f32[8,8]{0,1:T(8,128)S(1)}, f32[8,8]{0,1:T(8,128)S(1)}, u32[]{:S(2)}, u32[]{:S(2)}) %collective-permute-start.15) | collective-permute-done | bytes 288 | tf_op jit(solution)/shard_map/ppermute | solution.py:17
  108.2 5.8 %shard_map.71 = f32[4,8,256,128]{3,2,1,0:T(8,128)} custom-call(f32[8,8]{1,0:T(8,128)} %fusion.inv_ref, f32[4,8,256,128]{3,2,1,0:T(8,128)} %get-tuple-element.21.r_ref), custom_call_target="tpu_custom_call" | custom-call | tf_op jit(solution)/shard_map/pallas_call | solution.py:234
  (49 shorter events, 11.3 us)
Async XLA Ops:
  6.1 13.6 %collective-permute-start.3 = (f32[64,256]{1,0:T(8,128)}, f32[64,256]{1,0:T(8,128)S(1)}, u32[]{:S(2)}, u32[]{:S(2)}) collective-permute-start(f32[64,256]{1,0:T(8,128)} %get-tuple-element.14), channel_id=1, source_target_pairs={{1,0},{2,1},{3,2},{4,3},{5,4},{6,5},{7,6},{8,7},{9,8},{10,9},{11,1... | collective-permute-start | bytes 196616 | tf_op jit(solution)/shard_map/ppermute | solution.py:25
  10.9 8.7 %collective-permute-start.2 = (f32[64,256]{1,0:T(8,128)}, f32[64,256]{1,0:T(8,128)S(1)}, u32[]{:S(2)}, u32[]{:S(2)}) collective-permute-start(f32[64,256]{1,0:T(8,128)} %get-tuple-element.14), channel_id=1, source_target_pairs={{0,1},{1,2},{2,3},{3,4},{4,5},{5,6},{6,7},{7,8},{8,9},{9,10},{10,1... | collective-permute-start | bytes 196616 | tf_op jit(solution)/shard_map/ppermute | solution.py:24
  12.9 2.8 %collective-permute-start = (f32[8,4,128]{2,1,0:T(4,128)}, f32[8,4,128]{2,1,0:T(4,128)S(1)}, u32[]{:S(2)}, u32[]{:S(2)}) collective-permute-start(f32[8,4,128]{2,1,0:T(4,128)} %get-tuple-element.12), channel_id=1, source_target_pairs={{0,16},{16,32},{32,48},{48,64},{64,80},{80,96},{96,112},{112,128},... | collective-permute-start | bytes 49160 | tf_op jit(solution)/shard_map/ppermute | solution.py:24
  14.3 5.3 %collective-permute-start.1 = (f32[8,4,128]{2,1,0:T(4,128)}, f32[8,4,128]{2,1,0:T(4,128)S(1)}, u32[]{:S(2)}, u32[]{:S(2)}) collective-permute-start(f32[8,4,128]{2,1,0:T(4,128)} %get-tuple-element.13), channel_id=1, source_target_pairs={{16,0},{32,16},{48,32},{64,48},{80,64},{96,80},{112,96},{128,112},... | collective-permute-start | bytes 49160 | tf_op jit(solution)/shard_map/ppermute | solution.py:25
  15.7 4.0 %copy-start.4 = (f32[8,4,128]{2,1,0:T(4,128)}, f32[8,4,128]{2,1,0:T(4,128)S(1)}, u32[]{:S(2)}) copy-start(f32[8,4,128]{2,1,0:T(4,128)S(1)} %collective-permute-done.hw_ref) | copy-start | bytes 49156
  19.6 0.6 copy-start.5
  19.6 0.6 copy-start
  20.3 0.6 copy-start.2
  34.0 15.4 %collective-permute-start.7 = (f32[64,256]{1,0:T(8,128)}, f32[64,256]{1,0:T(8,128)S(1)}, u32[]{:S(2)}, u32[]{:S(2)}) collective-permute-start(f32[64,256]{1,0:T(8,128)} %get-tuple-element.19), channel_id=1, source_target_pairs={{1,0},{2,1},{3,2},{4,3},{5,4},{6,5},{7,6},{8,7},{9,8},{10,9},{11,1... | collective-permute-start | bytes 196616 | tf_op jit(solution)/shard_map/ppermute | solution.py:25
  40.0 9.3 %collective-permute-start.6 = (f32[64,256]{1,0:T(8,128)}, f32[64,256]{1,0:T(8,128)S(1)}, u32[]{:S(2)}, u32[]{:S(2)}) collective-permute-start(f32[64,256]{1,0:T(8,128)} %get-tuple-element.19), channel_id=1, source_target_pairs={{0,1},{1,2},{2,3},{3,4},{4,5},{5,6},{6,7},{7,8},{8,9},{9,10},{10,1... | collective-permute-start | bytes 196616 | tf_op jit(solution)/shard_map/ppermute | solution.py:24
  42.0 5.4 %collective-permute-start.4 = (f32[8,4,128]{2,1,0:T(4,128)}, f32[8,4,128]{2,1,0:T(4,128)S(1)}, u32[]{:S(2)}, u32[]{:S(2)}) collective-permute-start(f32[8,4,128]{2,1,0:T(4,128)} %get-tuple-element.17), channel_id=1, source_target_pairs={{0,16},{16,32},{32,48},{48,64},{64,80},{80,96},{96,112},{112,128},... | collective-permute-start | bytes 49160 | tf_op jit(solution)/shard_map/ppermute | solution.py:24
  46.1 3.3 %collective-permute-start.5 = (f32[8,4,128]{2,1,0:T(4,128)}, f32[8,4,128]{2,1,0:T(4,128)S(1)}, u32[]{:S(2)}, u32[]{:S(2)}) collective-permute-start(f32[8,4,128]{2,1,0:T(4,128)} %get-tuple-element.18), channel_id=1, source_target_pairs={{16,0},{32,16},{48,32},{64,48},{80,64},{96,80},{112,96},{128,112},... | collective-permute-start | bytes 49160 | tf_op jit(solution)/shard_map/ppermute | solution.py:25
  47.4 2.0 %copy-start.6 = (f32[8,4,128]{2,1,0:T(4,128)}, f32[8,4,128]{2,1,0:T(4,128)S(1)}, u32[]{:S(2)}) copy-start(f32[8,4,128]{2,1,0:T(4,128)S(1)} %collective-permute-done.4.hw_ref) | copy-start | bytes 49156
  49.4 0.6 copy-start.7
  49.4 0.6 copy-start.1
  49.4 0.6 copy-start.3
  65.6 3.6 %collective-permute-start.8 = (f32[8,8]{0,1:T(8,128)S(1)}, f32[8,8]{0,1:T(8,128)S(1)}, u32[]{:S(2)}, u32[]{:S(2)}) collective-permute-start(f32[8,8]{0,1:T(8,128)S(1)} %copy.8), channel_id=1, source_target_pairs={{0,1},{1,0},{2,3},{3,2},{4,5},{5,4},{6,7},{7,6},{8,9},{9,8},{10,11... | collective-permute-start | bytes 776 | tf_op jit(solution)/shard_map/ppermute | solution.py:17
  69.3 5.1 %collective-permute-start.9 = (f32[8,8]{0,1:T(8,128)S(1)}, f32[8,8]{0,1:T(8,128)S(1)}, u32[]{:S(2)}, u32[]{:S(2)}) collective-permute-start(f32[8,8]{0,1:T(8,128)S(1)} %add.35), channel_id=1, source_target_pairs={{0,2},{1,3},{2,0},{3,1},{4,6},{5,7},{6,4},{7,5},{8,10},{9,11},{10,... | collective-permute-start | bytes 776 | tf_op jit(solution)/shard_map/ppermute | solution.py:17
  74.4 3.6 %collective-permute-start.10 = (f32[8,8]{0,1:T(8,128)S(1)}, f32[8,8]{0,1:T(8,128)S(1)}, u32[]{:S(2)}, u32[]{:S(2)}) collective-permute-start(f32[8,8]{0,1:T(8,128)S(1)} %add.36), channel_id=1, source_target_pairs={{0,4},{1,5},{2,6},{3,7},{4,0},{5,1},{6,2},{7,3},{8,12},{9,13},{10,... | collective-permute-start | bytes 776 | tf_op jit(solution)/shard_map/ppermute | solution.py:17
  78.0 5.1 %collective-permute-start.11 = (f32[8,8]{0,1:T(8,128)S(1)}, f32[8,8]{0,1:T(8,128)S(1)}, u32[]{:S(2)}, u32[]{:S(2)}) collective-permute-start(f32[8,8]{0,1:T(8,128)S(1)} %add.37), channel_id=1, source_target_pairs={{0,8},{1,9},{2,10},{3,11},{4,12},{5,13},{6,14},{7,15},{8,0},{9,1},... | collective-permute-start | bytes 776 | tf_op jit(solution)/shard_map/ppermute | solution.py:17
  83.1 1.2 %collective-permute-start.12 = (f32[8,8]{0,1:T(8,128)S(1)}, f32[8,8]{0,1:T(8,128)S(1)}, u32[]{:S(2)}, u32[]{:S(2)}) collective-permute-start(f32[8,8]{0,1:T(8,128)S(1)} %add.38), channel_id=1, source_target_pairs={{0,16},{16,0},{32,48},{48,32},{64,80},{80,64},{96,112},{112,96},{1... | collective-permute-start | bytes 776 | tf_op jit(solution)/shard_map/ppermute | solution.py:17
  84.3 3.8 %collective-permute-start.13 = (f32[8,8]{0,1:T(8,128)S(1)}, f32[8,8]{0,1:T(8,128)S(1)}, u32[]{:S(2)}, u32[]{:S(2)}) collective-permute-start(f32[8,8]{0,1:T(8,128)S(1)} %add.39), channel_id=1, source_target_pairs={{0,32},{16,48},{32,0},{48,16},{64,96},{80,112},{96,64},{112,80},{1... | collective-permute-start | bytes 776 | tf_op jit(solution)/shard_map/ppermute | solution.py:17
  88.1 7.2 %collective-permute-start.14 = (f32[8,8]{0,1:T(8,128)S(1)}, f32[8,8]{0,1:T(8,128)S(1)}, u32[]{:S(2)}, u32[]{:S(2)}) collective-permute-start(f32[8,8]{0,1:T(8,128)S(1)} %add.40), channel_id=1, source_target_pairs={{0,64},{16,80},{32,96},{48,112},{64,0},{80,16},{96,32},{112,48},{1... | collective-permute-start | bytes 776 | tf_op jit(solution)/shard_map/ppermute | solution.py:17
  95.3 8.6 %collective-permute-start.15 = (f32[8,8]{0,1:T(8,128)S(1)}, f32[8,8]{0,1:T(8,128)S(1)}, u32[]{:S(2)}, u32[]{:S(2)}) collective-permute-start(f32[8,8]{0,1:T(8,128)S(1)} %add.41), channel_id=1, source_target_pairs={{0,128},{16,144},{32,160},{48,176},{64,192},{80,208},{96,224},{112... | collective-permute-start | bytes 776 | tf_op jit(solution)/shard_map/ppermute | solution.py:17

commit v7 on v6

--- a/solution.py
+++ b/solution.py
@@ -1,3 +1,5 @@
+import functools
+
 import jax
 import jax.numpy as jnp
 from jax import lax
@@ -113,11 +115,19 @@
         send_packed(pack_ref, g_ref)
 
 
-def stage_two(f_ref, first_ref, mid_ref, vel_ref, visc_ref, snd_ref, coup_ref, hw_ref, he_ref, gb_ref, ga_ref,
-              resp_ref, gram_ref, below_ref, above_ref):
+def stage_two(c0, nprev, f_ref, first_ref, mid_ref, vel_ref, visc_ref, snd_ref, coup_ref, hw_ref, he_ref, gb_ref,
+              ga_ref, *rest):
+    prev_refs = rest[:nprev]
+    resp_ref, gram_ref, below_ref, above_ref = rest[nprev:]
     c = pl.program_id(0)
     ncol = resp_ref.shape[1]
+    total_cols = int(round(gram_ref.shape[0] ** 0.5))
     nx, ny = f_ref.shape[2], f_ref.shape[3]
+
+    @pl.when(c == 0)
+    def _():
+        gram_ref[...] = jnp.zeros_like(gram_ref)
+
     receive(c, gb_ref, ga_ref, below_ref, above_ref, ny)
     q = [mid_ref[v, 0] for v in range(NV)]
     west = [hw_ref[0, v:v + 1, :] for v in range(NV)]
@@ -130,20 +140,30 @@
         r = forcing + 0.5 * STEP * (first_ref[v, 0] + second)
         resp_ref[v, pl.ds(c, 1)] = r[None]
         resp.append(r)
+    me = c0 + c
+
+    def put(other, field_of):
+        acc = None
+        for v in range(NV):
+            prod = (field_of(v) * resp[v]).reshape(nx // 8, 8, ny).sum(axis=0)
+            acc = prod if acc is None else acc + prod
+        row = jnp.sum(acc, axis=0, keepdims=True)
+        gram_ref[pl.ds(me * total_cols + other, 1), :] = row
+        gram_ref[pl.ds(other * total_cols + me, 1), :] = row
+
+    base = 0
+    for ref in prev_refs:
+        for d in range(ref.shape[1]):
+            put(base + d, lambda v, ref=ref, d=d: ref[v, d])
+        base += ref.shape[1]
     for d in range(ncol):
         @pl.when(d <= c)
         def _():
-            acc = None
-            for v in range(NV):
-                prod = (resp_ref[v, d] * resp[v]).reshape(nx // 8, 8, ny).sum(axis=0)
-                acc = prod if acc is None else acc + prod
-            row = jnp.sum(acc, axis=0, keepdims=True)
-            gram_ref[pl.ds(c * ncol + d, 1), :] = row
-            gram_ref[pl.ds(d * ncol + c, 1), :] = row
+            put(c0 + d, lambda v: resp_ref[v, d])
 
 
 def edges(f_ref, w_ref, e_ref, g_ref, pack_ref):
-    ncol, nx = f_ref.shape[1], f_ref.shape[2]
+    ncol, nx = w_ref.shape[0], f_ref.shape[2]
     for c in range(ncol):
         fields = [f_ref[v, c] for v in range(NV)]
         for v in range(NV):
@@ -153,9 +173,10 @@
     send_packed(pack_ref, g_ref)
 
 
-def combine(inv_ref, r_ref, out_ref):
-    ncol = r_ref.shape[1]
-    rs = [r_ref[0, d] for d in range(ncol)]
+def combine(inv_ref, *refs):
+    out_ref = refs[-1]
+    rs = [r_ref[0, d] for r_ref in refs[:-1] for d in range(r_ref.shape[1])]
+    ncol = len(rs)
     for c in range(ncol):
         acc = inv_ref[c, 0] * rs[0]
         for d in range(1, ncol):
@@ -165,67 +186,69 @@
 
 def local(forcing, velocity, viscosity, sound, coupling):
     nv, ncol, nx, ny = forcing.shape
+    groups = 2
+    size = ncol // groups
     f32 = jnp.float32
     whole = lambda shape: pl.BlockSpec(shape, lambda c: (0,) * len(shape))
-    column = pl.BlockSpec((nv, 1, nx, ny), lambda c: (0, c, 0, 0))
-    edge_x = pl.BlockSpec((1, nv, ny), lambda c: (c, 0, 0))
     coef_specs = [whole((2, nx, ny)), whole((nx, ny)), whole((nx, ny)), whole((nv, nv, nx, ny))]
     params = pltpu.CompilerParams(vmem_limit_bytes=60 * 1024 * 1024)
-
-    width = 2 * nv * ncol
+    width = 2 * nv * size
     packed = whole((width, nx))
     packed_shape = jax.ShapeDtypeStruct((width, nx), f32)
     tile = pltpu.VMEM((nx, ny), f32)
-    fw, fe, fg = pl.pallas_call(
-        edges,
-        in_specs=[pl.BlockSpec(memory_space=pltpu.VMEM)],
-        out_specs=[pl.BlockSpec(memory_space=pltpu.VMEM)] * 3,
-        out_shape=[
-            jax.ShapeDtypeStruct((ncol, nv, ny), f32),
-            jax.ShapeDtypeStruct((ncol, nv, ny), f32),
-            packed_shape,
-        ],
-        scratch_shapes=[tile],
-        compiler_params=params,
-    )(forcing)
-    hw, he = exchange(fw, fe, "gx")
-    gb, ga = exchange(fg, fg, "gy")
-
-    first, middle, mw, me, mg = pl.pallas_call(
-        stage_one,
-        grid=(ncol,),
-        in_specs=[column] + coef_specs + [edge_x, edge_x, packed, packed],
-        out_specs=[column, column, edge_x, edge_x, packed],
-        out_shape=[
-            jax.ShapeDtypeStruct(forcing.shape, f32),
-            jax.ShapeDtypeStruct(forcing.shape, f32),
-            jax.ShapeDtypeStruct((ncol, nv, ny), f32),
-            jax.ShapeDtypeStruct((ncol, nv, ny), f32),
-            packed_shape,
-        ],
-        scratch_shapes=[tile, tile, tile],
-        compiler_params=params,
-    )(forcing, velocity, viscosity, sound, coupling, hw, he, gb, ga)
-
-    hw2, he2 = exchange(mw, me, "gx")
-    gb2, ga2 = exchange(mg, mg, "gy")
-
-    response, partial = pl.pallas_call(
-        stage_two,
-        grid=(ncol,),
-        in_specs=[column, column, column] + coef_specs + [edge_x, edge_x, packed, packed],
-        out_specs=[whole(forcing.shape), whole((ncol * ncol, ny))],
-        out_shape=[
-            jax.ShapeDtypeStruct(forcing.shape, f32),
-            jax.ShapeDtypeStruct((ncol * ncol, ny), f32),
-        ],
-        compiler_params=pltpu.CompilerParams(
-            vmem_limit_bytes=60 * 1024 * 1024, dimension_semantics=("arbitrary",)
-        ),
-        scratch_shapes=[tile, tile],
-    )(forcing, first, middle, velocity, viscosity, sound, coupling, hw2, he2, gb2, ga2)
+    edge_x = pl.BlockSpec((1, nv, ny), lambda c: (c, 0, 0))
+    local_col = pl.BlockSpec((nv, 1, nx, ny), lambda c: (0, c, 0, 0))
+    group_shape = jax.ShapeDtypeStruct((nv, size, nx, ny), f32)
+    edge_shape = jax.ShapeDtypeStruct((size, nv, ny), f32)
+
+    responses, partials = [], []
+    for g in range(groups):
+        c0 = g * size
+        global_col = pl.BlockSpec((nv, 1, nx, ny), lambda c, c0=c0: (0, c + c0, 0, 0))
+        fw, fe, fg = pl.pallas_call(
+            edges,
+            grid=(1,),
+            in_specs=[pl.BlockSpec((nv, size, nx, ny), lambda i, g=g: (0, g, 0, 0))],
+            out_specs=[whole((size, nv, ny)), whole((size, nv, ny)), packed],
+            out_shape=[edge_shape, edge_shape, packed_shape],
+            scratch_shapes=[tile],
+            compiler_params=params,
+        )(forcing)
+        hw, he = exchange(fw, fe, "gx")
+        gb, ga = exchange(fg, fg, "gy")
+
+        first, middle, mw, me, mg = pl.pallas_call(
+            stage_one,
+            grid=(size,),
+            in_specs=[global_col] + coef_specs + [edge_x, edge_x, packed, packed],
+            out_specs=[local_col, local_col, edge_x, edge_x, packed],
+            out_shape=[group_shape, group_shape, edge_shape, edge_shape, packed_shape],
+            scratch_shapes=[tile, tile, tile],
+            compiler_params=params,
+        )(forcing, velocity, viscosity, sound, coupling, hw, he, gb, ga)
+
+        hw2, he2 = exchange(mw, me, "gx")
+        gb2, ga2 = exchange(mg, mg, "gy")
+
+        response, partial = pl.pallas_call(
+            functools.partial(stage_two, c0, len(responses)),
+            grid=(size,),
+            in_specs=[global_col, local_col, local_col] + coef_specs + [edge_x, edge_x, packed, packed]
+            + [whole((nv, size, nx, ny))] * len(responses),
+            out_specs=[whole((nv, size, nx, ny)), whole((ncol * ncol, ny))],
+            out_shape=[group_shape, jax.ShapeDtypeStruct((ncol * ncol, ny), f32)],
+            compiler_params=pltpu.CompilerParams(
+                vmem_limit_bytes=60 * 1024 * 1024, dimension_semantics=("arbitrary",)
+            ),
+            scratch_shapes=[tile, tile],
+        )(forcing, first, middle, velocity, viscosity, sound, coupling, hw2, he2, gb2, ga2, *responses)
+        responses.append(response)
+        partials.append(partial)
 
     rows_total = float(nv * nx * ny * lax.axis_size("gx") * lax.axis_size("gy"))
+    partial = partials[0]
+    for more in partials[1:]:
+        partial = partial + more
     local_gram = jnp.sum(partial, axis=1).reshape(ncol, ncol) / rows_total
     lower = jnp.linalg.cholesky(all_sum(local_gram))
     identity = jnp.eye(lower.shape[0], dtype=lower.dtype)
@@ -234,14 +257,12 @@
     basis = pl.pallas_call(
         combine,
         grid=(nv,),
-        in_specs=[
-            pl.BlockSpec(memory_space=pltpu.SMEM),
-            pl.BlockSpec((1, ncol, nx, ny), lambda v: (v, 0, 0, 0)),
-        ],
+        in_specs=[pl.BlockSpec(memory_space=pltpu.SMEM)]
+        + [pl.BlockSpec((1, size, nx, ny), lambda v: (v, 0, 0, 0))] * groups,
         out_specs=pl.BlockSpec((1, ncol, nx, ny), lambda v: (v, 0, 0, 0)),
         out_shape=jax.ShapeDtypeStruct(forcing.shape, f32),
         compiler_params=params,
-    )(inverse, response)
+    )(inverse, *responses)
     return (basis, lower.T)
 
 

time: 116 us -> 157 us (1.35)
  starting transfers between devices: 44 us -> 72.8 us
  Pallas kernels: 38.9 us -> 46.5 us
  waiting for transfers between devices: 23.1 us -> 26.1 us
    ppermute x4 -> x8, starting transfers between devices: 13.5 us -> 28.4 us  [exchange(): from_above = lax.ppermute(low, axis, [(i + 1, i) for i in range(count - 1)])]
    ppermute x4 -> x8, starting transfers between devices: 9.4 us -> 20.8 us  [exchange(): lax.ppermute(high, axis, [(i, i + 1) for i in range(count - 1)])]
    pallas_call x3 -> x6, Pallas kernels: 33.1 us -> 40.8 us  [the longest x2 17.9 us: local(): pl.pallas_call(functools.partial(stage_two, c0, len(responses)), grid=(si...]
    ppermute x8, starting transfers between devices: 21.1 us -> 23.6 us  [all_sum(): lax.ppermute(value, axis, [(i, i ^ bit) for i in range(count)])]
    ppermute x4 -> x8, waiting for transfers between devices: 0.01 us -> 1.64 us  [exchange(): lax.ppermute(high, axis, [(i, i + 1) for i in range(count - 1)])]
    ppermute x4 -> x8, waiting for transfers between devices: 5.92 us -> 7.51 us  [exchange(): from_above = lax.ppermute(low, axis, [(i + 1, i) for i in range(count - 1)])]
    unnamed x17 -> x43, local copies, waits for them, and re-layouts: 2.53 us -> 3.66 us
  transfers between devices with their start and end apart: 16 -> 24, of which waited for: 10 -> 12; matrix products, arithmetic and copies ran while one was open for 0% -> 0% of each run, Pallas kernels for 0% -> 18%
where the time goes in v7:
time: 157 us; the launch traced here: 155 us
  starting transfers between devices  72.8 us (46%)
  Pallas kernels  46.5 us (30%)
  waiting for transfers between devices  26.1 us (17%)
  local copies, waits for them, and re-layouts  3.88 us (2%)
  other arithmetic  3.56 us (2%)
    ppermute x8, starting transfers between devices, exchange(): from_above = lax.ppermute(low, axis, [(i + 1, i) for i in range(count - 1)])  28.4 us
    ppermute x8, starting transfers between devices, all_sum(): lax.ppermute(value, axis, [(i, i ^ bit) for i in range(count)])  23.6 us
    ppermute x8, starting transfers between devices, exchange(): lax.ppermute(high, axis, [(i, i + 1) for i in range(count - 1)])  20.8 us
    pallas_call x2, Pallas kernels, local(): pl.pallas_call(functools.partial(stage_two, c0, len(responses)), grid=(si...  17.9 us
    ppermute x8, waiting for transfers between devices, all_sum(): lax.ppermute(value, axis, [(i, i ^ bit) for i in range(count)])  16.9 us
    pallas_call x2, Pallas kernels, local(): pl.pallas_call(stage_one, grid=(size,), in_specs=[global_col] + coef_spec...  16 us
    ppermute x8, waiting for transfers between devices, exchange(): from_above = lax.ppermute(low, axis, [(i + 1, i) for i in range(count - 1)])  7.51 us
    pallas_call x2, Pallas kernels, local(): pl.pallas_call(edges, grid=(1,), in_specs=[pl.BlockSpec((nv, size, nx, ny...  6.93 us
  transfers between devices with their start and end apart: 24, of which 12 were waited for; matrix products, arithmetic and copies ran while one was open for 0% of the time, Pallas kernels for 18%

profile of v7, /device:TPU:2, one launch (start us, length us, event | category | flops | bytes accessed | tf_op | source)
XLA Modules:
  0.0 154.7 jit_solution(8829922185928413612)
XLA Ops:
  0.6 3.5 %shard_map.68 = (f32[4,4,128]{2,1,0:T(4,128)}, f32[4,4,128]{2,1,0:T(4,128)}, f32[32,256]{1,0:T(8,128)}) custom-call(f32[4,8,256,128]{3,2,1,0:T(8,128)} %f_ref.11), custom_call_target="tpu_custom_call" | custom-call | tf_op jit(solution)/shard_map/pallas_call | solution.py:208
  4.1 5.0 %collective-permute-start.3 = (f32[32,256]{1,0:T(8,128)}, f32[32,256]{1,0:T(8,128)S(1)}, u32[]{:S(2)}, u32[]{:S(2)}) collective-permute-start(f32[32,256]{1,0:T(8,128)} %get-tuple-element.24), channel_id=1, source_target_pairs={{1,0},{2,1},{3,2},{4,3},{5,4},{6,5},{7,6},{8,7},{9,8},{10,9},{11,1... | collective-permute-start | bytes 98312 | tf_op jit(solution)/shard_map/ppermute | solution.py:27
  11.0 3.5 %shard_map.71 = (f32[4,4,128]{2,1,0:T(4,128)}, f32[4,4,128]{2,1,0:T(4,128)}, f32[32,256]{1,0:T(8,128)}) custom-call(f32[4,8,256,128]{3,2,1,0:T(8,128)} %f_ref.11), custom_call_target="tpu_custom_call" | custom-call | tf_op jit(solution)/shard_map/pallas_call | solution.py:208
  14.5 6.0 %collective-permute-start.11 = (f32[32,256]{1,0:T(8,128)}, f32[32,256]{1,0:T(8,128)S(1)}, u32[]{:S(2)}, u32[]{:S(2)}) collective-permute-start(f32[32,256]{1,0:T(8,128)} %get-tuple-element.33), channel_id=1, source_target_pairs={{1,0},{2,1},{3,2},{4,3},{5,4},{6,5},{7,6},{8,7},{9,8},{10,9},{11,1... | collective-permute-start | bytes 98312 | tf_op jit(solution)/shard_map/ppermute | solution.py:27
  25.9 3.9 %collective-permute-done.1.he_ref = f32[4,4,128]{2,1,0:T(4,128)S(1)} collective-permute-done((f32[4,4,128]{2,1,0:T(4,128)S(1)}, f32[4,4,128]{2,1,0:T(4,128)S(1)}, u32[]{:S(2)}, u32[]{:S(2)}) %collective-permute-start.1) | collective-permute-done | bytes 8224 | tf_op jit(solution)/shard_map/ppermute | solution.py:27
  29.8 4.8 %collective-permute-start.8 = (f32[4,4,128]{2,1,0:T(4,128)}, f32[4,4,128]{2,1,0:T(4,128)S(1)}, u32[]{:S(2)}, u32[]{:S(2)}) collective-permute-start(f32[4,4,128]{2,1,0:T(4,128)} %get-tuple-element.31), channel_id=1, source_target_pairs={{0,16},{16,32},{32,48},{48,64},{64,80},{80,96},{96,112},{112,128},... | collective-permute-start | bytes 24584 | tf_op jit(solution)/shard_map/ppermute | solution.py:26
  36.6 7.9 %shard_map.69 = (f32[4,4,256,128]{3,2,1,0:T(8,128)}, f32[4,4,256,128]{3,2,1,0:T(8,128)}, f32[4,4,128]{2,1,0:T(4,128)}, f32[4,4,128]{2,1,0:T(4,128)}, f32[32,256]{1,0:T(8,128)}) custom-call(f32[4,8,256,128]{3,2,1,0:T(8,128)} %f_ref.11, f32[2,256,128]{2,1,0:T(8,128)} %vel_ref.7, f32[256,128]{1,0:T(8,128)} %visc_ref.7, f32[256,128]{1,0:T(8,128)} %snd_ref.7, ...), custom_call_target="tpu_custom_call" | custom-call | tf_op jit(solution)/shard_map/pallas_call | solution.py:220
  44.5 6.2 %collective-permute-start.7 = (f32[32,256]{1,0:T(8,128)}, f32[32,256]{1,0:T(8,128)S(1)}, u32[]{:S(2)}, u32[]{:S(2)}) collective-permute-start(f32[32,256]{1,0:T(8,128)} %get-tuple-element.29), channel_id=1, source_target_pairs={{1,0},{2,1},{3,2},{4,3},{5,4},{6,5},{7,6},{8,7},{9,8},{10,9},{11,1... | collective-permute-start | bytes 98312 | tf_op jit(solution)/shard_map/ppermute | solution.py:27
  53.9 8.1 %shard_map.72 = (f32[4,4,256,128]{3,2,1,0:T(8,128)}, f32[4,4,256,128]{3,2,1,0:T(8,128)}, f32[4,4,128]{2,1,0:T(4,128)}, f32[4,4,128]{2,1,0:T(4,128)}, f32[32,256]{1,0:T(8,128)}) custom-call(f32[4,8,256,128]{3,2,1,0:T(8,128)} %f_ref.11, f32[2,256,128]{2,1,0:T(8,128)} %vel_ref.7, f32[256,128]{1,0:T(8,128)} %visc_ref.7, f32[256,128]{1,0:T(8,128)} %snd_ref.7, ...), custom_call_target="tpu_custom_call" | custom-call | tf_op jit(solution)/shard_map/pallas_call | solution.py:220
  61.9 6.0 %collective-permute-start.15 = (f32[32,256]{1,0:T(8,128)}, f32[32,256]{1,0:T(8,128)S(1)}, u32[]{:S(2)}, u32[]{:S(2)}) collective-permute-start(f32[32,256]{1,0:T(8,128)} %get-tuple-element.38), channel_id=1, source_target_pairs={{1,0},{2,1},{3,2},{4,3},{5,4},{6,5},{7,6},{8,7},{9,8},{10,9},{11,1... | collective-permute-start | bytes 98312 | tf_op jit(solution)/shard_map/ppermute | solution.py:27
  69.9 2.2 %collective-permute-start.4 = (f32[4,4,128]{2,1,0:T(4,128)S(1)}, f32[4,4,128]{2,1,0:T(4,128)S(1)}, u32[]{:S(2)}, u32[]{:S(2)}) collective-permute-start(f32[4,4,128]{2,1,0:T(4,128)S(1)} %copy-done.18), channel_id=1, source_target_pairs={{0,16},{16,32},{32,48},{48,64},{64,80},{80,96},{96,112},{112,128},... | collective-permute-start | bytes 24584 | tf_op jit(solution)/shard_map/ppermute | solution.py:26
  74.2 3.6 %collective-permute-done.5.he_ref = f32[4,4,128]{2,1,0:T(4,128)S(1)} collective-permute-done((f32[4,4,128]{2,1,0:T(4,128)S(1)}, f32[4,4,128]{2,1,0:T(4,128)S(1)}, u32[]{:S(2)}, u32[]{:S(2)}) %collective-permute-start.5) | collective-permute-done | bytes 8224 | tf_op jit(solution)/shard_map/ppermute | solution.py:27
  77.8 4.8 %collective-permute-start.12 = (f32[4,4,128]{2,1,0:T(4,128)}, f32[4,4,128]{2,1,0:T(4,128)S(1)}, u32[]{:S(2)}, u32[]{:S(2)}) collective-permute-start(f32[4,4,128]{2,1,0:T(4,128)} %get-tuple-element.36), channel_id=1, source_target_pairs={{0,16},{16,32},{32,48},{48,64},{64,80},{80,96},{96,112},{112,128},... | collective-permute-start | bytes 24584 | tf_op jit(solution)/shard_map/ppermute | solution.py:26
  84.6 8.4 %shard_map.70 = (f32[4,4,256,128]{3,2,1,0:T(8,128)}, f32[64,128]{1,0:T(8,128)}) custom-call(f32[4,8,256,128]{3,2,1,0:T(8,128)} %f_ref.11, f32[4,4,256,128]{3,2,1,0:T(8,128)} %get-tuple-element.25.first_ref, f32[4,4,256,128]{3,2,1,0:T(8,128)} %get-tuple-element.26.mid_ref, f32[2,256,128]{2,1,0:T(8,128)} %vel_ref.7, f32[256,128]{1,0:T(8,128)} %visc_ref.7, ...), custom_call_target="tpu_custom_call" | custom-call | tf_op jit(solution)/shard_map/pallas_call | solution.py:233
  93.7 9.5 %shard_map.73 = (f32[4,4,256,128]{3,2,1,0:T(8,128)}, f32[64,128]{1,0:T(8,128)}) custom-call(f32[4,8,256,128]{3,2,1,0:T(8,128)} %f_ref.11, f32[4,4,256,128]{3,2,1,0:T(8,128)} %get-tuple-element.34.first_ref, f32[4,4,256,128]{3,2,1,0:T(8,128)} %get-tuple-element.35.mid_ref, f32[2,256,128]{2,1,0:T(8,128)} %vel_ref.7, f32[256,128]{1,0:T(8,128)} %visc_ref.7, ...), custom_call_target="tpu_custom_call" | custom-call | tf_op jit(solution)/shard_map/pallas_call | solution.py:233
  104.2 3.6 %collective-permute-done.16 = f32[8,8]{0,1:T(8,128)S(1)} collective-permute-done((f32[8,8]{0,1:T(8,128)S(1)}, f32[8,8]{0,1:T(8,128)S(1)}, u32[]{:S(2)}, u32[]{:S(2)}) %collective-permute-start.16) | collective-permute-done | bytes 288 | tf_op jit(solution)/shard_map/ppermute | solution.py:19
  107.8 3.6 %collective-permute-start.17 = (f32[8,8]{0,1:T(8,128)S(1)}, f32[8,8]{0,1:T(8,128)S(1)}, u32[]{:S(2)}, u32[]{:S(2)}) collective-permute-start(f32[8,8]{0,1:T(8,128)S(1)} %add.39), channel_id=1, source_target_pairs={{0,2},{1,3},{2,0},{3,1},{4,6},{5,7},{6,4},{7,5},{8,10},{9,11},{10,... | collective-permute-start | bytes 776 | tf_op jit(solution)/shard_map/ppermute | solution.py:19
  113.6 3.1 %collective-permute-done.18 = f32[8,8]{0,1:T(8,128)S(1)} collective-permute-done((f32[8,8]{0,1:T(8,128)S(1)}, f32[8,8]{0,1:T(8,128)S(1)}, u32[]{:S(2)}, u32[]{:S(2)}) %collective-permute-start.18) | collective-permute-done | bytes 288 | tf_op jit(solution)/shard_map/ppermute | solution.py:19
  116.6 2.4 %collective-permute-start.19 = (f32[8,8]{0,1:T(8,128)S(1)}, f32[8,8]{0,1:T(8,128)S(1)}, u32[]{:S(2)}, u32[]{:S(2)}) collective-permute-start(f32[8,8]{0,1:T(8,128)S(1)} %add.41), channel_id=1, source_target_pairs={{0,8},{1,9},{2,10},{3,11},{4,12},{5,13},{6,14},{7,15},{8,0},{9,1},... | collective-permute-start | bytes 776 | tf_op jit(solution)/shard_map/ppermute | solution.py:19
  119.0 2.8 %collective-permute-done.19 = f32[8,8]{0,1:T(8,128)S(1)} collective-permute-done((f32[8,8]{0,1:T(8,128)S(1)}, f32[8,8]{0,1:T(8,128)S(1)}, u32[]{:S(2)}, u32[]{:S(2)}) %collective-permute-start.19) | collective-permute-done | bytes 288 | tf_op jit(solution)/shard_map/ppermute | solution.py:19
  122.9 2.5 %collective-permute-start.21 = (f32[8,8]{0,1:T(8,128)S(1)}, f32[8,8]{0,1:T(8,128)S(1)}, u32[]{:S(2)}, u32[]{:S(2)}) collective-permute-start(f32[8,8]{0,1:T(8,128)S(1)} %add.43), channel_id=1, source_target_pairs={{0,32},{16,48},{32,0},{48,16},{64,96},{80,112},{96,64},{112,80},{1... | collective-permute-start | bytes 776 | tf_op jit(solution)/shard_map/ppermute | solution.py:19
  127.1 7.9 %collective-permute-start.22 = (f32[8,8]{0,1:T(8,128)S(1)}, f32[8,8]{0,1:T(8,128)S(1)}, u32[]{:S(2)}, u32[]{:S(2)}) collective-permute-start(f32[8,8]{0,1:T(8,128)S(1)} %add.44), channel_id=1, source_target_pairs={{0,64},{16,80},{32,96},{48,112},{64,0},{80,16},{96,32},{112,48},{1... | collective-permute-start | bytes 776 | tf_op jit(solution)/shard_map/ppermute | solution.py:19
  136.5 6.7 %collective-permute-start.23 = (f32[8,8]{0,1:T(8,128)S(1)}, f32[8,8]{0,1:T(8,128)S(1)}, u32[]{:S(2)}, u32[]{:S(2)}) collective-permute-start(f32[8,8]{0,1:T(8,128)S(1)} %add.45), channel_id=1, source_target_pairs={{0,128},{16,144},{32,160},{48,176},{64,192},{80,208},{96,224},{112... | collective-permute-start | bytes 776 | tf_op jit(solution)/shard_map/ppermute | solution.py:19
  149.0 5.7 %shard_map.74 = f32[4,8,256,128]{3,2,1,0:T(8,128)} custom-call(f32[8,8]{1,0:T(8,128)} %fusion.inv_ref, f32[4,4,256,128]{3,2,1,0:T(8,128)} %get-tuple-element.39.rest_0_.refs_0_, f32[4,4,256,128]{3,2,1,0:T(8,128)} %get-tuple-element.41.refs_1_), custom_call_target="tpu_custom_call" | custom-call | tf_op jit(solution)/shard_map/pallas_call | solution.py:257
  (94 shorter events, 32.0 us)
Async XLA Ops:
  4.1 30.5 %collective-permute-start.3 = (f32[32,256]{1,0:T(8,128)}, f32[32,256]{1,0:T(8,128)S(1)}, u32[]{:S(2)}, u32[]{:S(2)}) collective-permute-start(f32[32,256]{1,0:T(8,128)} %get-tuple-element.24), channel_id=1, source_target_pairs={{1,0},{2,1},{3,2},{4,3},{5,4},{6,5},{7,6},{8,7},{9,8},{10,9},{11,1... | collective-permute-start | bytes 98312 | tf_op jit(solution)/shard_map/ppermute | solution.py:27
  9.1 26.8 %collective-permute-start.2 = (f32[32,256]{1,0:T(8,128)}, f32[32,256]{1,0:T(8,128)S(1)}, u32[]{:S(2)}, u32[]{:S(2)}) collective-permute-start(f32[32,256]{1,0:T(8,128)} %get-tuple-element.24), channel_id=1, source_target_pairs={{0,1},{1,2},{2,3},{3,4},{4,5},{5,6},{6,7},{7,8},{8,9},{9,10},{10,1... | collective-permute-start | bytes 98312 | tf_op jit(solution)/shard_map/ppermute | solution.py:26
  14.5 38.2 %collective-permute-start.11 = (f32[32,256]{1,0:T(8,128)}, f32[32,256]{1,0:T(8,128)S(1)}, u32[]{:S(2)}, u32[]{:S(2)}) collective-permute-start(f32[32,256]{1,0:T(8,128)} %get-tuple-element.33), channel_id=1, source_target_pairs={{1,0},{2,1},{3,2},{4,3},{5,4},{6,5},{7,6},{8,7},{9,8},{10,9},{11,1... | collective-permute-start | bytes 98312 | tf_op jit(solution)/shard_map/ppermute | solution.py:27
  20.5 32.1 %collective-permute-start.10 = (f32[32,256]{1,0:T(8,128)}, f32[32,256]{1,0:T(8,128)S(1)}, u32[]{:S(2)}, u32[]{:S(2)}) collective-permute-start(f32[32,256]{1,0:T(8,128)} %get-tuple-element.33), channel_id=1, source_target_pairs={{0,1},{1,2},{2,3},{3,4},{4,5},{5,6},{6,7},{7,8},{8,9},{9,10},{10,1... | collective-permute-start | bytes 98312 | tf_op jit(solution)/shard_map/ppermute | solution.py:26
  22.5 2.1 %collective-permute-start = (f32[4,4,128]{2,1,0:T(4,128)S(1)}, f32[4,4,128]{2,1,0:T(4,128)S(1)}, u32[]{:S(2)}, u32[]{:S(2)}) collective-permute-start(f32[4,4,128]{2,1,0:T(4,128)S(1)} %copy-done.20), channel_id=1, source_target_pairs={{0,16},{16,32},{32,48},{48,64},{64,80},{80,96},{96,112},{112,128},... | collective-permute-start | bytes 24584 | tf_op jit(solution)/shard_map/ppermute | solution.py:26
  24.6 5.2 %collective-permute-start.1 = (f32[4,4,128]{2,1,0:T(4,128)S(1)}, f32[4,4,128]{2,1,0:T(4,128)S(1)}, u32[]{:S(2)}, u32[]{:S(2)}) collective-permute-start(f32[4,4,128]{2,1,0:T(4,128)S(1)} %copy-done.19), channel_id=1, source_target_pairs={{16,0},{32,16},{48,32},{64,48},{80,64},{96,80},{112,96},{128,112},... | collective-permute-start | bytes 24584 | tf_op jit(solution)/shard_map/ppermute | solution.py:27
  29.8 20.9 %collective-permute-start.8 = (f32[4,4,128]{2,1,0:T(4,128)}, f32[4,4,128]{2,1,0:T(4,128)S(1)}, u32[]{:S(2)}, u32[]{:S(2)}) collective-permute-start(f32[4,4,128]{2,1,0:T(4,128)} %get-tuple-element.31), channel_id=1, source_target_pairs={{0,16},{16,32},{32,48},{48,64},{64,80},{80,96},{96,112},{112,128},... | collective-permute-start | bytes 24584 | tf_op jit(solution)/shard_map/ppermute | solution.py:26
  34.6 18.0 %collective-permute-start.9 = (f32[4,4,128]{2,1,0:T(4,128)}, f32[4,4,128]{2,1,0:T(4,128)S(1)}, u32[]{:S(2)}, u32[]{:S(2)}) collective-permute-start(f32[4,4,128]{2,1,0:T(4,128)} %get-tuple-element.32), channel_id=1, source_target_pairs={{16,0},{32,16},{48,32},{64,48},{80,64},{96,80},{112,96},{128,112},... | collective-permute-start | bytes 24584 | tf_op jit(solution)/shard_map/ppermute | solution.py:27
  44.5 38.2 %collective-permute-start.7 = (f32[32,256]{1,0:T(8,128)}, f32[32,256]{1,0:T(8,128)S(1)}, u32[]{:S(2)}, u32[]{:S(2)}) collective-permute-start(f32[32,256]{1,0:T(8,128)} %get-tuple-element.29), channel_id=1, source_target_pairs={{1,0},{2,1},{3,2},{4,3},{5,4},{6,5},{7,6},{8,7},{9,8},{10,9},{11,1... | collective-permute-start | bytes 98312 | tf_op jit(solution)/shard_map/ppermute | solution.py:27
  50.7 33.3 %collective-permute-start.6 = (f32[32,256]{1,0:T(8,128)}, f32[32,256]{1,0:T(8,128)S(1)}, u32[]{:S(2)}, u32[]{:S(2)}) collective-permute-start(f32[32,256]{1,0:T(8,128)} %get-tuple-element.29), channel_id=1, source_target_pairs={{0,1},{1,2},{2,3},{3,4},{4,5},{5,6},{6,7},{7,8},{8,9},{9,10},{10,1... | collective-permute-start | bytes 98312 | tf_op jit(solution)/shard_map/ppermute | solution.py:26
  61.9 31.1 %collective-permute-start.15 = (f32[32,256]{1,0:T(8,128)}, f32[32,256]{1,0:T(8,128)S(1)}, u32[]{:S(2)}, u32[]{:S(2)}) collective-permute-start(f32[32,256]{1,0:T(8,128)} %get-tuple-element.38), channel_id=1, source_target_pairs={{1,0},{2,1},{3,2},{4,3},{5,4},{6,5},{7,6},{8,7},{9,8},{10,9},{11,1... | collective-permute-start | bytes 98312 | tf_op jit(solution)/shard_map/ppermute | solution.py:27
  68.0 25.1 %collective-permute-start.14 = (f32[32,256]{1,0:T(8,128)}, f32[32,256]{1,0:T(8,128)S(1)}, u32[]{:S(2)}, u32[]{:S(2)}) collective-permute-start(f32[32,256]{1,0:T(8,128)} %get-tuple-element.38), channel_id=1, source_target_pairs={{0,1},{1,2},{2,3},{3,4},{4,5},{5,6},{6,7},{7,8},{8,9},{9,10},{10,1... | collective-permute-start | bytes 98312 | tf_op jit(solution)/shard_map/ppermute | solution.py:26
  69.9 3.0 %collective-permute-start.4 = (f32[4,4,128]{2,1,0:T(4,128)S(1)}, f32[4,4,128]{2,1,0:T(4,128)S(1)}, u32[]{:S(2)}, u32[]{:S(2)}) collective-permute-start(f32[4,4,128]{2,1,0:T(4,128)S(1)} %copy-done.18), channel_id=1, source_target_pairs={{0,16},{16,32},{32,48},{48,64},{64,80},{80,96},{96,112},{112,128},... | collective-permute-start | bytes 24584 | tf_op jit(solution)/shard_map/ppermute | solution.py:26
  72.9 4.9 %collective-permute-start.5 = (f32[4,4,128]{2,1,0:T(4,128)S(1)}, f32[4,4,128]{2,1,0:T(4,128)S(1)}, u32[]{:S(2)}, u32[]{:S(2)}) collective-permute-start(f32[4,4,128]{2,1,0:T(4,128)S(1)} %copy-done.17), channel_id=1, source_target_pairs={{16,0},{32,16},{48,32},{64,48},{80,64},{96,80},{112,96},{128,112},... | collective-permute-start | bytes 24584 | tf_op jit(solution)/shard_map/ppermute | solution.py:27
  77.8 15.2 %collective-permute-start.12 = (f32[4,4,128]{2,1,0:T(4,128)}, f32[4,4,128]{2,1,0:T(4,128)S(1)}, u32[]{:S(2)}, u32[]{:S(2)}) collective-permute-start(f32[4,4,128]{2,1,0:T(4,128)} %get-tuple-element.36), channel_id=1, source_target_pairs={{0,16},{16,32},{32,48},{48,64},{64,80},{80,96},{96,112},{112,128},... | collective-permute-start | bytes 24584 | tf_op jit(solution)/shard_map/ppermute | solution.py:26
  82.7 10.3 %collective-permute-start.13 = (f32[4,4,128]{2,1,0:T(4,128)}, f32[4,4,128]{2,1,0:T(4,128)S(1)}, u32[]{:S(2)}, u32[]{:S(2)}) collective-permute-start(f32[4,4,128]{2,1,0:T(4,128)} %get-tuple-element.37), channel_id=1, source_target_pairs={{16,0},{32,16},{48,32},{64,48},{80,64},{96,80},{112,96},{128,112},... | collective-permute-start | bytes 24584 | tf_op jit(solution)/shard_map/ppermute | solution.py:27
  104.2 3.6 %collective-permute-start.16 = (f32[8,8]{0,1:T(8,128)S(1)}, f32[8,8]{0,1:T(8,128)S(1)}, u32[]{:S(2)}, u32[]{:S(2)}) collective-permute-start(f32[8,8]{0,1:T(8,128)S(1)} %copy.8), channel_id=1, source_target_pairs={{0,1},{1,0},{2,3},{3,2},{4,5},{5,4},{6,7},{7,6},{8,9},{9,8},{10,11... | collective-permute-start | bytes 776 | tf_op jit(solution)/shard_map/ppermute | solution.py:19
  107.8 5.2 %collective-permute-start.17 = (f32[8,8]{0,1:T(8,128)S(1)}, f32[8,8]{0,1:T(8,128)S(1)}, u32[]{:S(2)}, u32[]{:S(2)}) collective-permute-start(f32[8,8]{0,1:T(8,128)S(1)} %add.39), channel_id=1, source_target_pairs={{0,2},{1,3},{2,0},{3,1},{4,6},{5,7},{6,4},{7,5},{8,10},{9,11},{10,... | collective-permute-start | bytes 776 | tf_op jit(solution)/shard_map/ppermute | solution.py:19
  113.0 3.6 %collective-permute-start.18 = (f32[8,8]{0,1:T(8,128)S(1)}, f32[8,8]{0,1:T(8,128)S(1)}, u32[]{:S(2)}, u32[]{:S(2)}) collective-permute-start(f32[8,8]{0,1:T(8,128)S(1)} %add.40), channel_id=1, source_target_pairs={{0,4},{1,5},{2,6},{3,7},{4,0},{5,1},{6,2},{7,3},{8,12},{9,13},{10,... | collective-permute-start | bytes 776 | tf_op jit(solution)/shard_map/ppermute | solution.py:19
  116.6 5.1 %collective-permute-start.19 = (f32[8,8]{0,1:T(8,128)S(1)}, f32[8,8]{0,1:T(8,128)S(1)}, u32[]{:S(2)}, u32[]{:S(2)}) collective-permute-start(f32[8,8]{0,1:T(8,128)S(1)} %add.41), channel_id=1, source_target_pairs={{0,8},{1,9},{2,10},{3,11},{4,12},{5,13},{6,14},{7,15},{8,0},{9,1},... | collective-permute-start | bytes 776 | tf_op jit(solution)/shard_map/ppermute | solution.py:19
  121.8 1.2 collective-permute-start.20
  122.9 4.1 %collective-permute-start.21 = (f32[8,8]{0,1:T(8,128)S(1)}, f32[8,8]{0,1:T(8,128)S(1)}, u32[]{:S(2)}, u32[]{:S(2)}) collective-permute-start(f32[8,8]{0,1:T(8,128)S(1)} %add.43), channel_id=1, source_target_pairs={{0,32},{16,48},{32,0},{48,16},{64,96},{80,112},{96,64},{112,80},{1... | collective-permute-start | bytes 776 | tf_op jit(solution)/shard_map/ppermute | solution.py:19
  127.1 9.4 %collective-permute-start.22 = (f32[8,8]{0,1:T(8,128)S(1)}, f32[8,8]{0,1:T(8,128)S(1)}, u32[]{:S(2)}, u32[]{:S(2)}) collective-permute-start(f32[8,8]{0,1:T(8,128)S(1)} %add.44), channel_id=1, source_target_pairs={{0,64},{16,80},{32,96},{48,112},{64,0},{80,16},{96,32},{112,48},{1... | collective-permute-start | bytes 776 | tf_op jit(solution)/shard_map/ppermute | solution.py:19
  136.5 8.3 %collective-permute-start.23 = (f32[8,8]{0,1:T(8,128)S(1)}, f32[8,8]{0,1:T(8,128)S(1)}, u32[]{:S(2)}, u32[]{:S(2)}) collective-permute-start(f32[8,8]{0,1:T(8,128)S(1)} %add.45), channel_id=1, source_target_pairs={{0,128},{16,144},{32,160},{48,176},{64,192},{80,208},{96,224},{112... | collective-permute-start | bytes 776 | tf_op jit(solution)/shard_map/ppermute | solution.py:19
  (21 other events, 147.2 us)

commit v8 on v6

--- a/solution.py
+++ b/solution.py
@@ -89,7 +89,7 @@
 
 
 def stage_one(f_ref, vel_ref, visc_ref, snd_ref, coup_ref, hw_ref, he_ref, gb_ref, ga_ref,
-              first_ref, mid_ref, mw_ref, me_ref, g_ref, below_ref, above_ref, pack_ref):
+              first_ref, mw_ref, me_ref, g_ref, below_ref, above_ref, pack_ref):
     c = pl.program_id(0)
     nx, ny = f_ref.shape[2], f_ref.shape[3]
     receive(c, gb_ref, ga_ref, below_ref, above_ref, ny)
@@ -102,7 +102,6 @@
         first = lq[v] + q[v]
         middle = q[v] + STEP * first
         first_ref[v, 0] = first
-        mid_ref[v, 0] = middle
         mw_ref[0, v:v + 1, :] = middle[0:1, :]
         me_ref[0, v:v + 1, :] = middle[nx - 1:nx, :]
         mids.append(middle)
@@ -113,13 +112,13 @@
         send_packed(pack_ref, g_ref)
 
 
-def stage_two(f_ref, first_ref, mid_ref, vel_ref, visc_ref, snd_ref, coup_ref, hw_ref, he_ref, gb_ref, ga_ref,
+def stage_two(f_ref, first_ref, vel_ref, visc_ref, snd_ref, coup_ref, hw_ref, he_ref, gb_ref, ga_ref,
               resp_ref, gram_ref, below_ref, above_ref):
     c = pl.program_id(0)
     ncol = resp_ref.shape[1]
     nx, ny = f_ref.shape[2], f_ref.shape[3]
     receive(c, gb_ref, ga_ref, below_ref, above_ref, ny)
-    q = [mid_ref[v, 0] for v in range(NV)]
+    q = [f_ref[v, 0] + STEP * first_ref[v, 0] for v in range(NV)]
     west = [hw_ref[0, v:v + 1, :] for v in range(NV)]
     east = [he_ref[0, v:v + 1, :] for v in range(NV)]
     lq = operator(q, west, east, below_ref, above_ref, c, vel_ref, visc_ref, snd_ref, coup_ref)
@@ -191,13 +190,12 @@
     hw, he = exchange(fw, fe, "gx")
     gb, ga = exchange(fg, fg, "gy")
 
-    first, middle, mw, me, mg = pl.pallas_call(
+    first, mw, me, mg = pl.pallas_call(
         stage_one,
         grid=(ncol,),
         in_specs=[column] + coef_specs + [edge_x, edge_x, packed, packed],
-        out_specs=[column, column, edge_x, edge_x, packed],
+        out_specs=[column, edge_x, edge_x, packed],
         out_shape=[
-            jax.ShapeDtypeStruct(forcing.shape, f32),
             jax.ShapeDtypeStruct(forcing.shape, f32),
             jax.ShapeDtypeStruct((ncol, nv, ny), f32),
             jax.ShapeDtypeStruct((ncol, nv, ny), f32),
@@ -213,7 +211,7 @@
     response, partial = pl.pallas_call(
         stage_two,
         grid=(ncol,),
-        in_specs=[column, column, column] + coef_specs + [edge_x, edge_x, packed, packed],
+        in_specs=[column, column] + coef_specs + [edge_x, edge_x, packed, packed],
         out_specs=[whole(forcing.shape), whole((ncol * ncol, ny))],
         out_shape=[
             jax.ShapeDtypeStruct(forcing.shape, f32),
@@ -223,7 +221,7 @@
             vmem_limit_bytes=60 * 1024 * 1024, dimension_semantics=("arbitrary",)
         ),
         scratch_shapes=[tile, tile],
-    )(forcing, first, middle, velocity, viscosity, sound, coupling, hw2, he2, gb2, ga2)
+    )(forcing, first, velocity, viscosity, sound, coupling, hw2, he2, gb2, ga2)
 
     rows_total = float(nv * nx * ny * lax.axis_size("gx") * lax.axis_size("gy"))
     local_gram = jnp.sum(partial, axis=1).reshape(ncol, ncol) / rows_total
@@ -233,12 +231,12 @@
 
     basis = pl.pallas_call(
         combine,
-        grid=(nv,),
+        grid=(nv, 2),
         in_specs=[
             pl.BlockSpec(memory_space=pltpu.SMEM),
-            pl.BlockSpec((1, ncol, nx, ny), lambda v: (v, 0, 0, 0)),
-        ],
-        out_specs=pl.BlockSpec((1, ncol, nx, ny), lambda v: (v, 0, 0, 0)),
+            pl.BlockSpec((1, ncol, nx // 2, ny), lambda v, h: (v, 0, h, 0)),
+        ],
+        out_specs=pl.BlockSpec((1, ncol, nx // 2, ny), lambda v, h: (v, 0, h, 0)),
         out_shape=jax.ShapeDtypeStruct(forcing.shape, f32),
         compiler_params=params,
     )(inverse, response)

time: 116 us -> 116 us (level)
  no operation moved by 1% of the time
where the time goes in v8:
time: 116 us; the launch traced here: 114 us
  starting transfers between devices  44 us (38%)
  Pallas kernels  39.2 us (34%)
  waiting for transfers between devices  23.1 us (20%)
  other arithmetic  3.56 us (3%)
  local copies, waits for them, and re-layouts  2.75 us (2%)
    ppermute x8, starting transfers between devices, all_sum(): lax.ppermute(value, axis, [(i, i ^ bit) for i in range(count)])  21.1 us
    ppermute x8, waiting for transfers between devices, all_sum(): lax.ppermute(value, axis, [(i, i ^ bit) for i in range(count)])  17.1 us
    pallas_call x1, Pallas kernels, local(): pl.pallas_call(stage_two, grid=(ncol,), in_specs=[column, column] + coef_...  14 us
    ppermute x4, starting transfers between devices, exchange(): from_above = lax.ppermute(low, axis, [(i + 1, i) for i in range(count - 1)])  13.5 us
    pallas_call x1, Pallas kernels, local(): pl.pallas_call(stage_one, grid=(ncol,), in_specs=[column] + coef_specs +...  12.3 us
    ppermute x4, starting transfers between devices, exchange(): lax.ppermute(high, axis, [(i, i + 1) for i in range(count - 1)])  9.4 us
    pallas_call x1, Pallas kernels, local(): pl.pallas_call(combine, grid=(nv, 2), in_specs=[pl.BlockSpec(memory_space...  7.5 us
    ppermute x4, waiting for transfers between devices, exchange(): from_above = lax.ppermute(low, axis, [(i + 1, i) for i in range(count - 1)])  5.92 us
  transfers between devices with their start and end apart: 16, of which 10 were waited for; matrix products, arithmetic and copies ran while one was open for 0% of the time, Pallas kernels for 0%

profile of v8, /device:TPU:2, one launch (start us, length us, event | category | flops | bytes accessed | tf_op | source)
XLA Modules:
  0.0 114.2 jit_solution(7044943887457016091)
XLA Ops:
  0.6 5.4 %shard_map.68 = (f32[8,4,128]{2,1,0:T(4,128)}, f32[8,4,128]{2,1,0:T(4,128)}, f32[64,256]{1,0:T(8,128)}) custom-call(f32[4,8,256,128]{3,2,1,0:T(8,128)} %f_ref.5), custom_call_target="tpu_custom_call" | custom-call | tf_op jit(solution)/shard_map/pallas_call | solution.py:178
  6.1 4.9 %collective-permute-start.3 = (f32[64,256]{1,0:T(8,128)}, f32[64,256]{1,0:T(8,128)S(1)}, u32[]{:S(2)}, u32[]{:S(2)}) collective-permute-start(f32[64,256]{1,0:T(8,128)} %get-tuple-element.13), channel_id=1, source_target_pairs={{1,0},{2,1},{3,2},{4,3},{5,4},{6,5},{7,6},{8,7},{9,8},{10,9},{11,1... | collective-permute-start | bytes 196616 | tf_op jit(solution)/shard_map/ppermute | solution.py:25
  10.9 1.9 %collective-permute-start.2 = (f32[64,256]{1,0:T(8,128)}, f32[64,256]{1,0:T(8,128)S(1)}, u32[]{:S(2)}, u32[]{:S(2)}) collective-permute-start(f32[64,256]{1,0:T(8,128)} %get-tuple-element.13), channel_id=1, source_target_pairs={{0,1},{1,2},{2,3},{3,4},{4,5},{5,6},{6,7},{7,8},{8,9},{9,10},{10,1... | collective-permute-start | bytes 196616 | tf_op jit(solution)/shard_map/ppermute | solution.py:24
  12.9 1.5 %collective-permute-start = (f32[8,4,128]{2,1,0:T(4,128)}, f32[8,4,128]{2,1,0:T(4,128)S(1)}, u32[]{:S(2)}, u32[]{:S(2)}) collective-permute-start(f32[8,4,128]{2,1,0:T(4,128)} %get-tuple-element.11), channel_id=1, source_target_pairs={{0,16},{16,32},{32,48},{48,64},{64,80},{80,96},{96,112},{112,128},... | collective-permute-start | bytes 49160 | tf_op jit(solution)/shard_map/ppermute | solution.py:24
  15.7 4.0 %collective-permute-done.1.he_ref = f32[8,4,128]{2,1,0:T(4,128)S(1)} collective-permute-done((f32[8,4,128]{2,1,0:T(4,128)}, f32[8,4,128]{2,1,0:T(4,128)S(1)}, u32[]{:S(2)}, u32[]{:S(2)}) %collective-permute-start.1) | collective-permute-done | bytes 16416 | tf_op jit(solution)/shard_map/ppermute | solution.py:25
  20.9 12.3 %shard_map.69 = (f32[4,8,256,128]{3,2,1,0:T(8,128)}, f32[8,4,128]{2,1,0:T(4,128)}, f32[8,4,128]{2,1,0:T(4,128)}, f32[64,256]{1,0:T(8,128)}) custom-call(f32[4,8,256,128]{3,2,1,0:T(8,128)} %f_ref.5, f32[2,256,128]{2,1,0:T(8,128)} %vel_ref.3, f32[256,128]{1,0:T(8,128)} %visc_ref.3, f32[256,128]{1,0:T(8,128)} %snd_ref.3, f32[4,4,256,128]{3,2,1,0:T(8,128)} %coup_ref.3, ...), custom_call_target="tpu_custom_call" | custom-call | tf_op jit(solution)/shard_map/pallas_call | solution.py:193
  33.2 6.0 %collective-permute-start.7 = (f32[64,256]{1,0:T(8,128)}, f32[64,256]{1,0:T(8,128)S(1)}, u32[]{:S(2)}, u32[]{:S(2)}) collective-permute-start(f32[64,256]{1,0:T(8,128)} %get-tuple-element.17), channel_id=1, source_target_pairs={{1,0},{2,1},{3,2},{4,3},{5,4},{6,5},{7,6},{8,7},{9,8},{10,9},{11,1... | collective-permute-start | bytes 196616 | tf_op jit(solution)/shard_map/ppermute | solution.py:25
  39.2 1.9 %collective-permute-start.6 = (f32[64,256]{1,0:T(8,128)}, f32[64,256]{1,0:T(8,128)S(1)}, u32[]{:S(2)}, u32[]{:S(2)}) collective-permute-start(f32[64,256]{1,0:T(8,128)} %get-tuple-element.17), channel_id=1, source_target_pairs={{0,1},{1,2},{2,3},{3,4},{4,5},{5,6},{6,7},{7,8},{8,9},{9,10},{10,1... | collective-permute-start | bytes 196616 | tf_op jit(solution)/shard_map/ppermute | solution.py:24
  41.1 4.1 %collective-permute-start.4 = (f32[8,4,128]{2,1,0:T(4,128)}, f32[8,4,128]{2,1,0:T(4,128)S(1)}, u32[]{:S(2)}, u32[]{:S(2)}) collective-permute-start(f32[8,4,128]{2,1,0:T(4,128)} %get-tuple-element.15), channel_id=1, source_target_pairs={{0,16},{16,32},{32,48},{48,64},{64,80},{80,96},{96,112},{112,128},... | collective-permute-start | bytes 49160 | tf_op jit(solution)/shard_map/ppermute | solution.py:24
  46.6 2.0 %collective-permute-done.5.he_ref = f32[8,4,128]{2,1,0:T(4,128)S(1)} collective-permute-done((f32[8,4,128]{2,1,0:T(4,128)}, f32[8,4,128]{2,1,0:T(4,128)S(1)}, u32[]{:S(2)}, u32[]{:S(2)}) %collective-permute-start.5) | collective-permute-done | bytes 16416 | tf_op jit(solution)/shard_map/ppermute | solution.py:25
  49.2 14.0 %shard_map.70 = (f32[4,8,256,128]{3,2,1,0:T(8,128)}, f32[64,128]{1,0:T(8,128)}) custom-call(f32[4,8,256,128]{3,2,1,0:T(8,128)} %f_ref.5, f32[4,8,256,128]{3,2,1,0:T(8,128)} %get-tuple-element.14.first_ref, f32[2,256,128]{2,1,0:T(8,128)} %vel_ref.3, f32[256,128]{1,0:T(8,128)} %visc_ref.3, f32[256,128]{1,0:T(8,128)} %snd_ref.3, f32[4,4,256,128]{3,2,1,0:T(8,128)} %coup_ref.3, ...), custom_call_target="tpu_custom_call" | custom-call | tf_op jit(solution)/shard_map/pallas_call | solution.py:211
  64.2 3.6 %collective-permute-done.8 = f32[8,8]{0,1:T(8,128)S(1)} collective-permute-done((f32[8,8]{0,1:T(8,128)S(1)}, f32[8,8]{0,1:T(8,128)S(1)}, u32[]{:S(2)}, u32[]{:S(2)}) %collective-permute-start.8) | collective-permute-done | bytes 288 | tf_op jit(solution)/shard_map/ppermute | solution.py:17
  67.8 3.4 %collective-permute-start.9 = (f32[8,8]{0,1:T(8,128)S(1)}, f32[8,8]{0,1:T(8,128)S(1)}, u32[]{:S(2)}, u32[]{:S(2)}) collective-permute-start(f32[8,8]{0,1:T(8,128)S(1)} %add.35), channel_id=1, source_target_pairs={{0,2},{1,3},{2,0},{3,1},{4,6},{5,7},{6,4},{7,5},{8,10},{9,11},{10,... | collective-permute-start | bytes 776 | tf_op jit(solution)/shard_map/ppermute | solution.py:17
  71.2 1.7 %collective-permute-done.9 = f32[8,8]{0,1:T(8,128)S(1)} collective-permute-done((f32[8,8]{0,1:T(8,128)S(1)}, f32[8,8]{0,1:T(8,128)S(1)}, u32[]{:S(2)}, u32[]{:S(2)}) %collective-permute-start.9) | collective-permute-done | bytes 288 | tf_op jit(solution)/shard_map/ppermute | solution.py:17
  73.3 3.2 %collective-permute-done.10 = f32[8,8]{0,1:T(8,128)S(1)} collective-permute-done((f32[8,8]{0,1:T(8,128)S(1)}, f32[8,8]{0,1:T(8,128)S(1)}, u32[]{:S(2)}, u32[]{:S(2)}) %collective-permute-start.10) | collective-permute-done | bytes 288 | tf_op jit(solution)/shard_map/ppermute | solution.py:17
  76.6 2.4 %collective-permute-start.11 = (f32[8,8]{0,1:T(8,128)S(1)}, f32[8,8]{0,1:T(8,128)S(1)}, u32[]{:S(2)}, u32[]{:S(2)}) collective-permute-start(f32[8,8]{0,1:T(8,128)S(1)} %add.37), channel_id=1, source_target_pairs={{0,8},{1,9},{2,10},{3,11},{4,12},{5,13},{6,14},{7,15},{8,0},{9,1},... | collective-permute-start | bytes 776 | tf_op jit(solution)/shard_map/ppermute | solution.py:17
  79.0 2.7 %collective-permute-done.11 = f32[8,8]{0,1:T(8,128)S(1)} collective-permute-done((f32[8,8]{0,1:T(8,128)S(1)}, f32[8,8]{0,1:T(8,128)S(1)}, u32[]{:S(2)}, u32[]{:S(2)}) %collective-permute-start.11) | collective-permute-done | bytes 288 | tf_op jit(solution)/shard_map/ppermute | solution.py:17
  82.8 2.3 %collective-permute-start.13 = (f32[8,8]{0,1:T(8,128)S(1)}, f32[8,8]{0,1:T(8,128)S(1)}, u32[]{:S(2)}, u32[]{:S(2)}) collective-permute-start(f32[8,8]{0,1:T(8,128)S(1)} %add.39), channel_id=1, source_target_pairs={{0,32},{16,48},{32,0},{48,16},{64,96},{80,112},{96,64},{112,80},{1... | collective-permute-start | bytes 776 | tf_op jit(solution)/shard_map/ppermute | solution.py:17
  85.1 1.6 %collective-permute-done.13 = f32[8,8]{0,1:T(8,128)S(1)} collective-permute-done((f32[8,8]{0,1:T(8,128)S(1)}, f32[8,8]{0,1:T(8,128)S(1)}, u32[]{:S(2)}, u32[]{:S(2)}) %collective-permute-start.13) | collective-permute-done | bytes 288 | tf_op jit(solution)/shard_map/ppermute | solution.py:17
  86.7 5.6 %collective-permute-start.14 = (f32[8,8]{0,1:T(8,128)S(1)}, f32[8,8]{0,1:T(8,128)S(1)}, u32[]{:S(2)}, u32[]{:S(2)}) collective-permute-start(f32[8,8]{0,1:T(8,128)S(1)} %add.40), channel_id=1, source_target_pairs={{0,64},{16,80},{32,96},{48,112},{64,0},{80,16},{96,32},{112,48},{1... | collective-permute-start | bytes 776 | tf_op jit(solution)/shard_map/ppermute | solution.py:17
  92.3 1.6 %collective-permute-done.14 = f32[8,8]{0,1:T(8,128)S(1)} collective-permute-done((f32[8,8]{0,1:T(8,128)S(1)}, f32[8,8]{0,1:T(8,128)S(1)}, u32[]{:S(2)}, u32[]{:S(2)}) %collective-permute-start.14) | collective-permute-done | bytes 288 | tf_op jit(solution)/shard_map/ppermute | solution.py:17
  93.9 7.0 %collective-permute-start.15 = (f32[8,8]{0,1:T(8,128)S(1)}, f32[8,8]{0,1:T(8,128)S(1)}, u32[]{:S(2)}, u32[]{:S(2)}) collective-permute-start(f32[8,8]{0,1:T(8,128)S(1)} %add.41), channel_id=1, source_target_pairs={{0,128},{16,144},{32,160},{48,176},{64,192},{80,208},{96,224},{112... | collective-permute-start | bytes 776 | tf_op jit(solution)/shard_map/ppermute | solution.py:17
  100.9 1.6 %collective-permute-done.15 = f32[8,8]{0,1:T(8,128)S(1)} collective-permute-done((f32[8,8]{0,1:T(8,128)S(1)}, f32[8,8]{0,1:T(8,128)S(1)}, u32[]{:S(2)}, u32[]{:S(2)}) %collective-permute-start.15) | collective-permute-done | bytes 288 | tf_op jit(solution)/shard_map/ppermute | solution.py:17
  106.7 7.5 %shard_map.71 = f32[4,8,256,128]{3,2,1,0:T(8,128)} custom-call(f32[8,8]{1,0:T(8,128)} %fusion.inv_ref, f32[4,8,256,128]{3,2,1,0:T(8,128)} %get-tuple-element.19.r_ref), custom_call_target="tpu_custom_call" | custom-call | tf_op jit(solution)/shard_map/pallas_call | solution.py:232
  (49 shorter events, 11.3 us)
Async XLA Ops:
  6.1 13.6 %collective-permute-start.3 = (f32[64,256]{1,0:T(8,128)}, f32[64,256]{1,0:T(8,128)S(1)}, u32[]{:S(2)}, u32[]{:S(2)}) collective-permute-start(f32[64,256]{1,0:T(8,128)} %get-tuple-element.13), channel_id=1, source_target_pairs={{1,0},{2,1},{3,2},{4,3},{5,4},{6,5},{7,6},{8,7},{9,8},{10,9},{11,1... | collective-permute-start | bytes 196616 | tf_op jit(solution)/shard_map/ppermute | solution.py:25
  10.9 8.7 %collective-permute-start.2 = (f32[64,256]{1,0:T(8,128)}, f32[64,256]{1,0:T(8,128)S(1)}, u32[]{:S(2)}, u32[]{:S(2)}) collective-permute-start(f32[64,256]{1,0:T(8,128)} %get-tuple-element.13), channel_id=1, source_target_pairs={{0,1},{1,2},{2,3},{3,4},{4,5},{5,6},{6,7},{7,8},{8,9},{9,10},{10,1... | collective-permute-start | bytes 196616 | tf_op jit(solution)/shard_map/ppermute | solution.py:24
  12.9 2.8 %collective-permute-start = (f32[8,4,128]{2,1,0:T(4,128)}, f32[8,4,128]{2,1,0:T(4,128)S(1)}, u32[]{:S(2)}, u32[]{:S(2)}) collective-permute-start(f32[8,4,128]{2,1,0:T(4,128)} %get-tuple-element.11), channel_id=1, source_target_pairs={{0,16},{16,32},{32,48},{48,64},{64,80},{80,96},{96,112},{112,128},... | collective-permute-start | bytes 49160 | tf_op jit(solution)/shard_map/ppermute | solution.py:24
  14.3 5.3 %collective-permute-start.1 = (f32[8,4,128]{2,1,0:T(4,128)}, f32[8,4,128]{2,1,0:T(4,128)S(1)}, u32[]{:S(2)}, u32[]{:S(2)}) collective-permute-start(f32[8,4,128]{2,1,0:T(4,128)} %get-tuple-element.12), channel_id=1, source_target_pairs={{16,0},{32,16},{48,32},{64,48},{80,64},{96,80},{112,96},{128,112},... | collective-permute-start | bytes 49160 | tf_op jit(solution)/shard_map/ppermute | solution.py:25
  15.7 4.0 %copy-start.4 = (f32[8,4,128]{2,1,0:T(4,128)}, f32[8,4,128]{2,1,0:T(4,128)S(1)}, u32[]{:S(2)}) copy-start(f32[8,4,128]{2,1,0:T(4,128)S(1)} %collective-permute-done.hw_ref) | copy-start | bytes 49156
  19.6 0.6 copy-start.6
  19.6 0.6 copy-start
  20.2 0.6 copy-start.2
  33.2 15.4 %collective-permute-start.7 = (f32[64,256]{1,0:T(8,128)}, f32[64,256]{1,0:T(8,128)S(1)}, u32[]{:S(2)}, u32[]{:S(2)}) collective-permute-start(f32[64,256]{1,0:T(8,128)} %get-tuple-element.17), channel_id=1, source_target_pairs={{1,0},{2,1},{3,2},{4,3},{5,4},{6,5},{7,6},{8,7},{9,8},{10,9},{11,1... | collective-permute-start | bytes 196616 | tf_op jit(solution)/shard_map/ppermute | solution.py:25
  39.2 9.3 %collective-permute-start.6 = (f32[64,256]{1,0:T(8,128)}, f32[64,256]{1,0:T(8,128)S(1)}, u32[]{:S(2)}, u32[]{:S(2)}) collective-permute-start(f32[64,256]{1,0:T(8,128)} %get-tuple-element.17), channel_id=1, source_target_pairs={{0,1},{1,2},{2,3},{3,4},{4,5},{5,6},{6,7},{7,8},{8,9},{9,10},{10,1... | collective-permute-start | bytes 196616 | tf_op jit(solution)/shard_map/ppermute | solution.py:24
  41.1 5.4 %collective-permute-start.4 = (f32[8,4,128]{2,1,0:T(4,128)}, f32[8,4,128]{2,1,0:T(4,128)S(1)}, u32[]{:S(2)}, u32[]{:S(2)}) collective-permute-start(f32[8,4,128]{2,1,0:T(4,128)} %get-tuple-element.15), channel_id=1, source_target_pairs={{0,16},{16,32},{32,48},{48,64},{64,80},{80,96},{96,112},{112,128},... | collective-permute-start | bytes 49160 | tf_op jit(solution)/shard_map/ppermute | solution.py:24
  45.2 3.3 %collective-permute-start.5 = (f32[8,4,128]{2,1,0:T(4,128)}, f32[8,4,128]{2,1,0:T(4,128)S(1)}, u32[]{:S(2)}, u32[]{:S(2)}) collective-permute-start(f32[8,4,128]{2,1,0:T(4,128)} %get-tuple-element.16), channel_id=1, source_target_pairs={{16,0},{32,16},{48,32},{64,48},{80,64},{96,80},{112,96},{128,112},... | collective-permute-start | bytes 49160 | tf_op jit(solution)/shard_map/ppermute | solution.py:25
  46.5 2.0 %copy-start.5 = (f32[8,4,128]{2,1,0:T(4,128)}, f32[8,4,128]{2,1,0:T(4,128)S(1)}, u32[]{:S(2)}) copy-start(f32[8,4,128]{2,1,0:T(4,128)S(1)} %collective-permute-done.4.hw_ref) | copy-start | bytes 49156
  48.5 0.6 copy-start.7
  48.5 0.6 copy-start.1
  48.5 0.6 copy-start.3
  64.2 3.6 %collective-permute-start.8 = (f32[8,8]{0,1:T(8,128)S(1)}, f32[8,8]{0,1:T(8,128)S(1)}, u32[]{:S(2)}, u32[]{:S(2)}) collective-permute-start(f32[8,8]{0,1:T(8,128)S(1)} %copy.8), channel_id=1, source_target_pairs={{0,1},{1,0},{2,3},{3,2},{4,5},{5,4},{6,7},{7,6},{8,9},{9,8},{10,11... | collective-permute-start | bytes 776 | tf_op jit(solution)/shard_map/ppermute | solution.py:17
  67.8 5.1 %collective-permute-start.9 = (f32[8,8]{0,1:T(8,128)S(1)}, f32[8,8]{0,1:T(8,128)S(1)}, u32[]{:S(2)}, u32[]{:S(2)}) collective-permute-start(f32[8,8]{0,1:T(8,128)S(1)} %add.35), channel_id=1, source_target_pairs={{0,2},{1,3},{2,0},{3,1},{4,6},{5,7},{6,4},{7,5},{8,10},{9,11},{10,... | collective-permute-start | bytes 776 | tf_op jit(solution)/shard_map/ppermute | solution.py:17
  72.9 3.6 %collective-permute-start.10 = (f32[8,8]{0,1:T(8,128)S(1)}, f32[8,8]{0,1:T(8,128)S(1)}, u32[]{:S(2)}, u32[]{:S(2)}) collective-permute-start(f32[8,8]{0,1:T(8,128)S(1)} %add.36), channel_id=1, source_target_pairs={{0,4},{1,5},{2,6},{3,7},{4,0},{5,1},{6,2},{7,3},{8,12},{9,13},{10,... | collective-permute-start | bytes 776 | tf_op jit(solution)/shard_map/ppermute | solution.py:17
  76.6 5.1 %collective-permute-start.11 = (f32[8,8]{0,1:T(8,128)S(1)}, f32[8,8]{0,1:T(8,128)S(1)}, u32[]{:S(2)}, u32[]{:S(2)}) collective-permute-start(f32[8,8]{0,1:T(8,128)S(1)} %add.37), channel_id=1, source_target_pairs={{0,8},{1,9},{2,10},{3,11},{4,12},{5,13},{6,14},{7,15},{8,0},{9,1},... | collective-permute-start | bytes 776 | tf_op jit(solution)/shard_map/ppermute | solution.py:17
  81.7 1.2 %collective-permute-start.12 = (f32[8,8]{0,1:T(8,128)S(1)}, f32[8,8]{0,1:T(8,128)S(1)}, u32[]{:S(2)}, u32[]{:S(2)}) collective-permute-start(f32[8,8]{0,1:T(8,128)S(1)} %add.38), channel_id=1, source_target_pairs={{0,16},{16,0},{32,48},{48,32},{64,80},{80,64},{96,112},{112,96},{1... | collective-permute-start | bytes 776 | tf_op jit(solution)/shard_map/ppermute | solution.py:17
  82.8 3.8 %collective-permute-start.13 = (f32[8,8]{0,1:T(8,128)S(1)}, f32[8,8]{0,1:T(8,128)S(1)}, u32[]{:S(2)}, u32[]{:S(2)}) collective-permute-start(f32[8,8]{0,1:T(8,128)S(1)} %add.39), channel_id=1, source_target_pairs={{0,32},{16,48},{32,0},{48,16},{64,96},{80,112},{96,64},{112,80},{1... | collective-permute-start | bytes 776 | tf_op jit(solution)/shard_map/ppermute | solution.py:17
  86.7 7.2 %collective-permute-start.14 = (f32[8,8]{0,1:T(8,128)S(1)}, f32[8,8]{0,1:T(8,128)S(1)}, u32[]{:S(2)}, u32[]{:S(2)}) collective-permute-start(f32[8,8]{0,1:T(8,128)S(1)} %add.40), channel_id=1, source_target_pairs={{0,64},{16,80},{32,96},{48,112},{64,0},{80,16},{96,32},{112,48},{1... | collective-permute-start | bytes 776 | tf_op jit(solution)/shard_map/ppermute | solution.py:17
  93.9 8.6 %collective-permute-start.15 = (f32[8,8]{0,1:T(8,128)S(1)}, f32[8,8]{0,1:T(8,128)S(1)}, u32[]{:S(2)}, u32[]{:S(2)}) collective-permute-start(f32[8,8]{0,1:T(8,128)S(1)} %add.41), channel_id=1, source_target_pairs={{0,128},{16,144},{32,160},{48,176},{64,192},{80,208},{96,224},{112... | collective-permute-start | bytes 776 | tf_op jit(solution)/shard_map/ppermute | solution.py:17

commit v9 on v8

--- a/solution.py
+++ b/solution.py
@@ -231,12 +231,12 @@
 
     basis = pl.pallas_call(
         combine,
-        grid=(nv, 2),
+        grid=(nv,),
         in_specs=[
             pl.BlockSpec(memory_space=pltpu.SMEM),
-            pl.BlockSpec((1, ncol, nx // 2, ny), lambda v, h: (v, 0, h, 0)),
-        ],
-        out_specs=pl.BlockSpec((1, ncol, nx // 2, ny), lambda v, h: (v, 0, h, 0)),
+            pl.BlockSpec((1, ncol, nx, ny), lambda v: (v, 0, 0, 0)),
+        ],
+        out_specs=pl.BlockSpec((1, ncol, nx, ny), lambda v: (v, 0, 0, 0)),
         out_shape=jax.ShapeDtypeStruct(forcing.shape, f32),
         compiler_params=params,
     )(inverse, response)

time: 116 us -> 114 us (0.983)
  Pallas kernels: 39.2 us -> 37.5 us
    pallas_call x1, Pallas kernels: 7.5 us -> 5.78 us  [local(): pl.pallas_call(combine, grid=(nv,), in_specs=[pl.BlockSpec(memory_space=p...]
where the time goes in v9:
time: 114 us; the launch traced here: 112 us
  starting transfers between devices  44 us (39%)
  Pallas kernels  37.5 us (33%)
  waiting for transfers between devices  23.1 us (20%)
  other arithmetic  3.56 us (3%)
  local copies, waits for them, and re-layouts  2.75 us (2%)
    ppermute x8, starting transfers between devices, all_sum(): lax.ppermute(value, axis, [(i, i ^ bit) for i in range(count)])  21.1 us
    ppermute x8, waiting for transfers between devices, all_sum(): lax.ppermute(value, axis, [(i, i ^ bit) for i in range(count)])  17.1 us
    pallas_call x1, Pallas kernels, local(): pl.pallas_call(stage_two, grid=(ncol,), in_specs=[column, column] + coef_...  14 us
    ppermute x4, starting transfers between devices, exchange(): from_above = lax.ppermute(low, axis, [(i + 1, i) for i in range(count - 1)])  13.5 us
    pallas_call x1, Pallas kernels, local(): pl.pallas_call(stage_one, grid=(ncol,), in_specs=[column] + coef_specs +...  12.3 us
    ppermute x4, starting transfers between devices, exchange(): lax.ppermute(high, axis, [(i, i + 1) for i in range(count - 1)])  9.4 us
    ppermute x4, waiting for transfers between devices, exchange(): from_above = lax.ppermute(low, axis, [(i + 1, i) for i in range(count - 1)])  5.92 us
    pallas_call x1, Pallas kernels, local(): pl.pallas_call(combine, grid=(nv,), in_specs=[pl.BlockSpec(memory_space=p...  5.78 us
  transfers between devices with their start and end apart: 16, of which 10 were waited for; matrix products, arithmetic and copies ran while one was open for 0% of the time, Pallas kernels for 0%

profile of v9, /device:TPU:2, one launch (start us, length us, event | category | flops | bytes accessed | tf_op | source)
XLA Modules:
  0.0 112.5 jit_solution(8711004440789705321)
XLA Ops:
  0.6 5.4 %shard_map.68 = (f32[8,4,128]{2,1,0:T(4,128)}, f32[8,4,128]{2,1,0:T(4,128)}, f32[64,256]{1,0:T(8,128)}) custom-call(f32[4,8,256,128]{3,2,1,0:T(8,128)} %f_ref.5), custom_call_target="tpu_custom_call" | custom-call | tf_op jit(solution)/shard_map/pallas_call | solution.py:178
  6.1 4.9 %collective-permute-start.3 = (f32[64,256]{1,0:T(8,128)}, f32[64,256]{1,0:T(8,128)S(1)}, u32[]{:S(2)}, u32[]{:S(2)}) collective-permute-start(f32[64,256]{1,0:T(8,128)} %get-tuple-element.13), channel_id=1, source_target_pairs={{1,0},{2,1},{3,2},{4,3},{5,4},{6,5},{7,6},{8,7},{9,8},{10,9},{11,1... | collective-permute-start | bytes 196616 | tf_op jit(solution)/shard_map/ppermute | solution.py:25
  10.9 1.9 %collective-permute-start.2 = (f32[64,256]{1,0:T(8,128)}, f32[64,256]{1,0:T(8,128)S(1)}, u32[]{:S(2)}, u32[]{:S(2)}) collective-permute-start(f32[64,256]{1,0:T(8,128)} %get-tuple-element.13), channel_id=1, source_target_pairs={{0,1},{1,2},{2,3},{3,4},{4,5},{5,6},{6,7},{7,8},{8,9},{9,10},{10,1... | collective-permute-start | bytes 196616 | tf_op jit(solution)/shard_map/ppermute | solution.py:24
  12.9 1.5 %collective-permute-start = (f32[8,4,128]{2,1,0:T(4,128)}, f32[8,4,128]{2,1,0:T(4,128)S(1)}, u32[]{:S(2)}, u32[]{:S(2)}) collective-permute-start(f32[8,4,128]{2,1,0:T(4,128)} %get-tuple-element.11), channel_id=1, source_target_pairs={{0,16},{16,32},{32,48},{48,64},{64,80},{80,96},{96,112},{112,128},... | collective-permute-start | bytes 49160 | tf_op jit(solution)/shard_map/ppermute | solution.py:24
  15.7 4.0 %collective-permute-done.1.he_ref = f32[8,4,128]{2,1,0:T(4,128)S(1)} collective-permute-done((f32[8,4,128]{2,1,0:T(4,128)}, f32[8,4,128]{2,1,0:T(4,128)S(1)}, u32[]{:S(2)}, u32[]{:S(2)}) %collective-permute-start.1) | collective-permute-done | bytes 16416 | tf_op jit(solution)/shard_map/ppermute | solution.py:25
  20.9 12.3 %shard_map.69 = (f32[4,8,256,128]{3,2,1,0:T(8,128)}, f32[8,4,128]{2,1,0:T(4,128)}, f32[8,4,128]{2,1,0:T(4,128)}, f32[64,256]{1,0:T(8,128)}) custom-call(f32[4,8,256,128]{3,2,1,0:T(8,128)} %f_ref.5, f32[2,256,128]{2,1,0:T(8,128)} %vel_ref.3, f32[256,128]{1,0:T(8,128)} %visc_ref.3, f32[256,128]{1,0:T(8,128)} %snd_ref.3, f32[4,4,256,128]{3,2,1,0:T(8,128)} %coup_ref.3, ...), custom_call_target="tpu_custom_call" | custom-call | tf_op jit(solution)/shard_map/pallas_call | solution.py:193
  33.2 6.0 %collective-permute-start.7 = (f32[64,256]{1,0:T(8,128)}, f32[64,256]{1,0:T(8,128)S(1)}, u32[]{:S(2)}, u32[]{:S(2)}) collective-permute-start(f32[64,256]{1,0:T(8,128)} %get-tuple-element.17), channel_id=1, source_target_pairs={{1,0},{2,1},{3,2},{4,3},{5,4},{6,5},{7,6},{8,7},{9,8},{10,9},{11,1... | collective-permute-start | bytes 196616 | tf_op jit(solution)/shard_map/ppermute | solution.py:25
  39.2 1.9 %collective-permute-start.6 = (f32[64,256]{1,0:T(8,128)}, f32[64,256]{1,0:T(8,128)S(1)}, u32[]{:S(2)}, u32[]{:S(2)}) collective-permute-start(f32[64,256]{1,0:T(8,128)} %get-tuple-element.17), channel_id=1, source_target_pairs={{0,1},{1,2},{2,3},{3,4},{4,5},{5,6},{6,7},{7,8},{8,9},{9,10},{10,1... | collective-permute-start | bytes 196616 | tf_op jit(solution)/shard_map/ppermute | solution.py:24
  41.1 4.1 %collective-permute-start.4 = (f32[8,4,128]{2,1,0:T(4,128)}, f32[8,4,128]{2,1,0:T(4,128)S(1)}, u32[]{:S(2)}, u32[]{:S(2)}) collective-permute-start(f32[8,4,128]{2,1,0:T(4,128)} %get-tuple-element.15), channel_id=1, source_target_pairs={{0,16},{16,32},{32,48},{48,64},{64,80},{80,96},{96,112},{112,128},... | collective-permute-start | bytes 49160 | tf_op jit(solution)/shard_map/ppermute | solution.py:24
  46.6 2.0 %collective-permute-done.5.he_ref = f32[8,4,128]{2,1,0:T(4,128)S(1)} collective-permute-done((f32[8,4,128]{2,1,0:T(4,128)}, f32[8,4,128]{2,1,0:T(4,128)S(1)}, u32[]{:S(2)}, u32[]{:S(2)}) %collective-permute-start.5) | collective-permute-done | bytes 16416 | tf_op jit(solution)/shard_map/ppermute | solution.py:25
  49.2 14.0 %shard_map.70 = (f32[4,8,256,128]{3,2,1,0:T(8,128)}, f32[64,128]{1,0:T(8,128)}) custom-call(f32[4,8,256,128]{3,2,1,0:T(8,128)} %f_ref.5, f32[4,8,256,128]{3,2,1,0:T(8,128)} %get-tuple-element.14.first_ref, f32[2,256,128]{2,1,0:T(8,128)} %vel_ref.3, f32[256,128]{1,0:T(8,128)} %visc_ref.3, f32[256,128]{1,0:T(8,128)} %snd_ref.3, f32[4,4,256,128]{3,2,1,0:T(8,128)} %coup_ref.3, ...), custom_call_target="tpu_custom_call" | custom-call | tf_op jit(solution)/shard_map/pallas_call | solution.py:211
  64.2 3.6 %collective-permute-done.8 = f32[8,8]{0,1:T(8,128)S(1)} collective-permute-done((f32[8,8]{0,1:T(8,128)S(1)}, f32[8,8]{0,1:T(8,128)S(1)}, u32[]{:S(2)}, u32[]{:S(2)}) %collective-permute-start.8) | collective-permute-done | bytes 288 | tf_op jit(solution)/shard_map/ppermute | solution.py:17
  67.8 3.4 %collective-permute-start.9 = (f32[8,8]{0,1:T(8,128)S(1)}, f32[8,8]{0,1:T(8,128)S(1)}, u32[]{:S(2)}, u32[]{:S(2)}) collective-permute-start(f32[8,8]{0,1:T(8,128)S(1)} %add.35), channel_id=1, source_target_pairs={{0,2},{1,3},{2,0},{3,1},{4,6},{5,7},{6,4},{7,5},{8,10},{9,11},{10,... | collective-permute-start | bytes 776 | tf_op jit(solution)/shard_map/ppermute | solution.py:17
  71.2 1.7 %collective-permute-done.9 = f32[8,8]{0,1:T(8,128)S(1)} collective-permute-done((f32[8,8]{0,1:T(8,128)S(1)}, f32[8,8]{0,1:T(8,128)S(1)}, u32[]{:S(2)}, u32[]{:S(2)}) %collective-permute-start.9) | collective-permute-done | bytes 288 | tf_op jit(solution)/shard_map/ppermute | solution.py:17
  73.3 3.2 %collective-permute-done.10 = f32[8,8]{0,1:T(8,128)S(1)} collective-permute-done((f32[8,8]{0,1:T(8,128)S(1)}, f32[8,8]{0,1:T(8,128)S(1)}, u32[]{:S(2)}, u32[]{:S(2)}) %collective-permute-start.10) | collective-permute-done | bytes 288 | tf_op jit(solution)/shard_map/ppermute | solution.py:17
  76.6 2.4 %collective-permute-start.11 = (f32[8,8]{0,1:T(8,128)S(1)}, f32[8,8]{0,1:T(8,128)S(1)}, u32[]{:S(2)}, u32[]{:S(2)}) collective-permute-start(f32[8,8]{0,1:T(8,128)S(1)} %add.37), channel_id=1, source_target_pairs={{0,8},{1,9},{2,10},{3,11},{4,12},{5,13},{6,14},{7,15},{8,0},{9,1},... | collective-permute-start | bytes 776 | tf_op jit(solution)/shard_map/ppermute | solution.py:17
  79.0 2.7 %collective-permute-done.11 = f32[8,8]{0,1:T(8,128)S(1)} collective-permute-done((f32[8,8]{0,1:T(8,128)S(1)}, f32[8,8]{0,1:T(8,128)S(1)}, u32[]{:S(2)}, u32[]{:S(2)}) %collective-permute-start.11) | collective-permute-done | bytes 288 | tf_op jit(solution)/shard_map/ppermute | solution.py:17
  82.8 2.3 %collective-permute-start.13 = (f32[8,8]{0,1:T(8,128)S(1)}, f32[8,8]{0,1:T(8,128)S(1)}, u32[]{:S(2)}, u32[]{:S(2)}) collective-permute-start(f32[8,8]{0,1:T(8,128)S(1)} %add.39), channel_id=1, source_target_pairs={{0,32},{16,48},{32,0},{48,16},{64,96},{80,112},{96,64},{112,80},{1... | collective-permute-start | bytes 776 | tf_op jit(solution)/shard_map/ppermute | solution.py:17
  85.1 1.6 %collective-permute-done.13 = f32[8,8]{0,1:T(8,128)S(1)} collective-permute-done((f32[8,8]{0,1:T(8,128)S(1)}, f32[8,8]{0,1:T(8,128)S(1)}, u32[]{:S(2)}, u32[]{:S(2)}) %collective-permute-start.13) | collective-permute-done | bytes 288 | tf_op jit(solution)/shard_map/ppermute | solution.py:17
  86.7 5.6 %collective-permute-start.14 = (f32[8,8]{0,1:T(8,128)S(1)}, f32[8,8]{0,1:T(8,128)S(1)}, u32[]{:S(2)}, u32[]{:S(2)}) collective-permute-start(f32[8,8]{0,1:T(8,128)S(1)} %add.40), channel_id=1, source_target_pairs={{0,64},{16,80},{32,96},{48,112},{64,0},{80,16},{96,32},{112,48},{1... | collective-permute-start | bytes 776 | tf_op jit(solution)/shard_map/ppermute | solution.py:17
  92.3 1.6 %collective-permute-done.14 = f32[8,8]{0,1:T(8,128)S(1)} collective-permute-done((f32[8,8]{0,1:T(8,128)S(1)}, f32[8,8]{0,1:T(8,128)S(1)}, u32[]{:S(2)}, u32[]{:S(2)}) %collective-permute-start.14) | collective-permute-done | bytes 288 | tf_op jit(solution)/shard_map/ppermute | solution.py:17
  93.9 7.0 %collective-permute-start.15 = (f32[8,8]{0,1:T(8,128)S(1)}, f32[8,8]{0,1:T(8,128)S(1)}, u32[]{:S(2)}, u32[]{:S(2)}) collective-permute-start(f32[8,8]{0,1:T(8,128)S(1)} %add.41), channel_id=1, source_target_pairs={{0,128},{16,144},{32,160},{48,176},{64,192},{80,208},{96,224},{112... | collective-permute-start | bytes 776 | tf_op jit(solution)/shard_map/ppermute | solution.py:17
  100.9 1.6 %collective-permute-done.15 = f32[8,8]{0,1:T(8,128)S(1)} collective-permute-done((f32[8,8]{0,1:T(8,128)S(1)}, f32[8,8]{0,1:T(8,128)S(1)}, u32[]{:S(2)}, u32[]{:S(2)}) %collective-permute-start.15) | collective-permute-done | bytes 288 | tf_op jit(solution)/shard_map/ppermute | solution.py:17
  106.7 5.8 %shard_map.71 = f32[4,8,256,128]{3,2,1,0:T(8,128)} custom-call(f32[8,8]{1,0:T(8,128)} %fusion.inv_ref, f32[4,8,256,128]{3,2,1,0:T(8,128)} %get-tuple-element.19.r_ref), custom_call_target="tpu_custom_call" | custom-call | tf_op jit(solution)/shard_map/pallas_call | solution.py:232
  (49 shorter events, 11.3 us)
Async XLA Ops:
  6.1 13.6 %collective-permute-start.3 = (f32[64,256]{1,0:T(8,128)}, f32[64,256]{1,0:T(8,128)S(1)}, u32[]{:S(2)}, u32[]{:S(2)}) collective-permute-start(f32[64,256]{1,0:T(8,128)} %get-tuple-element.13), channel_id=1, source_target_pairs={{1,0},{2,1},{3,2},{4,3},{5,4},{6,5},{7,6},{8,7},{9,8},{10,9},{11,1... | collective-permute-start | bytes 196616 | tf_op jit(solution)/shard_map/ppermute | solution.py:25
  10.9 8.7 %collective-permute-start.2 = (f32[64,256]{1,0:T(8,128)}, f32[64,256]{1,0:T(8,128)S(1)}, u32[]{:S(2)}, u32[]{:S(2)}) collective-permute-start(f32[64,256]{1,0:T(8,128)} %get-tuple-element.13), channel_id=1, source_target_pairs={{0,1},{1,2},{2,3},{3,4},{4,5},{5,6},{6,7},{7,8},{8,9},{9,10},{10,1... | collective-permute-start | bytes 196616 | tf_op jit(solution)/shard_map/ppermute | solution.py:24
  12.9 2.8 %collective-permute-start = (f32[8,4,128]{2,1,0:T(4,128)}, f32[8,4,128]{2,1,0:T(4,128)S(1)}, u32[]{:S(2)}, u32[]{:S(2)}) collective-permute-start(f32[8,4,128]{2,1,0:T(4,128)} %get-tuple-element.11), channel_id=1, source_target_pairs={{0,16},{16,32},{32,48},{48,64},{64,80},{80,96},{96,112},{112,128},... | collective-permute-start | bytes 49160 | tf_op jit(solution)/shard_map/ppermute | solution.py:24
  14.3 5.3 %collective-permute-start.1 = (f32[8,4,128]{2,1,0:T(4,128)}, f32[8,4,128]{2,1,0:T(4,128)S(1)}, u32[]{:S(2)}, u32[]{:S(2)}) collective-permute-start(f32[8,4,128]{2,1,0:T(4,128)} %get-tuple-element.12), channel_id=1, source_target_pairs={{16,0},{32,16},{48,32},{64,48},{80,64},{96,80},{112,96},{128,112},... | collective-permute-start | bytes 49160 | tf_op jit(solution)/shard_map/ppermute | solution.py:25
  15.7 4.0 %copy-start.4 = (f32[8,4,128]{2,1,0:T(4,128)}, f32[8,4,128]{2,1,0:T(4,128)S(1)}, u32[]{:S(2)}) copy-start(f32[8,4,128]{2,1,0:T(4,128)S(1)} %collective-permute-done.hw_ref) | copy-start | bytes 49156
  19.6 0.6 copy-start.6
  19.6 0.6 copy-start
  20.2 0.6 copy-start.2
  33.2 15.4 %collective-permute-start.7 = (f32[64,256]{1,0:T(8,128)}, f32[64,256]{1,0:T(8,128)S(1)}, u32[]{:S(2)}, u32[]{:S(2)}) collective-permute-start(f32[64,256]{1,0:T(8,128)} %get-tuple-element.17), channel_id=1, source_target_pairs={{1,0},{2,1},{3,2},{4,3},{5,4},{6,5},{7,6},{8,7},{9,8},{10,9},{11,1... | collective-permute-start | bytes 196616 | tf_op jit(solution)/shard_map/ppermute | solution.py:25
  39.2 9.3 %collective-permute-start.6 = (f32[64,256]{1,0:T(8,128)}, f32[64,256]{1,0:T(8,128)S(1)}, u32[]{:S(2)}, u32[]{:S(2)}) collective-permute-start(f32[64,256]{1,0:T(8,128)} %get-tuple-element.17), channel_id=1, source_target_pairs={{0,1},{1,2},{2,3},{3,4},{4,5},{5,6},{6,7},{7,8},{8,9},{9,10},{10,1... | collective-permute-start | bytes 196616 | tf_op jit(solution)/shard_map/ppermute | solution.py:24
  41.1 5.4 %collective-permute-start.4 = (f32[8,4,128]{2,1,0:T(4,128)}, f32[8,4,128]{2,1,0:T(4,128)S(1)}, u32[]{:S(2)}, u32[]{:S(2)}) collective-permute-start(f32[8,4,128]{2,1,0:T(4,128)} %get-tuple-element.15), channel_id=1, source_target_pairs={{0,16},{16,32},{32,48},{48,64},{64,80},{80,96},{96,112},{112,128},... | collective-permute-start | bytes 49160 | tf_op jit(solution)/shard_map/ppermute | solution.py:24
  45.2 3.3 %collective-permute-start.5 = (f32[8,4,128]{2,1,0:T(4,128)}, f32[8,4,128]{2,1,0:T(4,128)S(1)}, u32[]{:S(2)}, u32[]{:S(2)}) collective-permute-start(f32[8,4,128]{2,1,0:T(4,128)} %get-tuple-element.16), channel_id=1, source_target_pairs={{16,0},{32,16},{48,32},{64,48},{80,64},{96,80},{112,96},{128,112},... | collective-permute-start | bytes 49160 | tf_op jit(solution)/shard_map/ppermute | solution.py:25
  46.5 2.0 %copy-start.5 = (f32[8,4,128]{2,1,0:T(4,128)}, f32[8,4,128]{2,1,0:T(4,128)S(1)}, u32[]{:S(2)}) copy-start(f32[8,4,128]{2,1,0:T(4,128)S(1)} %collective-permute-done.4.hw_ref) | copy-start | bytes 49156
  48.5 0.6 copy-start.7
  48.5 0.6 copy-start.1
  48.5 0.6 copy-start.3
  64.2 3.6 %collective-permute-start.8 = (f32[8,8]{0,1:T(8,128)S(1)}, f32[8,8]{0,1:T(8,128)S(1)}, u32[]{:S(2)}, u32[]{:S(2)}) collective-permute-start(f32[8,8]{0,1:T(8,128)S(1)} %copy.8), channel_id=1, source_target_pairs={{0,1},{1,0},{2,3},{3,2},{4,5},{5,4},{6,7},{7,6},{8,9},{9,8},{10,11... | collective-permute-start | bytes 776 | tf_op jit(solution)/shard_map/ppermute | solution.py:17
  67.8 5.1 %collective-permute-start.9 = (f32[8,8]{0,1:T(8,128)S(1)}, f32[8,8]{0,1:T(8,128)S(1)}, u32[]{:S(2)}, u32[]{:S(2)}) collective-permute-start(f32[8,8]{0,1:T(8,128)S(1)} %add.35), channel_id=1, source_target_pairs={{0,2},{1,3},{2,0},{3,1},{4,6},{5,7},{6,4},{7,5},{8,10},{9,11},{10,... | collective-permute-start | bytes 776 | tf_op jit(solution)/shard_map/ppermute | solution.py:17
  72.9 3.6 %collective-permute-start.10 = (f32[8,8]{0,1:T(8,128)S(1)}, f32[8,8]{0,1:T(8,128)S(1)}, u32[]{:S(2)}, u32[]{:S(2)}) collective-permute-start(f32[8,8]{0,1:T(8,128)S(1)} %add.36), channel_id=1, source_target_pairs={{0,4},{1,5},{2,6},{3,7},{4,0},{5,1},{6,2},{7,3},{8,12},{9,13},{10,... | collective-permute-start | bytes 776 | tf_op jit(solution)/shard_map/ppermute | solution.py:17
  76.6 5.1 %collective-permute-start.11 = (f32[8,8]{0,1:T(8,128)S(1)}, f32[8,8]{0,1:T(8,128)S(1)}, u32[]{:S(2)}, u32[]{:S(2)}) collective-permute-start(f32[8,8]{0,1:T(8,128)S(1)} %add.37), channel_id=1, source_target_pairs={{0,8},{1,9},{2,10},{3,11},{4,12},{5,13},{6,14},{7,15},{8,0},{9,1},... | collective-permute-start | bytes 776 | tf_op jit(solution)/shard_map/ppermute | solution.py:17
  81.7 1.2 %collective-permute-start.12 = (f32[8,8]{0,1:T(8,128)S(1)}, f32[8,8]{0,1:T(8,128)S(1)}, u32[]{:S(2)}, u32[]{:S(2)}) collective-permute-start(f32[8,8]{0,1:T(8,128)S(1)} %add.38), channel_id=1, source_target_pairs={{0,16},{16,0},{32,48},{48,32},{64,80},{80,64},{96,112},{112,96},{1... | collective-permute-start | bytes 776 | tf_op jit(solution)/shard_map/ppermute | solution.py:17
  82.8 3.8 %collective-permute-start.13 = (f32[8,8]{0,1:T(8,128)S(1)}, f32[8,8]{0,1:T(8,128)S(1)}, u32[]{:S(2)}, u32[]{:S(2)}) collective-permute-start(f32[8,8]{0,1:T(8,128)S(1)} %add.39), channel_id=1, source_target_pairs={{0,32},{16,48},{32,0},{48,16},{64,96},{80,112},{96,64},{112,80},{1... | collective-permute-start | bytes 776 | tf_op jit(solution)/shard_map/ppermute | solution.py:17
  86.7 7.2 %collective-permute-start.14 = (f32[8,8]{0,1:T(8,128)S(1)}, f32[8,8]{0,1:T(8,128)S(1)}, u32[]{:S(2)}, u32[]{:S(2)}) collective-permute-start(f32[8,8]{0,1:T(8,128)S(1)} %add.40), channel_id=1, source_target_pairs={{0,64},{16,80},{32,96},{48,112},{64,0},{80,16},{96,32},{112,48},{1... | collective-permute-start | bytes 776 | tf_op jit(solution)/shard_map/ppermute | solution.py:17
  93.9 8.6 %collective-permute-start.15 = (f32[8,8]{0,1:T(8,128)S(1)}, f32[8,8]{0,1:T(8,128)S(1)}, u32[]{:S(2)}, u32[]{:S(2)}) collective-permute-start(f32[8,8]{0,1:T(8,128)S(1)} %add.41), channel_id=1, source_target_pairs={{0,128},{16,144},{32,160},{48,176},{64,192},{80,208},{96,224},{112... | collective-permute-start | bytes 776 | tf_op jit(solution)/shard_map/ppermute | solution.py:17

commit v10 on v9

--- a/solution.py
+++ b/solution.py
@@ -48,7 +48,7 @@
 
 def operator(q, west, east, below_ref, above_ref, c, vel_ref, visc_ref, snd_ref, coup_ref):
     nx, ny = q[0].shape
-    rows = lax.broadcasted_iota(jnp.int32, (nx, ny), 0)
+    slab = lax.broadcasted_iota(jnp.int32, (8, ny), 0)
     lanes = lax.broadcasted_iota(jnp.int32, (nx, ny), 1)
     vel0 = vel_ref[0]
     vel1 = vel_ref[1]
@@ -60,8 +60,10 @@
         lo = 2 * NV * c + 2 * v
         north = pltpu.roll(above_ref[...], ny - 1 - lo, 1)
         south = pltpu.roll(below_ref[...], ny - 1 - lo, 1)
-        e = jnp.where(rows == nx - 1, east[v], pltpu.roll(field, nx - 1, 0))
-        w = jnp.where(rows == 0, west[v], pltpu.roll(field, 1, 0))
+        e = pltpu.roll(field, nx - 1, 0)
+        e = jnp.concatenate([e[:nx - 8], jnp.where(slab == 7, east[v], e[nx - 8:])], axis=0)
+        w = pltpu.roll(field, 1, 0)
+        w = jnp.concatenate([jnp.where(slab == 0, west[v], w[:8]), w[8:]], axis=0)
         n = jnp.where(lanes == ny - 1, north, pltpu.roll(field, ny - 1, 1))
         s = jnp.where(lanes == 0, south, pltpu.roll(field, 1, 1))
         gx = 0.5 * (e - w)

time: 114 us -> 114 us (level)
  no operation moved by 1% of the time
where the time goes in v10:
time: 114 us; the launch traced here: 112 us
  starting transfers between devices  44 us (39%)
  Pallas kernels  37.5 us (33%)
  waiting for transfers between devices  23.1 us (20%)
  other arithmetic  3.56 us (3%)
  local copies, waits for them, and re-layouts  2.75 us (2%)
    ppermute x8, starting transfers between devices, all_sum(): lax.ppermute(value, axis, [(i, i ^ bit) for i in range(count)])  21.1 us
    ppermute x8, waiting for transfers between devices, all_sum(): lax.ppermute(value, axis, [(i, i ^ bit) for i in range(count)])  17.1 us
    pallas_call x1, Pallas kernels, local(): pl.pallas_call(stage_two, grid=(ncol,), in_specs=[column, column] + coef_...  14 us
    ppermute x4, starting transfers between devices, exchange(): from_above = lax.ppermute(low, axis, [(i + 1, i) for i in range(count - 1)])  13.5 us
    pallas_call x1, Pallas kernels, local(): pl.pallas_call(stage_one, grid=(ncol,), in_specs=[column] + coef_specs +...  12.3 us
    ppermute x4, starting transfers between devices, exchange(): lax.ppermute(high, axis, [(i, i + 1) for i in range(count - 1)])  9.4 us
    ppermute x4, waiting for transfers between devices, exchange(): from_above = lax.ppermute(low, axis, [(i + 1, i) for i in range(count - 1)])  5.92 us
    pallas_call x1, Pallas kernels, local(): pl.pallas_call(combine, grid=(nv,), in_specs=[pl.BlockSpec(memory_space=p...  5.78 us
  transfers between devices with their start and end apart: 16, of which 10 were waited for; matrix products, arithmetic and copies ran while one was open for 0% of the time, Pallas kernels for 0%

profile of v10, /device:TPU:2, one launch (start us, length us, event | category | flops | bytes accessed | tf_op | source)
XLA Modules:
  0.0 112.5 jit_solution(9045063806516917893)
XLA Ops:
  0.6 5.4 %shard_map.68 = (f32[8,4,128]{2,1,0:T(4,128)}, f32[8,4,128]{2,1,0:T(4,128)}, f32[64,256]{1,0:T(8,128)}) custom-call(f32[4,8,256,128]{3,2,1,0:T(8,128)} %f_ref.5), custom_call_target="tpu_custom_call" | custom-call | tf_op jit(solution)/shard_map/pallas_call | solution.py:180
  6.1 4.9 %collective-permute-start.3 = (f32[64,256]{1,0:T(8,128)}, f32[64,256]{1,0:T(8,128)S(1)}, u32[]{:S(2)}, u32[]{:S(2)}) collective-permute-start(f32[64,256]{1,0:T(8,128)} %get-tuple-element.13), channel_id=1, source_target_pairs={{1,0},{2,1},{3,2},{4,3},{5,4},{6,5},{7,6},{8,7},{9,8},{10,9},{11,1... | collective-permute-start | bytes 196616 | tf_op jit(solution)/shard_map/ppermute | solution.py:25
  10.9 1.9 %collective-permute-start.2 = (f32[64,256]{1,0:T(8,128)}, f32[64,256]{1,0:T(8,128)S(1)}, u32[]{:S(2)}, u32[]{:S(2)}) collective-permute-start(f32[64,256]{1,0:T(8,128)} %get-tuple-element.13), channel_id=1, source_target_pairs={{0,1},{1,2},{2,3},{3,4},{4,5},{5,6},{6,7},{7,8},{8,9},{9,10},{10,1... | collective-permute-start | bytes 196616 | tf_op jit(solution)/shard_map/ppermute | solution.py:24
  12.9 1.5 %collective-permute-start = (f32[8,4,128]{2,1,0:T(4,128)}, f32[8,4,128]{2,1,0:T(4,128)S(1)}, u32[]{:S(2)}, u32[]{:S(2)}) collective-permute-start(f32[8,4,128]{2,1,0:T(4,128)} %get-tuple-element.11), channel_id=1, source_target_pairs={{0,16},{16,32},{32,48},{48,64},{64,80},{80,96},{96,112},{112,128},... | collective-permute-start | bytes 49160 | tf_op jit(solution)/shard_map/ppermute | solution.py:24
  15.7 4.0 %collective-permute-done.1.he_ref = f32[8,4,128]{2,1,0:T(4,128)S(1)} collective-permute-done((f32[8,4,128]{2,1,0:T(4,128)}, f32[8,4,128]{2,1,0:T(4,128)S(1)}, u32[]{:S(2)}, u32[]{:S(2)}) %collective-permute-start.1) | collective-permute-done | bytes 16416 | tf_op jit(solution)/shard_map/ppermute | solution.py:25
  20.9 12.3 %shard_map.69 = (f32[4,8,256,128]{3,2,1,0:T(8,128)}, f32[8,4,128]{2,1,0:T(4,128)}, f32[8,4,128]{2,1,0:T(4,128)}, f32[64,256]{1,0:T(8,128)}) custom-call(f32[4,8,256,128]{3,2,1,0:T(8,128)} %f_ref.5, f32[2,256,128]{2,1,0:T(8,128)} %vel_ref.3, f32[256,128]{1,0:T(8,128)} %visc_ref.3, f32[256,128]{1,0:T(8,128)} %snd_ref.3, f32[4,4,256,128]{3,2,1,0:T(8,128)} %coup_ref.3, ...), custom_call_target="tpu_custom_call" | custom-call | tf_op jit(solution)/shard_map/pallas_call | solution.py:195
  33.2 6.0 %collective-permute-start.7 = (f32[64,256]{1,0:T(8,128)}, f32[64,256]{1,0:T(8,128)S(1)}, u32[]{:S(2)}, u32[]{:S(2)}) collective-permute-start(f32[64,256]{1,0:T(8,128)} %get-tuple-element.17), channel_id=1, source_target_pairs={{1,0},{2,1},{3,2},{4,3},{5,4},{6,5},{7,6},{8,7},{9,8},{10,9},{11,1... | collective-permute-start | bytes 196616 | tf_op jit(solution)/shard_map/ppermute | solution.py:25
  39.2 1.9 %collective-permute-start.6 = (f32[64,256]{1,0:T(8,128)}, f32[64,256]{1,0:T(8,128)S(1)}, u32[]{:S(2)}, u32[]{:S(2)}) collective-permute-start(f32[64,256]{1,0:T(8,128)} %get-tuple-element.17), channel_id=1, source_target_pairs={{0,1},{1,2},{2,3},{3,4},{4,5},{5,6},{6,7},{7,8},{8,9},{9,10},{10,1... | collective-permute-start | bytes 196616 | tf_op jit(solution)/shard_map/ppermute | solution.py:24
  41.1 4.1 %collective-permute-start.4 = (f32[8,4,128]{2,1,0:T(4,128)}, f32[8,4,128]{2,1,0:T(4,128)S(1)}, u32[]{:S(2)}, u32[]{:S(2)}) collective-permute-start(f32[8,4,128]{2,1,0:T(4,128)} %get-tuple-element.15), channel_id=1, source_target_pairs={{0,16},{16,32},{32,48},{48,64},{64,80},{80,96},{96,112},{112,128},... | collective-permute-start | bytes 49160 | tf_op jit(solution)/shard_map/ppermute | solution.py:24
  46.6 2.0 %collective-permute-done.5.he_ref = f32[8,4,128]{2,1,0:T(4,128)S(1)} collective-permute-done((f32[8,4,128]{2,1,0:T(4,128)}, f32[8,4,128]{2,1,0:T(4,128)S(1)}, u32[]{:S(2)}, u32[]{:S(2)}) %collective-permute-start.5) | collective-permute-done | bytes 16416 | tf_op jit(solution)/shard_map/ppermute | solution.py:25
  49.2 14.0 %shard_map.70 = (f32[4,8,256,128]{3,2,1,0:T(8,128)}, f32[64,128]{1,0:T(8,128)}) custom-call(f32[4,8,256,128]{3,2,1,0:T(8,128)} %f_ref.5, f32[4,8,256,128]{3,2,1,0:T(8,128)} %get-tuple-element.14.first_ref, f32[2,256,128]{2,1,0:T(8,128)} %vel_ref.3, f32[256,128]{1,0:T(8,128)} %visc_ref.3, f32[256,128]{1,0:T(8,128)} %snd_ref.3, f32[4,4,256,128]{3,2,1,0:T(8,128)} %coup_ref.3, ...), custom_call_target="tpu_custom_call" | custom-call | tf_op jit(solution)/shard_map/pallas_call | solution.py:213
  64.2 3.6 %collective-permute-done.8 = f32[8,8]{0,1:T(8,128)S(1)} collective-permute-done((f32[8,8]{0,1:T(8,128)S(1)}, f32[8,8]{0,1:T(8,128)S(1)}, u32[]{:S(2)}, u32[]{:S(2)}) %collective-permute-start.8) | collective-permute-done | bytes 288 | tf_op jit(solution)/shard_map/ppermute | solution.py:17
  67.8 3.4 %collective-permute-start.9 = (f32[8,8]{0,1:T(8,128)S(1)}, f32[8,8]{0,1:T(8,128)S(1)}, u32[]{:S(2)}, u32[]{:S(2)}) collective-permute-start(f32[8,8]{0,1:T(8,128)S(1)} %add.35), channel_id=1, source_target_pairs={{0,2},{1,3},{2,0},{3,1},{4,6},{5,7},{6,4},{7,5},{8,10},{9,11},{10,... | collective-permute-start | bytes 776 | tf_op jit(solution)/shard_map/ppermute | solution.py:17
  71.2 1.7 %collective-permute-done.9 = f32[8,8]{0,1:T(8,128)S(1)} collective-permute-done((f32[8,8]{0,1:T(8,128)S(1)}, f32[8,8]{0,1:T(8,128)S(1)}, u32[]{:S(2)}, u32[]{:S(2)}) %collective-permute-start.9) | collective-permute-done | bytes 288 | tf_op jit(solution)/shard_map/ppermute | solution.py:17
  73.4 3.2 %collective-permute-done.10 = f32[8,8]{0,1:T(8,128)S(1)} collective-permute-done((f32[8,8]{0,1:T(8,128)S(1)}, f32[8,8]{0,1:T(8,128)S(1)}, u32[]{:S(2)}, u32[]{:S(2)}) %collective-permute-start.10) | collective-permute-done | bytes 288 | tf_op jit(solution)/shard_map/ppermute | solution.py:17
  76.6 2.4 %collective-permute-start.11 = (f32[8,8]{0,1:T(8,128)S(1)}, f32[8,8]{0,1:T(8,128)S(1)}, u32[]{:S(2)}, u32[]{:S(2)}) collective-permute-start(f32[8,8]{0,1:T(8,128)S(1)} %add.37), channel_id=1, source_target_pairs={{0,8},{1,9},{2,10},{3,11},{4,12},{5,13},{6,14},{7,15},{8,0},{9,1},... | collective-permute-start | bytes 776 | tf_op jit(solution)/shard_map/ppermute | solution.py:17
  79.0 2.7 %collective-permute-done.11 = f32[8,8]{0,1:T(8,128)S(1)} collective-permute-done((f32[8,8]{0,1:T(8,128)S(1)}, f32[8,8]{0,1:T(8,128)S(1)}, u32[]{:S(2)}, u32[]{:S(2)}) %collective-permute-start.11) | collective-permute-done | bytes 288 | tf_op jit(solution)/shard_map/ppermute | solution.py:17
  82.9 2.3 %collective-permute-start.13 = (f32[8,8]{0,1:T(8,128)S(1)}, f32[8,8]{0,1:T(8,128)S(1)}, u32[]{:S(2)}, u32[]{:S(2)}) collective-permute-start(f32[8,8]{0,1:T(8,128)S(1)} %add.39), channel_id=1, source_target_pairs={{0,32},{16,48},{32,0},{48,16},{64,96},{80,112},{96,64},{112,80},{1... | collective-permute-start | bytes 776 | tf_op jit(solution)/shard_map/ppermute | solution.py:17
  85.1 1.6 %collective-permute-done.13 = f32[8,8]{0,1:T(8,128)S(1)} collective-permute-done((f32[8,8]{0,1:T(8,128)S(1)}, f32[8,8]{0,1:T(8,128)S(1)}, u32[]{:S(2)}, u32[]{:S(2)}) %collective-permute-start.13) | collective-permute-done | bytes 288 | tf_op jit(solution)/shard_map/ppermute | solution.py:17
  86.7 5.6 %collective-permute-start.14 = (f32[8,8]{0,1:T(8,128)S(1)}, f32[8,8]{0,1:T(8,128)S(1)}, u32[]{:S(2)}, u32[]{:S(2)}) collective-permute-start(f32[8,8]{0,1:T(8,128)S(1)} %add.40), channel_id=1, source_target_pairs={{0,64},{16,80},{32,96},{48,112},{64,0},{80,16},{96,32},{112,48},{1... | collective-permute-start | bytes 776 | tf_op jit(solution)/shard_map/ppermute | solution.py:17
  92.3 1.6 %collective-permute-done.14 = f32[8,8]{0,1:T(8,128)S(1)} collective-permute-done((f32[8,8]{0,1:T(8,128)S(1)}, f32[8,8]{0,1:T(8,128)S(1)}, u32[]{:S(2)}, u32[]{:S(2)}) %collective-permute-start.14) | collective-permute-done | bytes 288 | tf_op jit(solution)/shard_map/ppermute | solution.py:17
  93.9 7.0 %collective-permute-start.15 = (f32[8,8]{0,1:T(8,128)S(1)}, f32[8,8]{0,1:T(8,128)S(1)}, u32[]{:S(2)}, u32[]{:S(2)}) collective-permute-start(f32[8,8]{0,1:T(8,128)S(1)} %add.41), channel_id=1, source_target_pairs={{0,128},{16,144},{32,160},{48,176},{64,192},{80,208},{96,224},{112... | collective-permute-start | bytes 776 | tf_op jit(solution)/shard_map/ppermute | solution.py:17
  100.9 1.6 %collective-permute-done.15 = f32[8,8]{0,1:T(8,128)S(1)} collective-permute-done((f32[8,8]{0,1:T(8,128)S(1)}, f32[8,8]{0,1:T(8,128)S(1)}, u32[]{:S(2)}, u32[]{:S(2)}) %collective-permute-start.15) | collective-permute-done | bytes 288 | tf_op jit(solution)/shard_map/ppermute | solution.py:17
  106.7 5.8 %shard_map.71 = f32[4,8,256,128]{3,2,1,0:T(8,128)} custom-call(f32[8,8]{1,0:T(8,128)} %fusion.inv_ref, f32[4,8,256,128]{3,2,1,0:T(8,128)} %get-tuple-element.19.r_ref), custom_call_target="tpu_custom_call" | custom-call | tf_op jit(solution)/shard_map/pallas_call | solution.py:234
  (49 shorter events, 11.3 us)
Async XLA Ops:
  6.1 13.6 %collective-permute-start.3 = (f32[64,256]{1,0:T(8,128)}, f32[64,256]{1,0:T(8,128)S(1)}, u32[]{:S(2)}, u32[]{:S(2)}) collective-permute-start(f32[64,256]{1,0:T(8,128)} %get-tuple-element.13), channel_id=1, source_target_pairs={{1,0},{2,1},{3,2},{4,3},{5,4},{6,5},{7,6},{8,7},{9,8},{10,9},{11,1... | collective-permute-start | bytes 196616 | tf_op jit(solution)/shard_map/ppermute | solution.py:25
  10.9 8.7 %collective-permute-start.2 = (f32[64,256]{1,0:T(8,128)}, f32[64,256]{1,0:T(8,128)S(1)}, u32[]{:S(2)}, u32[]{:S(2)}) collective-permute-start(f32[64,256]{1,0:T(8,128)} %get-tuple-element.13), channel_id=1, source_target_pairs={{0,1},{1,2},{2,3},{3,4},{4,5},{5,6},{6,7},{7,8},{8,9},{9,10},{10,1... | collective-permute-start | bytes 196616 | tf_op jit(solution)/shard_map/ppermute | solution.py:24
  12.9 2.8 %collective-permute-start = (f32[8,4,128]{2,1,0:T(4,128)}, f32[8,4,128]{2,1,0:T(4,128)S(1)}, u32[]{:S(2)}, u32[]{:S(2)}) collective-permute-start(f32[8,4,128]{2,1,0:T(4,128)} %get-tuple-element.11), channel_id=1, source_target_pairs={{0,16},{16,32},{32,48},{48,64},{64,80},{80,96},{96,112},{112,128},... | collective-permute-start | bytes 49160 | tf_op jit(solution)/shard_map/ppermute | solution.py:24
  14.3 5.3 %collective-permute-start.1 = (f32[8,4,128]{2,1,0:T(4,128)}, f32[8,4,128]{2,1,0:T(4,128)S(1)}, u32[]{:S(2)}, u32[]{:S(2)}) collective-permute-start(f32[8,4,128]{2,1,0:T(4,128)} %get-tuple-element.12), channel_id=1, source_target_pairs={{16,0},{32,16},{48,32},{64,48},{80,64},{96,80},{112,96},{128,112},... | collective-permute-start | bytes 49160 | tf_op jit(solution)/shard_map/ppermute | solution.py:25
  15.7 4.0 %copy-start.4 = (f32[8,4,128]{2,1,0:T(4,128)}, f32[8,4,128]{2,1,0:T(4,128)S(1)}, u32[]{:S(2)}) copy-start(f32[8,4,128]{2,1,0:T(4,128)S(1)} %collective-permute-done.hw_ref) | copy-start | bytes 49156
  19.6 0.6 copy-start.6
  19.6 0.6 copy-start
  20.2 0.6 copy-start.2
  33.2 15.4 %collective-permute-start.7 = (f32[64,256]{1,0:T(8,128)}, f32[64,256]{1,0:T(8,128)S(1)}, u32[]{:S(2)}, u32[]{:S(2)}) collective-permute-start(f32[64,256]{1,0:T(8,128)} %get-tuple-element.17), channel_id=1, source_target_pairs={{1,0},{2,1},{3,2},{4,3},{5,4},{6,5},{7,6},{8,7},{9,8},{10,9},{11,1... | collective-permute-start | bytes 196616 | tf_op jit(solution)/shard_map/ppermute | solution.py:25
  39.2 9.3 %collective-permute-start.6 = (f32[64,256]{1,0:T(8,128)}, f32[64,256]{1,0:T(8,128)S(1)}, u32[]{:S(2)}, u32[]{:S(2)}) collective-permute-start(f32[64,256]{1,0:T(8,128)} %get-tuple-element.17), channel_id=1, source_target_pairs={{0,1},{1,2},{2,3},{3,4},{4,5},{5,6},{6,7},{7,8},{8,9},{9,10},{10,1... | collective-permute-start | bytes 196616 | tf_op jit(solution)/shard_map/ppermute | solution.py:24
  41.1 5.4 %collective-permute-start.4 = (f32[8,4,128]{2,1,0:T(4,128)}, f32[8,4,128]{2,1,0:T(4,128)S(1)}, u32[]{:S(2)}, u32[]{:S(2)}) collective-permute-start(f32[8,4,128]{2,1,0:T(4,128)} %get-tuple-element.15), channel_id=1, source_target_pairs={{0,16},{16,32},{32,48},{48,64},{64,80},{80,96},{96,112},{112,128},... | collective-permute-start | bytes 49160 | tf_op jit(solution)/shard_map/ppermute | solution.py:24
  45.2 3.3 %collective-permute-start.5 = (f32[8,4,128]{2,1,0:T(4,128)}, f32[8,4,128]{2,1,0:T(4,128)S(1)}, u32[]{:S(2)}, u32[]{:S(2)}) collective-permute-start(f32[8,4,128]{2,1,0:T(4,128)} %get-tuple-element.16), channel_id=1, source_target_pairs={{16,0},{32,16},{48,32},{64,48},{80,64},{96,80},{112,96},{128,112},... | collective-permute-start | bytes 49160 | tf_op jit(solution)/shard_map/ppermute | solution.py:25
  46.5 2.0 %copy-start.5 = (f32[8,4,128]{2,1,0:T(4,128)}, f32[8,4,128]{2,1,0:T(4,128)S(1)}, u32[]{:S(2)}) copy-start(f32[8,4,128]{2,1,0:T(4,128)S(1)} %collective-permute-done.4.hw_ref) | copy-start | bytes 49156
  48.5 0.6 copy-start.7
  48.5 0.6 copy-start.1
  48.5 0.6 copy-start.3
  64.2 3.6 %collective-permute-start.8 = (f32[8,8]{0,1:T(8,128)S(1)}, f32[8,8]{0,1:T(8,128)S(1)}, u32[]{:S(2)}, u32[]{:S(2)}) collective-permute-start(f32[8,8]{0,1:T(8,128)S(1)} %copy.8), channel_id=1, source_target_pairs={{0,1},{1,0},{2,3},{3,2},{4,5},{5,4},{6,7},{7,6},{8,9},{9,8},{10,11... | collective-permute-start | bytes 776 | tf_op jit(solution)/shard_map/ppermute | solution.py:17
  67.8 5.1 %collective-permute-start.9 = (f32[8,8]{0,1:T(8,128)S(1)}, f32[8,8]{0,1:T(8,128)S(1)}, u32[]{:S(2)}, u32[]{:S(2)}) collective-permute-start(f32[8,8]{0,1:T(8,128)S(1)} %add.35), channel_id=1, source_target_pairs={{0,2},{1,3},{2,0},{3,1},{4,6},{5,7},{6,4},{7,5},{8,10},{9,11},{10,... | collective-permute-start | bytes 776 | tf_op jit(solution)/shard_map/ppermute | solution.py:17
  73.0 3.6 %collective-permute-start.10 = (f32[8,8]{0,1:T(8,128)S(1)}, f32[8,8]{0,1:T(8,128)S(1)}, u32[]{:S(2)}, u32[]{:S(2)}) collective-permute-start(f32[8,8]{0,1:T(8,128)S(1)} %add.36), channel_id=1, source_target_pairs={{0,4},{1,5},{2,6},{3,7},{4,0},{5,1},{6,2},{7,3},{8,12},{9,13},{10,... | collective-permute-start | bytes 776 | tf_op jit(solution)/shard_map/ppermute | solution.py:17
  76.6 5.1 %collective-permute-start.11 = (f32[8,8]{0,1:T(8,128)S(1)}, f32[8,8]{0,1:T(8,128)S(1)}, u32[]{:S(2)}, u32[]{:S(2)}) collective-permute-start(f32[8,8]{0,1:T(8,128)S(1)} %add.37), channel_id=1, source_target_pairs={{0,8},{1,9},{2,10},{3,11},{4,12},{5,13},{6,14},{7,15},{8,0},{9,1},... | collective-permute-start | bytes 776 | tf_op jit(solution)/shard_map/ppermute | solution.py:17
  81.7 1.2 %collective-permute-start.12 = (f32[8,8]{0,1:T(8,128)S(1)}, f32[8,8]{0,1:T(8,128)S(1)}, u32[]{:S(2)}, u32[]{:S(2)}) collective-permute-start(f32[8,8]{0,1:T(8,128)S(1)} %add.38), channel_id=1, source_target_pairs={{0,16},{16,0},{32,48},{48,32},{64,80},{80,64},{96,112},{112,96},{1... | collective-permute-start | bytes 776 | tf_op jit(solution)/shard_map/ppermute | solution.py:17
  82.9 3.8 %collective-permute-start.13 = (f32[8,8]{0,1:T(8,128)S(1)}, f32[8,8]{0,1:T(8,128)S(1)}, u32[]{:S(2)}, u32[]{:S(2)}) collective-permute-start(f32[8,8]{0,1:T(8,128)S(1)} %add.39), channel_id=1, source_target_pairs={{0,32},{16,48},{32,0},{48,16},{64,96},{80,112},{96,64},{112,80},{1... | collective-permute-start | bytes 776 | tf_op jit(solution)/shard_map/ppermute | solution.py:17
  86.7 7.2 %collective-permute-start.14 = (f32[8,8]{0,1:T(8,128)S(1)}, f32[8,8]{0,1:T(8,128)S(1)}, u32[]{:S(2)}, u32[]{:S(2)}) collective-permute-start(f32[8,8]{0,1:T(8,128)S(1)} %add.40), channel_id=1, source_target_pairs={{0,64},{16,80},{32,96},{48,112},{64,0},{80,16},{96,32},{112,48},{1... | collective-permute-start | bytes 776 | tf_op jit(solution)/shard_map/ppermute | solution.py:17
  93.9 8.6 %collective-permute-start.15 = (f32[8,8]{0,1:T(8,128)S(1)}, f32[8,8]{0,1:T(8,128)S(1)}, u32[]{:S(2)}, u32[]{:S(2)}) collective-permute-start(f32[8,8]{0,1:T(8,128)S(1)} %add.41), channel_id=1, source_target_pairs={{0,128},{16,144},{32,160},{48,176},{64,192},{80,208},{96,224},{112... | collective-permute-start | bytes 776 | tf_op jit(solution)/shard_map/ppermute | solution.py:17
